TPU v7x, 32 devices: a whole 2x2x4 slice. The times are simulated.
32 devices in a mesh: dp: 1, tensor: 32 (over z, y, x, core).
Axes of the slice: x: 2, y: 2, z: 4, core: 2. Of those that a mesh axis runs over, the one named last changes fastest.
Arguments:
- decode_queries: bfloat16 [1, 32, 2048], P('dp'), may hold values from -17.5 to 17.5
- new_keys: bfloat16 [1, 32, 2048], P('dp'), may hold values from -7 to 7
- new_values: bfloat16 [1, 32, 2048], P('dp'), may hold values from -6 to 6
- cache_keys: bfloat16 [1, 4, 8192, 2048], P('dp', None, 'tensor'), may hold values from -32 to 32
- cache_values: bfloat16 [1, 4, 8192, 2048], P('dp', None, 'tensor'), may hold values from -6 to 6
- group_of: int32 [1, 32], P('dp'), may hold values from 0 to 3, never falling along the last dimension, each value on 1 to 16 neighbouring positions
- cache_lengths: int32 [1, 4], P('dp'), may hold values from 1024 to 8192, as said below
- decode_residual: bfloat16 [1, 32, 2048], P('dp', 'tensor'), may hold values from -3 to 3
- out_weight: bfloat16 [2048, 2048], P('tensor'), may hold values from -0.125 to 0.125
- prefill_states: bfloat16 [2048, 2048], P(('dp', 'tensor')), may hold values from -6 to 6
- norm_gain: float32 [2048], replicated, may hold values from 0.1 to 1.9
- routes: int32 [2080, 8], P(('dp', 'tensor')), may hold values from 0 to 31, all different within a row; in each aligned block of 65 rows (0 to 64, 65 to 129, ...) at most 24 rows name the same one
- route_weights: float32 [2080, 8], P(('dp', 'tensor')), may hold values from 0.05 to 0.5
- w_gate: bfloat16 [32, 2048, 1024], P('tensor', None, 'dp'), may hold values from -0.125 to 0.125
- w_up: bfloat16 [32, 2048, 1024], P('tensor', None, 'dp'), may hold values from -0.125 to 0.125
- w_down: bfloat16 [32, 1024, 2048], P('tensor', 'dp'), may hold values from -0.1875 to 0.1875
Outputs:
- prefill_out: bfloat16 [2048, 2048], P(('dp', 'tensor'))
- decode_out: bfloat16 [1, 32, 2048], P('dp', 'tensor')
Inputs may be any that keep to these rules, and one draw needn't show every extreme that they name: `group_of`: groups never fall along the requests of one dp index; each of the 4 groups has 1 to 16 requests, and some group has exactly 16. `cache_lengths`: every group's cache holds an eighth of 8192 positions or more, and in every draw some group holds all 8192. `routes`: the 8 experts of a row differ. Within the rows of one device no expert is named by more than 24 rows, a bound that some block reaches.
All inputs are finite; a program needn't handle non-finite values.
Results may differ from a plain program's by a relative error of at most 0.023.
Values may be sent and summed in bfloat16 or wider, within the bound.
No kernel may reach another device: no remote copies, remote signals or barrier semaphores. Data moves between devices by JAX's collectives and lax.ppermute only.
A program may use at most 128 MiB of HBM per device.

v0:
```python
import math

import jax
import jax.numpy as jnp
from jax import lax
from jax.sharding import PartitionSpec as P

HEADS = 16
HEAD_DIM = 128


def expert_mlp(inputs, gate_w, up_w, down_w):
    flat_rows = inputs.reshape(-1, inputs.shape[-1])
    gate = jnp.dot(flat_rows, gate_w, preferred_element_type=jnp.float32)
    upper = jnp.dot(flat_rows, up_w, preferred_element_type=jnp.float32)
    active = (jax.nn.silu(gate) * upper).astype(jnp.bfloat16)
    return jnp.dot(active, down_w, preferred_element_type=jnp.float32)


def per_device(
    decode_queries,
    new_keys,
    new_values,
    cache_keys,
    cache_values,
    group_of,
    cache_lengths,
    decode_residual,
    out_weight,
    prefill_states,
    norm_gain,
    routes,
    route_weights,
    w_gate,
    w_up,
    w_down,
):
    tensor_count = lax.axis_size("tensor")
    tensor_rank = lax.axis_index("tensor")
    requests = decode_queries.shape[1]
    groups = cache_keys.shape[1]
    reach = cache_keys.shape[2]
    model_width = decode_queries.shape[2]
    width = out_weight.shape[0]
    factor = 1.0 / math.sqrt(HEAD_DIM)
    query_heads = decode_queries[0].reshape(requests, HEADS, HEAD_DIM)
    key_table = cache_keys[0].reshape(groups, reach, HEADS, HEAD_DIM)
    value_table = cache_values[0].reshape(groups, reach, HEADS, HEAD_DIM)
    scores = (
        jnp.einsum("rhd,gjhd->grhj", query_heads, key_table, preferred_element_type=jnp.float32)
        * factor
    )
    positions = tensor_rank * reach + jnp.arange(reach, dtype=jnp.int32)
    member = group_of[0][None, :] == jnp.arange(groups, dtype=jnp.int32)[:, None]
    within = positions[None, :] < cache_lengths[0][:, None]
    visible = (member[:, :, None] & within[:, None, :])[:, :, None, :]
    own_keys = new_keys[0].astype(jnp.float32).reshape(requests, HEADS, HEAD_DIM)
    own_score = jnp.sum(query_heads.astype(jnp.float32) * own_keys, axis=2) * factor
    local_peak = jnp.maximum(jnp.max(jnp.where(visible, scores, -jnp.inf), axis=(0, 3)), own_score)
    peak = lax.pmax(local_peak, "tensor")
    expon = jnp.where(visible, jnp.exp(scores - peak[None, :, :, None]), 0.0)
    probs = expon.astype(jnp.bfloat16)
    partial_totals = jnp.sum(expon, axis=(0, 3))
    mixture = jnp.einsum(
        "grhj,gjhd->rhd", probs, value_table, preferred_element_type=jnp.float32
    ).reshape(requests, model_width)
    own_exp = jnp.exp(own_score - peak)
    own_prob = lax.optimization_barrier(own_exp.astype(jnp.bfloat16)).astype(jnp.float32)
    own_values = new_values[0].astype(jnp.float32)
    first_column = tensor_rank * width
    summed_mix, summed_totals = lax.psum((mixture, partial_totals), "tensor")
    totals = summed_totals + own_exp
    own_part = own_prob[:, :, None] * own_values.reshape(requests, HEADS, HEAD_DIM)
    merged = (
        (summed_mix.reshape(requests, HEADS, HEAD_DIM) + own_part) / totals[:, :, None]
    ).astype(jnp.bfloat16)
    columns = lax.dynamic_slice_in_dim(
        merged.reshape(requests, model_width), first_column, width, 1
    )
    block = columns
    projected = lax.psum_scatter(
        jnp.dot(block, out_weight, preferred_element_type=jnp.float32),
        "tensor",
        scatter_dimension=0,
        tiled=True,
    )
    decode_hidden = (decode_residual[0].astype(jnp.float32) + projected).astype(jnp.bfloat16)
    residual_rows = jnp.concatenate([prefill_states, decode_hidden], axis=0)
    row_float = residual_rows.astype(jnp.float32)
    inverse = lax.rsqrt(jnp.mean(row_float * row_float, axis=1, keepdims=True) + 1e-06)
    normed = (row_float * inverse * norm_gain).astype(jnp.bfloat16)
    row_count, top_count = routes.shape
    capacity = max(8, (row_count * top_count * 3 // (2 * tensor_count) + 7) // 8 * 8)
    flat_expert = routes.reshape(-1)
    one_hot = (flat_expert[:, None] == jnp.arange(tensor_count, dtype=jnp.int32)[None, :]).astype(
        jnp.int32
    )
    earlier = jnp.cumsum(one_hot, axis=0) - one_hot
    rank_within = jnp.sum(earlier * one_hot, axis=1)
    slot_index = flat_expert * capacity + rank_within
    source_row = jnp.arange(row_count * top_count, dtype=jnp.int32) // top_count
    outgoing = (
        jnp.zeros((tensor_count * capacity, model_width), jnp.bfloat16)
        .at[slot_index]
        .set(normed[source_row])
    )
    outgoing = outgoing.reshape(tensor_count, capacity, model_width)
    both_groups = lax.all_gather(
        lax.all_to_all(outgoing, "tensor", split_axis=0, concat_axis=0, tiled=True),
        "dp",
        axis=0,
        tiled=True,
    )
    block = both_groups
    returned = lax.all_to_all(
        lax.psum_scatter(
            expert_mlp(block, w_gate[0], w_up[0], w_down[0])
            .reshape(block.shape)
            .astype(jnp.bfloat16),
            "dp",
            scatter_dimension=0,
            tiled=True,
        ),
        "tensor",
        split_axis=0,
        concat_axis=0,
        tiled=True,
    )
    gathered = returned.reshape(tensor_count * capacity, model_width)[slot_index].astype(
        jnp.float32
    )
    weighted = jnp.sum(
        (gathered * route_weights.reshape(-1)[:, None]).reshape(row_count, top_count, model_width),
        axis=1,
    )
    mixed_rows = (row_float + weighted).astype(jnp.bfloat16)
    prefill_count = prefill_states.shape[0]
    return (mixed_rows[:prefill_count], mixed_rows[prefill_count:][None])


def solution(mesh):
    in_specs = (
        P("dp", None, None),
        P("dp", None, None),
        P("dp", None, None),
        P("dp", None, "tensor", None),
        P("dp", None, "tensor", None),
        P("dp", None),
        P("dp", None),
        P("dp", "tensor", None),
        P("tensor", None),
        P(("dp", "tensor"), None),
        P(),
        P(("dp", "tensor"), None),
        P(("dp", "tensor"), None),
        P("tensor", None, "dp"),
        P("tensor", None, "dp"),
        P("tensor", "dp", None),
    )
    out_specs = (P(("dp", "tensor"), None), P("dp", "tensor", None))
    return jax.shard_map(
        per_device, mesh=mesh, in_specs=in_specs, out_specs=out_specs, check_vma=False
    )
```

profile of v0, /device:TPU:0, one launch (start us, length us, event | category | flops | bytes accessed | tf_op | source)
XLA Modules:
  0.0 536.8 jit_solution(14567608873344330455)
XLA Ops:
  7.9 0.9 copy.65
  8.9 5.6 %copy.64 = bf16[128,8,16,128]{3,2,1,0:T(8,128)(2,1)} copy(bf16[128,8,16,128]{3,1,2,0:T(8,128)(2,1)} %bitcast.97) | data formatting | bytes 8388608
  14.9 4.7 fusion.18
  19.6 42.1 %pmax.7 = f32[32,16]{0,1:T(8,128)S(1)} all-reduce(f32[32,16]{0,1:T(8,128)S(1)} %multiply_maximum_fusion), channel_id=1, replica_groups=mesh['dp'=1,'tensor'=32] {'tensor'}, use_global_device_ids=true, to_apply=%region_2.3 | all-reduce | flops 512 | bytes 4096 | tf_op jit(solution)/shard_map/pmax | solution.py:60
  61.7 3.6 copy.67
  65.3 2.4 fusion.24
  69.1 40.4 %psum.15 = f32[32,16]{0,1:T(8,128)S(1)} all-reduce(f32[32,16]{0,1:T(8,128)S(1)} %fusion.21), channel_id=1, replica_groups=mesh['dp'=1,'tensor'=32] {'tensor'}, use_global_device_ids=true, to_apply=%region_5.6 | all-reduce | flops 512 | bytes 4096 | tf_op jit(solution)/shard_map/psum | solution.py:71
  109.9 1.5 reduce-window.6
  112.3 81.4 %all-reduce.5.cloned.1.call-done = f32[32,2048]{1,0:T(8,128)} async-done(((f32[32,2048]{1,0:T(8,128)}), f32[32,2048]{1,0:T(8,128)}) %all-reduce.5.cloned.1.call-update) | async-done | bytes 262160 | tf_op jit(solution)/shard_map/psum | solution.py:71
  193.6 1.7 fusion.40
  195.6 128.2 %all-reduce.7.cloned.1.call-done = f32[32,2048]{1,0:T(8,128)} async-done(((f32[32,2048]{1,0:T(8,128)}), f32[32,2048]{1,0:T(8,128)}) %all-reduce.7.cloned.1.call-update) | async-done | bytes 262160
  323.8 0.9 fusion.43
  324.9 0.8 fusion.34
  325.7 32.7 %scatter_custom_fusion = bf16[768,2048]{1,0:T(8,128)(2,1)S(1)} fusion(s32[520]{0:T(1024)S(1)} %fusion.46, bf16[65,2048]{1,0:T(8,128)(2,1)} %fusion.34, s32[1024]{0:T(1024)S(1)} %pad_clamp_fusion.1, bf16[]{:T(256)} %constant.47.clone.1), kind=kCustom, calls=%fused_computation.17 | custom fusion | bytes 3146240 | tf_op jit(solution)/shard_map/scatter | solution.py:105
  358.4 74.6 %all_to_all.10 = bf16[32,24,2048]{2,1,0:T(8,128)(2,1)S(1)} all-to-all(bf16[32,24,2048]{2,1,0:T(8,128)(2,1)S(1)} %bitcast.96), channel_id=1, replica_groups=mesh['dp'=1,'tensor'=32] {'tensor'}, dimensions={0} | all-to-all | bytes 6291456 | tf_op jit(solution)/shard_map/all_to_all | solution.py:109
  433.0 3.4 fusion.3
  436.5 3.8 multiply_convert_fusion
  440.3 4.8 fusion.11
  445.1 3.7 all-to-all-start.1
  448.9 71.3 %all-to-all-done.1 = bf16[32,24,2048]{2,1,0:T(8,128)(2,1)S(1)} async-done(((bf16[32,24,2048]{2,1,0:T(8,128)(2,1)}), bf16[32,24,2048]{2,1,0:T(8,128)(2,1)S(1)}, u32[]{:S(2)}, u32[]{:S(2)}) %all-to-all-start.1) | async-done | bytes 3145760 | tf_op jit(solution)/shard_map/all_to_all | solution.py:115
  520.3 3.9 gather_fusion
  524.2 3.4 fusion
  527.6 1.0 fusion.35
  528.6 0.7 slice.26
  (62 shorter events, 5.0 us)
Async XLA Ops:
  7.2 186.5 %copy-start = (bf16[64,2048]{1,0:T(8,128)(2,1)S(1)}, bf16[64,2048]{1,0:T(8,128)(2,1)}, u32[]{:S(2)}) copy-start(bf16[64,2048]{1,0:T(8,128)(2,1)} %param.24) | copy-start | bytes 786436
  7.2 186.5 %all-reduce.5.cloned.1.call-start = ((), (), s32[]{:S(2)}) async-start(), calls=%async_computation.2 | async-start | bytes 524288 | tf_op jit(solution)/shard_map/psum | solution.py:71
  8.9 5.6 %copy-start.2 = (bf16[1,32,2048]{2,1,0:T(8,128)(2,1)S(1)}, bf16[1,32,2048]{2,1,0:T(8,128)(2,1)}, u32[]{:S(2)}) copy-start(bf16[1,32,2048]{2,1,0:T(8,128)(2,1)} %param.17) | copy-start | bytes 393220
  8.9 5.9 %copy-start.7 = (s32[1,4]{1,0:T(1,128)S(1)}, s32[1,4]{1,0:T(1,128)}, u32[]{:S(2)}) copy-start(s32[1,4]{1,0:T(1,128)} %param.22) | copy-start | bytes 52
  65.3 44.4 %copy-start.3 = (s32[65,8]{0,1:T(8,128)S(1)}, s32[65,8]{0,1:T(8,128)}, u32[]{:S(2)}) copy-start(s32[65,8]{0,1:T(8,128)} %param.27) | copy-start | bytes 6244
  67.7 256.1 %copy-start.4 = (bf16[1,1,2048]{2,1,0:T(2,128)(2,1)S(1)}, bf16[1,1,2048]{2,1,0:T(2,128)(2,1)}, u32[]{:S(2)}) copy-start(bf16[1,1,2048]{2,1,0:T(2,128)(2,1)} %param.23) | copy-start | bytes 12292
  67.7 257.0 %copy-start.1 = (bf16[64,2048]{1,0:T(8,128)(2,1)S(1)}, bf16[64,2048]{1,0:T(8,128)(2,1)}, u32[]{:S(2)}) copy-start(bf16[64,2048]{1,0:T(8,128)(2,1)} %param.25) | copy-start | bytes 786436
  68.5 256.4 %copy-start.5 = (f32[2048]{0:T(1024)S(1)}, f32[2048]{0:T(1024)}, u32[]{:S(2)}) copy-start(f32[2048]{0:T(1024)} %param.26) | copy-start | bytes 24580
  68.5 255.3 %all-reduce.7.cloned.1.call-start = ((), (), s32[]{:S(2)}) async-start(), calls=%async_computation.3 | async-start | bytes 524288
  358.4 74.6 %copy-start.8 = (bf16[1,2048,1024]{2,1,0:T(8,128)(2,1)S(1)}, bf16[1,2048,1024]{2,1,0:T(8,128)(2,1)}, u32[]{:S(2)}) copy-start(bf16[1,2048,1024]{2,1,0:T(8,128)(2,1)} %param.30) | copy-start | bytes 12582916
  433.0 3.5 copy-start.9
  436.5 3.8 copy-start.10
  445.1 3.7 copy-start.6
  445.1 75.1 %all-to-all-start.1 = ((bf16[32,24,2048]{2,1,0:T(8,128)(2,1)}), bf16[32,24,2048]{2,1,0:T(8,128)(2,1)S(1)}, u32[]{:S(2)}, u32[]{:S(2)}) async-start(bf16[32,24,2048]{2,1,0:T(8,128)(2,1)} %fusion.11), calls=%async_computation.1 | async-start | bytes 6291456 | tf_op jit(solution)/shard_map/all_to_all | solution.py:115
Sparse Core Ops, SparseCore 0:
  68.6 124.9 all-reduce.4
  199.7 124.0 all-reduce.6
where the time goes:
time: 537 us
  waiting for transfers between devices  281 us (52%)
  blocking collectives  157 us (29%)
  local copies, waits for them, and re-layouts  50.2 us (9%)
  matrix products  20.8 us (4%)
  between operations  14.4 us (3%)
  other arithmetic  9.66 us (2%)
    unnamed x3, waiting for transfers between devices  128 us
    psum x1, waiting for transfers between devices, per_device(): summed_mix, summed_totals = lax.psum((mixture, partial_totals), 'tensor')  81.4 us
    all_to_all x1, blocking collectives, per_device(): lax.all_to_all(outgoing, 'tensor', split_axis=0, concat_axis=0, tiled=True)  74.6 us
    all_to_all x1, waiting for transfers between devices, per_device(): lax.all_to_all(lax.psum_scatter(expert_mlp(block, w_gate[0], w_up[0], w_d...  71.3 us
    pmax x1, blocking collectives, per_device(): peak = lax.pmax(local_peak, 'tensor')  42.1 us
    psum x1, blocking collectives, per_device(): summed_mix, summed_totals = lax.psum((mixture, partial_totals), 'tensor')  40.4 us
    scatter x1, local copies, waits for them, and re-layouts, per_device(): outgoing = jnp.zeros((tensor_count * capacity, model_width), jnp.bfloat16...  32.7 us
  transfers between devices with their start and end apart: 3, of which 3 were waited for; matrix products, arithmetic and copies ran while one was open for 1% of the time, Pallas kernels for 0%

commit v1 on v0

v1 whole, which is shorter than its diff:
```python
import math

import jax
import jax.numpy as jnp
from jax import lax
from jax.sharding import PartitionSpec as P

HEADS = 16
HEAD_DIM = 128


def expert_mlp(inputs, gate_w, up_w, down_w):
    flat_rows = inputs.reshape(-1, inputs.shape[-1])
    gate = jnp.dot(flat_rows, gate_w, preferred_element_type=jnp.float32)
    upper = jnp.dot(flat_rows, up_w, preferred_element_type=jnp.float32)
    active = (jax.nn.silu(gate) * upper).astype(jnp.bfloat16)
    return jnp.dot(active, down_w, preferred_element_type=jnp.float32)


def attention_rows(
    decode_queries,
    new_keys,
    new_values,
    cache_keys,
    cache_values,
    group_of,
    cache_lengths,
    decode_residual,
    out_weight,
):
    tensor_count = lax.axis_size("tensor")
    tensor_rank = lax.axis_index("tensor")
    requests = decode_queries.shape[1]
    groups = cache_keys.shape[1]
    reach = cache_keys.shape[2]
    model_width = decode_queries.shape[2]
    width = out_weight.shape[0]
    assert HEAD_DIM % width == 0
    factor = 1.0 / math.sqrt(HEAD_DIM)
    query_heads = decode_queries[0].reshape(requests, HEADS, HEAD_DIM)
    key_table = cache_keys[0].reshape(groups, reach, HEADS, HEAD_DIM)
    value_table = cache_values[0].reshape(groups, reach, HEADS, HEAD_DIM)
    scores = (
        jnp.einsum("rhd,gjhd->grhj", query_heads, key_table, preferred_element_type=jnp.float32)
        * factor
    )
    positions = tensor_rank * reach + jnp.arange(reach, dtype=jnp.int32)
    member = group_of[0][None, :] == jnp.arange(groups, dtype=jnp.int32)[:, None]
    within = positions[None, :] < cache_lengths[0][:, None]
    visible = (member[:, :, None] & within[:, None, :])[:, :, None, :]
    own_keys = new_keys[0].astype(jnp.float32).reshape(requests, HEADS, HEAD_DIM)
    own_score = jnp.sum(query_heads.astype(jnp.float32) * own_keys, axis=2) * factor
    local_peak = jnp.maximum(jnp.max(jnp.where(visible, scores, -jnp.inf), axis=(0, 3)), own_score)
    expon = jnp.where(visible, jnp.exp(scores - local_peak[None, :, :, None]), 0.0)
    probs = expon.astype(jnp.bfloat16)
    local_totals = jnp.sum(expon, axis=(0, 3))
    mixture = jnp.einsum(
        "grhj,gjhd->rhd", probs, value_table, preferred_element_type=jnp.float32
    ).reshape(requests, tensor_count, width)
    head_of = (jnp.arange(tensor_count, dtype=jnp.int32) * width) // HEAD_DIM
    peak_to = local_peak.T[head_of]
    totals_to = local_totals.T[head_of]
    payload = jnp.concatenate(
        [jnp.transpose(mixture, (1, 0, 2)), peak_to[:, :, None], totals_to[:, :, None]], axis=2
    )
    received = lax.all_to_all(payload, "tensor", 0, 0, tiled=True)
    part_mix = received[:, :, :width]
    part_peak = received[:, :, width]
    part_totals = received[:, :, width + 1]
    peak = jnp.max(part_peak, axis=0)
    scale = jnp.exp(part_peak - peak[None, :])
    my_head = (tensor_rank * width) // HEAD_DIM
    first_column = tensor_rank * width
    own_here = lax.dynamic_index_in_dim(own_score, my_head, axis=1, keepdims=False)
    own_exp = jnp.exp(own_here - peak)
    own_prob = lax.optimization_barrier(own_exp.astype(jnp.bfloat16)).astype(jnp.float32)
    totals = jnp.sum(scale * part_totals, axis=0) + own_exp
    own_values = lax.dynamic_slice_in_dim(new_values[0], first_column, width, 1).astype(jnp.float32)
    summed_mix = jnp.sum(scale[:, :, None] * part_mix, axis=0) + own_prob[:, None] * own_values
    attended = (summed_mix / totals[:, None]).astype(jnp.bfloat16)
    partial = jnp.dot(attended, out_weight, preferred_element_type=jnp.float32)
    per_device = requests // tensor_count
    gathered = lax.all_to_all(
        partial.reshape(tensor_count, per_device, model_width), "tensor", 0, 0, tiled=True
    )
    projected = jnp.sum(gathered, axis=0)
    return (decode_residual[0].astype(jnp.float32) + projected).astype(jnp.bfloat16)


def per_device(
    decode_queries,
    new_keys,
    new_values,
    cache_keys,
    cache_values,
    group_of,
    cache_lengths,
    decode_residual,
    out_weight,
    prefill_states,
    norm_gain,
    routes,
    route_weights,
    w_gate,
    w_up,
    w_down,
):
    tensor_count = lax.axis_size("tensor")
    model_width = decode_queries.shape[2]
    decode_hidden = attention_rows(
        decode_queries,
        new_keys,
        new_values,
        cache_keys,
        cache_values,
        group_of,
        cache_lengths,
        decode_residual,
        out_weight,
    )
    residual_rows = jnp.concatenate([prefill_states, decode_hidden], axis=0)
    row_float = residual_rows.astype(jnp.float32)
    inverse = lax.rsqrt(jnp.mean(row_float * row_float, axis=1, keepdims=True) + 1e-06)
    normed = (row_float * inverse * norm_gain).astype(jnp.bfloat16)
    row_count, top_count = routes.shape
    capacity = max(8, (row_count * top_count * 3 // (2 * tensor_count) + 7) // 8 * 8)
    flat_expert = routes.reshape(-1)
    one_hot = (flat_expert[:, None] == jnp.arange(tensor_count, dtype=jnp.int32)[None, :]).astype(
        jnp.int32
    )
    earlier = jnp.cumsum(one_hot, axis=0) - one_hot
    rank_within = jnp.sum(earlier * one_hot, axis=1)
    slot_index = flat_expert * capacity + rank_within
    slots = jnp.arange(tensor_count * capacity, dtype=jnp.int32)
    select = jnp.any(
        slot_index.reshape(row_count, top_count)[None, :, :] == slots[:, None, None], axis=2
    ).astype(jnp.bfloat16)
    outgoing = jnp.dot(select, normed, preferred_element_type=jnp.float32).astype(jnp.bfloat16)
    outgoing = outgoing.reshape(tensor_count, capacity, model_width)
    both_groups = lax.all_gather(
        lax.all_to_all(outgoing, "tensor", split_axis=0, concat_axis=0, tiled=True),
        "dp",
        axis=0,
        tiled=True,
    )
    block = both_groups
    returned = lax.all_to_all(
        lax.psum_scatter(
            expert_mlp(block, w_gate[0], w_up[0], w_down[0])
            .reshape(block.shape)
            .astype(jnp.bfloat16),
            "dp",
            scatter_dimension=0,
            tiled=True,
        ),
        "tensor",
        split_axis=0,
        concat_axis=0,
        tiled=True,
    )
    gathered = returned.reshape(tensor_count * capacity, model_width)[slot_index].astype(
        jnp.float32
    )
    weighted = jnp.sum(
        (gathered * route_weights.reshape(-1)[:, None]).reshape(row_count, top_count, model_width),
        axis=1,
    )
    mixed_rows = (row_float + weighted).astype(jnp.bfloat16)
    prefill_count = prefill_states.shape[0]
    return (mixed_rows[:prefill_count], mixed_rows[prefill_count:][None])


def solution(mesh):
    in_specs = (
        P("dp", None, None),
        P("dp", None, None),
        P("dp", None, None),
        P("dp", None, "tensor", None),
        P("dp", None, "tensor", None),
        P("dp", None),
        P("dp", None),
        P("dp", "tensor", None),
        P("tensor", None),
        P(("dp", "tensor"), None),
        P(),
        P(("dp", "tensor"), None),
        P(("dp", "tensor"), None),
        P("tensor", None, "dp"),
        P("tensor", None, "dp"),
        P("tensor", "dp", None),
    )
    out_specs = (P(("dp", "tensor"), None), P("dp", "tensor", None))
    return jax.shard_map(
        per_device, mesh=mesh, in_specs=in_specs, out_specs=out_specs, check_vma=False
    )
```

time: 537 us -> 232 us (0.43)
  waiting for transfers between devices: 281 us -> 94.4 us
  blocking collectives: 157 us -> 73.4 us
  local copies, waits for them, and re-layouts: 50.2 us -> 19.3 us
  between operations: 14.4 us -> 1.06 us
  starting transfers between devices: 3.76 us -> 14.2 us
    unnamed x3 -> x0, waiting for transfers between devices: 128 us -> none
    psum x1 -> x0, waiting for transfers between devices: 81.4 us -> none  [per_device(): summed_mix, summed_totals = lax.psum((mixture, partial_totals), 'tensor')]
    pmax x1 -> x0, blocking collectives: 42.1 us -> none  [per_device(): peak = lax.pmax(local_peak, 'tensor')]
    psum x1 -> x0, blocking collectives: 40.4 us -> none  [per_device(): summed_mix, summed_totals = lax.psum((mixture, partial_totals), 'tensor')]
    scatter x1 -> x0, local copies, waits for them, and re-layouts: 32.7 us -> none  [per_device(): outgoing = jnp.zeros((tensor_count * capacity, model_width), jnp.bfloat16...]
    all_to_all x0 -> x2, waiting for transfers between devices: none -> 23.2 us  [the longest x1 13.5 us: attention_rows(): received = lax.all_to_all(payload, 'tensor', 0, 0, tiled=True)]
    all_to_all x0 -> x2, starting transfers between devices: none -> 10.6 us  [the longest x1 7.3 us: attention_rows(): received = lax.all_to_all(payload, 'tensor', 0, 0, tiled=True)]
where the time goes in v1:
time: 232 us
  waiting for transfers between devices  94.4 us (41%)
  blocking collectives  73.4 us (32%)
  local copies, waits for them, and re-layouts  19.3 us (8%)
  matrix products  18.9 us (8%)
  starting transfers between devices  14.2 us (6%)
  other arithmetic  10.6 us (5%)
    all_to_all x1, blocking collectives, per_device(): lax.all_to_all(outgoing, 'tensor', split_axis=0, concat_axis=0, tiled=True)  73.4 us
    all_to_all x1, waiting for transfers between devices, per_device(): lax.all_to_all(lax.psum_scatter(expert_mlp(block, w_gate[0], w_up[0], w_d...  71.2 us
    all_to_all x1, waiting for transfers between devices, attention_rows(): received = lax.all_to_all(payload, 'tensor', 0, 0, tiled=True)  13.5 us
    all_to_all x1, waiting for transfers between devices, attention_rows(): lax.all_to_all(partial.reshape(tensor_count, per_device, model_width), 't...  9.63 us
    unnamed x28, local copies, waits for them, and re-layouts  8.92 us
    all_to_all x1, starting transfers between devices, attention_rows(): received = lax.all_to_all(payload, 'tensor', 0, 0, tiled=True)  7.3 us
    dot_general x1, matrix products, expert_mlp(): return jnp.dot(active, down_w, preferred_element_type=jnp.float32)  4.83 us
  transfers between devices with their start and end apart: 3, of which 3 were waited for; matrix products, arithmetic and copies ran while one was open for 1% of the time, Pallas kernels for 0%

profile of v1, /device:TPU:0, one launch (start us, length us, event | category | flops | bytes accessed | tf_op | source)
XLA Modules:
  0.0 231.9 jit_solution(13010993246244983397)
XLA Ops:
  1.4 0.9 copy.96
  2.3 0.9 convert_bitcast_fusion
  3.5 3.6 %copy.95 = bf16[128,8,16,128]{3,2,1,0:T(8,128)(2,1)S(1)} copy(bf16[128,8,16,128]{3,1,2,0:T(8,128)(2,1)} %bitcast.134) | data formatting | bytes 8388608
  7.3 2.5 %fusion.16 = (f32[32,16]{0,1:T(8,128)S(1)}, f32[16,4,256,32]{2,3,1,0:T(8,128)S(1)}) fusion(pred[4,32,256]{2,1,0:T(8,128)(4,1)S(1)} %broadcast_and_fusion, bf16[32,16,128,1]{2,1,0,3:T(8,128)(2,1)S(1)} %bitcast.145, bf16[4,256,16,128]{3,2,1,0:T(8,128)(2,1)S(1)} %bitcast.136), kind=kOutput, calls=%fused_computation.21 | convolution fusion | flops 135790080 | bytes 6457344 | tf_op jit(solution)/shard_map/rhd,gjhd->grhj/dot_general | solution.py:44
  12.6 3.6 %copy.98 = bf16[128,8,16,128]{3,2,1,0:T(8,128)(2,1)S(1)} copy(bf16[128,8,16,128]{3,1,2,0:T(8,128)(2,1)} %bitcast.135) | data formatting | bytes 8388608
  16.2 2.4 %fusion.22 = f32[32,16,128]{2,0,1:T(8,128)S(1)} fusion(bf16[4,256,16,128]{3,2,1,0:T(8,128)(2,1)S(1)} %bitcast.137, f32[16,4,256,32]{2,3,1,0:T(8,128)S(1)} %get-tuple-element.10, f32[32,16]{0,1:T(8,128)S(1)} %get-tuple-element.8, pred[4,32,256]{2,1,0:T(8,128)(4,1)S(1)} %broadcast_and_fusion), kind=kOutput, calls=%fused_computation.28 | convolution fusion | flops 136314880 | bytes 6588416 | tf_op jit(solution)/shard_map/grhj,gjhd->rhd/dot_general | solution.py:57
  19.3 1.1 copy.77
  20.4 7.3 %all-to-all-start = ((f32[32,32,66]{2,1,0:T(8,128)}), f32[32,32,66]{2,1,0:T(8,128)S(1)}, u32[]{:S(2)}, u32[]{:S(2)}) async-start(f32[32,32,66]{2,1,0:T(8,128)} %copy.77), calls=%async_computation | async-start | bytes 1048576 | tf_op jit(solution)/shard_map/all_to_all | solution.py:66
  28.0 1.5 reduce-window.6
  29.7 13.5 %all-to-all-done = f32[32,32,66]{2,1,0:T(8,128)S(1)} async-done(((f32[32,32,66]{2,1,0:T(8,128)}), f32[32,32,66]{2,1,0:T(8,128)S(1)}, u32[]{:S(2)}, u32[]{:S(2)}) %all-to-all-start) | async-done | bytes 270368 | tf_op jit(solution)/shard_map/all_to_all | solution.py:66
  44.5 0.9 convolution_bitcast_fusion
  45.5 1.0 copy.80
  46.4 3.3 %all-to-all-start.1 = ((f32[32,1,2048]{2,1,0:T(1,128)}), f32[32,1,2048]{2,1,0:T(1,128)S(1)}, u32[]{:S(2)}, u32[]{:S(2)}) async-start(f32[32,1,2048]{2,1,0:T(1,128)} %copy.80), calls=%async_computation.1 | async-start | bytes 524288 | tf_op jit(solution)/shard_map/all_to_all | solution.py:83
  50.5 9.6 %all-to-all-done.1 = f32[32,1,2048]{2,1,0:T(1,128)S(1)} async-done(((f32[32,1,2048]{2,1,0:T(1,128)}), f32[32,1,2048]{2,1,0:T(1,128)S(1)}, u32[]{:S(2)}, u32[]{:S(2)}) %all-to-all-start.1) | async-done | bytes 262176 | tf_op jit(solution)/shard_map/all_to_all | solution.py:83
  60.5 1.1 convolution_convert_fusion
  61.6 73.4 %all_to_all.20 = bf16[32,24,2048]{2,1,0:T(8,128)(2,1)S(1)} all-to-all(bf16[32,24,2048]{2,1,0:T(8,128)(2,1)S(1)} %bitcast.133), channel_id=1, replica_groups=mesh['dp'=1,'tensor'=32] {'tensor'}, dimensions={0} | all-to-all | bytes 6291456 | tf_op jit(solution)/shard_map/all_to_all | solution.py:141
  135.0 3.4 %fusion.3 = f32[768,1024]{1,0:T(8,128)S(1)} fusion(bf16[768,2048]{1,0:T(8,128)(2,1)S(1)} %bitcast.138, bf16[1,2048,1024]{2,1,0:T(8,128)(2,1)S(1)} %copy-done.7), kind=kOutput, calls=%fused_computation.7 | convolution fusion | flops 3221225472 | bytes 10485760 | tf_op jit(solution)/shard_map/dot_general | solution.py:15
  138.4 3.8 %multiply_convert_fusion = bf16[768,1024]{1,0:T(8,128)(2,1)S(1)} fusion(f32[768,1024]{1,0:T(8,128)S(1)} %fusion.3, bf16[768,2048]{1,0:T(8,128)(2,1)S(1)} %bitcast.139, bf16[1,2048,1024]{2,1,0:T(8,128)(2,1)S(1)} %copy-done.8), kind=kOutput, calls=%fused_computation.17 | convolution fusion | flops 3225944064 | bytes 12058624 | tf_op jit(solution)/shard_map/dot_general | solution.py:14
  142.2 4.8 %fusion.11 = bf16[32,24,2048]{2,1,0:T(8,128)(2,1)} fusion(bf16[32,24,1024]{2,1,0:T(8,128)(2,1)S(1)} %bitcast.153, bf16[1,1024,2048]{2,1,0:T(8,128)(2,1)S(1)} %copy-done.9), kind=kOutput, calls=%fused_computation.15 | convolution fusion | flops 3222798336 | bytes 8912896 | tf_op jit(solution)/shard_map/dot_general | solution.py:17
  147.0 3.7 %all-to-all-start.3 = ((bf16[32,24,2048]{2,1,0:T(8,128)(2,1)}), bf16[32,24,2048]{2,1,0:T(8,128)(2,1)S(1)}, u32[]{:S(2)}, u32[]{:S(2)}) async-start(bf16[32,24,2048]{2,1,0:T(8,128)(2,1)} %fusion.11), calls=%async_computation.3 | async-start | bytes 6291456 | tf_op jit(solution)/shard_map/all_to_all | solution.py:147
  151.0 71.2 %all-to-all-done.3 = bf16[32,24,2048]{2,1,0:T(8,128)(2,1)S(1)} async-done(((bf16[32,24,2048]{2,1,0:T(8,128)(2,1)}), bf16[32,24,2048]{2,1,0:T(8,128)(2,1)S(1)}, u32[]{:S(2)}, u32[]{:S(2)}) %all-to-all-start.3) | async-done | bytes 3145760 | tf_op jit(solution)/shard_map/all_to_all | solution.py:147
  222.2 3.9 %gather_fusion.2 = bf16[520,2048]{1,0:T(8,128)(2,1)} fusion(bf16[768,2048]{1,0:T(8,128)(2,1)S(1)} %bitcast.132, s32[1024]{0:T(1024)S(1)} %pad_clamp_fusion), kind=kCustom, calls=%fused_computation.2 | custom fusion | bytes 4261920 | tf_op jit(solution)/shard_map/gather | solution.py:161
  226.1 3.4 %fusion = f32[65,2048]{1,0:T(8,128)S(1)} fusion(bf16[520,2048]{1,0:T(8,128)(2,1)} %gather_fusion.2, f32[65,8]{1,0:T(8,128)S(1)} %copy.85), kind=kLoop, calls=%fused_computation.4 | loop fusion | flops 3061760 | bytes 2664480 | tf_op jit(solution)/shard_map/reduce_sum | solution.py:164
  229.5 1.0 fusion.33
  (68 shorter events, 9.0 us)
Async XLA Ops:
  0.6 43.9 %copy-start = (bf16[64,2048]{1,0:T(8,128)(2,1)S(1)}, bf16[64,2048]{1,0:T(8,128)(2,1)}, u32[]{:S(2)}) copy-start(bf16[64,2048]{1,0:T(8,128)(2,1)} %param.24) | copy-start | bytes 786436
  3.5 3.6 %copy-start.6 = (s32[1,4]{1,0:T(1,128)S(1)}, s32[1,4]{1,0:T(1,128)}, u32[]{:S(2)}) copy-start(s32[1,4]{1,0:T(1,128)} %param.22) | copy-start | bytes 52
  18.6 9.1 %copy-start.4 = (s32[65,8]{0,1:T(8,128)S(1)}, s32[65,8]{0,1:T(8,128)}, u32[]{:S(2)}) copy-start(s32[65,8]{0,1:T(8,128)} %param.27) | copy-start | bytes 6244
  20.4 22.9 %all-to-all-start = ((f32[32,32,66]{2,1,0:T(8,128)}), f32[32,32,66]{2,1,0:T(8,128)S(1)}, u32[]{:S(2)}, u32[]{:S(2)}) async-start(f32[32,32,66]{2,1,0:T(8,128)} %copy.77), calls=%async_computation | async-start | bytes 1048576 | tf_op jit(solution)/shard_map/all_to_all | solution.py:66
  29.4 30.9 %copy-start.3 = (bf16[1,1,2048]{2,1,0:T(2,128)(2,1)S(1)}, bf16[1,1,2048]{2,1,0:T(2,128)(2,1)}, u32[]{:S(2)}) copy-start(bf16[1,1,2048]{2,1,0:T(2,128)(2,1)} %param.23) | copy-start | bytes 12292
  29.7 30.6 %copy-start.1 = (bf16[64,2048]{1,0:T(8,128)(2,1)S(1)}, bf16[64,2048]{1,0:T(8,128)(2,1)}, u32[]{:S(2)}) copy-start(bf16[64,2048]{1,0:T(8,128)(2,1)} %param.25) | copy-start | bytes 786436
  29.7 30.8 %copy-start.2 = (f32[2048]{0:T(1024)S(1)}, f32[2048]{0:T(1024)}, u32[]{:S(2)}) copy-start(f32[2048]{0:T(1024)} %param.26) | copy-start | bytes 24580
  46.4 13.7 %all-to-all-start.1 = ((f32[32,1,2048]{2,1,0:T(1,128)}), f32[32,1,2048]{2,1,0:T(1,128)S(1)}, u32[]{:S(2)}, u32[]{:S(2)}) async-start(f32[32,1,2048]{2,1,0:T(1,128)} %copy.80), calls=%async_computation.1 | async-start | bytes 524288 | tf_op jit(solution)/shard_map/all_to_all | solution.py:83
  61.6 73.4 %copy-start.7 = (bf16[1,2048,1024]{2,1,0:T(8,128)(2,1)S(1)}, bf16[1,2048,1024]{2,1,0:T(8,128)(2,1)}, u32[]{:S(2)}) copy-start(bf16[1,2048,1024]{2,1,0:T(8,128)(2,1)} %param.30) | copy-start | bytes 12582916
  135.0 3.4 %copy-start.8 = (bf16[1,2048,1024]{2,1,0:T(8,128)(2,1)S(1)}, bf16[1,2048,1024]{2,1,0:T(8,128)(2,1)}, u32[]{:S(2)}) copy-start(bf16[1,2048,1024]{2,1,0:T(8,128)(2,1)} %param.29) | copy-start | bytes 12582916
  138.4 3.8 %copy-start.9 = (bf16[1,1024,2048]{2,1,0:T(8,128)(2,1)S(1)}, bf16[1,1024,2048]{2,1,0:T(8,128)(2,1)}, u32[]{:S(2)}) copy-start(bf16[1,1024,2048]{2,1,0:T(8,128)(2,1)} %param.31) | copy-start | bytes 12582916
  147.0 3.7 %copy-start.5 = (f32[65,8]{0,1:T(8,128)S(1)}, f32[65,8]{0,1:T(8,128)}, u32[]{:S(2)}) copy-start(f32[65,8]{0,1:T(8,128)} %param.28) | copy-start | bytes 6244
  147.0 75.1 %all-to-all-start.3 = ((bf16[32,24,2048]{2,1,0:T(8,128)(2,1)}), bf16[32,24,2048]{2,1,0:T(8,128)(2,1)S(1)}, u32[]{:S(2)}, u32[]{:S(2)}) async-start(bf16[32,24,2048]{2,1,0:T(8,128)(2,1)} %fusion.11), calls=%async_computation.3 | async-start | bytes 6291456 | tf_op jit(solution)/shard_map/all_to_all | solution.py:147

commit v2 on v1

--- a/solution.py
+++ b/solution.py
@@ -17,24 +17,14 @@
     return jnp.dot(active, down_w, preferred_element_type=jnp.float32)
 
 
-def attention_rows(
-    decode_queries,
-    new_keys,
-    new_values,
-    cache_keys,
-    cache_values,
-    group_of,
-    cache_lengths,
-    decode_residual,
-    out_weight,
+def attention_partials(
+    decode_queries, new_keys, cache_keys, cache_values, group_of, cache_lengths, width
 ):
     tensor_count = lax.axis_size("tensor")
     tensor_rank = lax.axis_index("tensor")
     requests = decode_queries.shape[1]
     groups = cache_keys.shape[1]
     reach = cache_keys.shape[2]
-    model_width = decode_queries.shape[2]
-    width = out_weight.shape[0]
     assert HEAD_DIM % width == 0
     factor = 1.0 / math.sqrt(HEAD_DIM)
     query_heads = decode_queries[0].reshape(requests, HEADS, HEAD_DIM)
@@ -63,7 +53,14 @@
     payload = jnp.concatenate(
         [jnp.transpose(mixture, (1, 0, 2)), peak_to[:, :, None], totals_to[:, :, None]], axis=2
     )
-    received = lax.all_to_all(payload, "tensor", 0, 0, tiled=True)
+    return payload, own_score
+
+
+def attention_finish(received, own_score, new_values, decode_residual, out_weight):
+    tensor_count = lax.axis_size("tensor")
+    tensor_rank = lax.axis_index("tensor")
+    requests, model_width = new_values.shape[1], new_values.shape[2]
+    width = out_weight.shape[0]
     part_mix = received[:, :, :width]
     part_peak = received[:, :, width]
     part_totals = received[:, :, width + 1]
@@ -87,6 +84,37 @@
     return (decode_residual[0].astype(jnp.float32) + projected).astype(jnp.bfloat16)
 
 
+def rms_normed(residual_rows, norm_gain):
+    row_float = residual_rows.astype(jnp.float32)
+    inverse = lax.rsqrt(jnp.mean(row_float * row_float, axis=1, keepdims=True) + 1e-06)
+    return row_float, (row_float * inverse * norm_gain).astype(jnp.bfloat16)
+
+
+def dispatch(normed, slot_index, slot_count):
+    row_count = normed.shape[0]
+    slots = jnp.arange(slot_count, dtype=jnp.int32)
+    select = jnp.any(
+        slot_index.reshape(row_count, -1)[None, :, :] == slots[:, None, None], axis=2
+    ).astype(jnp.bfloat16)
+    outgoing = jnp.dot(select, normed, preferred_element_type=jnp.float32).astype(jnp.bfloat16)
+    tensor_count = lax.axis_size("tensor")
+    outgoing = outgoing.reshape(tensor_count, slot_count // tensor_count, normed.shape[1])
+    return lax.all_to_all(outgoing, "tensor", split_axis=0, concat_axis=0, tiled=True)
+
+
+def experts_on(received, experts):
+    block = lax.all_gather(received, "dp", axis=0, tiled=True)
+    return expert_mlp(block, *experts).reshape(block.shape).astype(jnp.bfloat16)
+
+
+def rank_in_expert(flat_expert, tensor_count):
+    one_hot = (flat_expert[:, None] == jnp.arange(tensor_count, dtype=jnp.int32)[None, :]).astype(
+        jnp.int32
+    )
+    earlier = jnp.cumsum(one_hot, axis=0) - one_hot
+    return jnp.sum(earlier * one_hot, axis=1)
+
+
 def per_device(
     decode_queries,
     new_keys,
@@ -107,66 +135,63 @@
 ):
     tensor_count = lax.axis_size("tensor")
     model_width = decode_queries.shape[2]
-    decode_hidden = attention_rows(
-        decode_queries,
-        new_keys,
-        new_values,
-        cache_keys,
-        cache_values,
-        group_of,
-        cache_lengths,
-        decode_residual,
-        out_weight,
-    )
-    residual_rows = jnp.concatenate([prefill_states, decode_hidden], axis=0)
-    row_float = residual_rows.astype(jnp.float32)
-    inverse = lax.rsqrt(jnp.mean(row_float * row_float, axis=1, keepdims=True) + 1e-06)
-    normed = (row_float * inverse * norm_gain).astype(jnp.bfloat16)
+    prefill_count = prefill_states.shape[0]
     row_count, top_count = routes.shape
+    decode_count = row_count - prefill_count
     capacity = max(8, (row_count * top_count * 3 // (2 * tensor_count) + 7) // 8 * 8)
-    flat_expert = routes.reshape(-1)
-    one_hot = (flat_expert[:, None] == jnp.arange(tensor_count, dtype=jnp.int32)[None, :]).astype(
-        jnp.int32
-    )
-    earlier = jnp.cumsum(one_hot, axis=0) - one_hot
-    rank_within = jnp.sum(earlier * one_hot, axis=1)
-    slot_index = flat_expert * capacity + rank_within
-    slots = jnp.arange(tensor_count * capacity, dtype=jnp.int32)
-    select = jnp.any(
-        slot_index.reshape(row_count, top_count)[None, :, :] == slots[:, None, None], axis=2
-    ).astype(jnp.bfloat16)
-    outgoing = jnp.dot(select, normed, preferred_element_type=jnp.float32).astype(jnp.bfloat16)
-    outgoing = outgoing.reshape(tensor_count, capacity, model_width)
-    both_groups = lax.all_gather(
-        lax.all_to_all(outgoing, "tensor", split_axis=0, concat_axis=0, tiled=True),
-        "dp",
-        axis=0,
-        tiled=True,
-    )
-    block = both_groups
+    stride = capacity + decode_count
+    experts = (w_gate[0], w_up[0], w_down[0])
+    prefill_routes = routes[:prefill_count].reshape(-1)
+    decode_routes = routes[prefill_count:]
+    prefill_rank = rank_in_expert(prefill_routes, tensor_count)
+    prefill_float, prefill_normed = rms_normed(prefill_states, norm_gain)
+    prefill_in = dispatch(
+        prefill_normed, prefill_routes * capacity + prefill_rank, tensor_count * capacity
+    )
+    payload, own_score = attention_partials(
+        decode_queries, new_keys, cache_keys, cache_values, group_of, cache_lengths,
+        out_weight.shape[0],
+    )
+    payload, prefill_in = lax.optimization_barrier((payload, prefill_in))
+    received = lax.all_to_all(payload, "tensor", 0, 0, tiled=True)
+    prefill_done = experts_on(prefill_in, experts)
+    decode_hidden = attention_finish(received, own_score, new_values, decode_residual, out_weight)
+    decode_float, decode_normed = rms_normed(decode_hidden, norm_gain)
+    decode_slot = decode_routes * decode_count + jnp.arange(decode_count, dtype=jnp.int32)[:, None]
+    decode_in = dispatch(decode_normed, decode_slot.reshape(-1), tensor_count * decode_count)
+    decode_done = experts_on(decode_in, experts)
+    merged = jnp.concatenate([prefill_done, decode_done], axis=1)
     returned = lax.all_to_all(
-        lax.psum_scatter(
-            expert_mlp(block, w_gate[0], w_up[0], w_down[0])
-            .reshape(block.shape)
-            .astype(jnp.bfloat16),
-            "dp",
-            scatter_dimension=0,
-            tiled=True,
-        ),
+        lax.psum_scatter(merged, "dp", scatter_dimension=0, tiled=True),
         "tensor",
         split_axis=0,
         concat_axis=0,
         tiled=True,
-    )
-    gathered = returned.reshape(tensor_count * capacity, model_width)[slot_index].astype(
-        jnp.float32
-    )
-    weighted = jnp.sum(
-        (gathered * route_weights.reshape(-1)[:, None]).reshape(row_count, top_count, model_width),
+    ).reshape(tensor_count * stride, model_width)
+    place = jnp.concatenate(
+        [
+            prefill_routes.reshape(prefill_count, top_count) * stride
+            + prefill_rank.reshape(prefill_count, top_count),
+            decode_routes * stride + capacity
+            + jnp.arange(decode_count, dtype=jnp.int32)[:, None],
+        ],
+        axis=0,
+    )
+    columns = jnp.arange(tensor_count * stride, dtype=jnp.int32)
+    mixing = jnp.sum(
+        jnp.where(place[:, :, None] == columns[None, None, :], route_weights[:, :, None], 0.0),
         axis=1,
     )
+    high = mixing.astype(jnp.bfloat16)
+    rest = mixing - high.astype(jnp.float32)
+    middle = rest.astype(jnp.bfloat16)
+    low = (rest - middle.astype(jnp.float32)).astype(jnp.bfloat16)
+    parts = jnp.dot(
+        jnp.concatenate([high, middle, low], axis=0), returned, preferred_element_type=jnp.float32
+    ).reshape(3, row_count, model_width)
+    weighted = (parts[0] + parts[1]) + parts[2]
+    row_float = jnp.concatenate([prefill_float, decode_float], axis=0)
     mixed_rows = (row_float + weighted).astype(jnp.bfloat16)
-    prefill_count = prefill_states.shape[0]
     return (mixed_rows[:prefill_count], mixed_rows[prefill_count:][None])
 
 

time: 232 us -> 260 us (1.12)
  blocking collectives: 73.4 us -> 0 us
  waiting for transfers between devices: 94.4 us -> 142 us
  matrix products: 18.9 us -> 45.9 us
  local copies, waits for them, and re-layouts: 19.3 us -> 31.3 us
  starting transfers between devices: 14.2 us -> 22.8 us
  other arithmetic: 10.6 us -> 15.7 us
    all_to_all x1 -> x0, blocking collectives: 73.4 us -> none  [per_device(): lax.all_to_all(outgoing, 'tensor', split_axis=0, concat_axis=0, tiled=True)]
    all_to_all x3 -> x5, waiting for transfers between devices: 94.4 us -> 142 us  [the longest x1 91.4 us: per_device(): lax.all_to_all(lax.psum_scatter(merged, 'dp', scatter_dimension=0, tiled=...]
    dot_general x1 -> x2, matrix products: 3.78 us -> 12.6 us  [expert_mlp(): gate = jnp.dot(flat_rows, gate_w, preferred_element_type=jnp.float32)]
    all_to_all x3 -> x5, starting transfers between devices: 14.2 us -> 22.8 us  [the longest x2 11.8 us: dispatch(): lax.all_to_all(outgoing, 'tensor', split_axis=0, concat_axis=0, tiled=True)]
    dot_general x4 -> x5, matrix products: 6.9 us -> 13.8 us  [the longest x1 4.67 us: attention_partials(): jnp.einsum('rhd,gjhd->grhj', query_heads, key_table, preferred_element_ty...]
    dot_general x1 -> x2, matrix products: 4.83 us -> 11.2 us  [expert_mlp(): return jnp.dot(active, down_w, preferred_element_type=jnp.float32)]
    reshape x2 -> x4, local copies, waits for them, and re-layouts: 1.12 us -> 6.82 us  [the longest x1 3.42 us: per_device(): returned = lax.all_to_all(lax.psum_scatter(merged, 'dp', scatter_dimensio...]
    unnamed x28 -> x47, local copies, waits for them, and re-layouts: 8.92 us -> 14 us
  transfers between devices with their start and end apart: 3 -> 5, of which waited for: 3 -> 5; matrix products, arithmetic and copies ran while one was open for 1% -> 22% of each run, Pallas kernels for 0% -> 0%
where the time goes in v2:
time: 260 us; the launch traced here: 259 us
  waiting for transfers between devices  142 us (55%)
  matrix products  45.9 us (18%)
  local copies, waits for them, and re-layouts  31.3 us (12%)
  starting transfers between devices  22.8 us (9%)
  other arithmetic  15.7 us (6%)
    all_to_all x1, waiting for transfers between devices, per_device(): lax.all_to_all(lax.psum_scatter(merged, 'dp', scatter_dimension=0, tiled=...  91.4 us
    all_to_all x2, waiting for transfers between devices, dispatch(): lax.all_to_all(outgoing, 'tensor', split_axis=0, concat_axis=0, tiled=True)  41.7 us
    unnamed x47, local copies, waits for them, and re-layouts  14 us
    dot_general x2, matrix products, expert_mlp(): gate = jnp.dot(flat_rows, gate_w, preferred_element_type=jnp.float32)  12.6 us
    all_to_all x2, starting transfers between devices, dispatch(): lax.all_to_all(outgoing, 'tensor', split_axis=0, concat_axis=0, tiled=True)  11.8 us
    dot_general x2, matrix products, expert_mlp(): return jnp.dot(active, down_w, preferred_element_type=jnp.float32)  11.2 us
    dot_general x1, matrix products, expert_mlp(): upper = jnp.dot(flat_rows, up_w, preferred_element_type=jnp.float32)  8.26 us
    all_to_all x1, waiting for transfers between devices, per_device(): received = lax.all_to_all(payload, 'tensor', 0, 0, tiled=True)  7.11 us
  transfers between devices with their start and end apart: 5, of which 5 were waited for; matrix products, arithmetic and copies ran while one was open for 22% of the time, Pallas kernels for 0%

profile of v2, /device:TPU:0, one launch (start us, length us, event | category | flops | bytes accessed | tf_op | source)
XLA Modules:
  0.0 259.2 jit_solution(13667294084585249830)
XLA Ops:
  5.6 3.7 %convolution_convert_fusion = bf16[768,2048]{1,0:T(8,128)(2,1)} fusion(pred[768,64]{0,1:T(8,128)(4,1)S(1)} %fusion.32, f32[2048]{0:T(1024)} %param.26, f32[64]{0:T(128)S(1)} %add_rsqrt_fusion, bf16[64,2048]{1,0:T(8,128)(2,1)} %param.25), kind=kOutput, calls=%fused_computation.20 | convolution fusion | flops 203423744 | bytes 3465472 | tf_op jit(solution)/shard_map/dot_general | solution.py:99
  9.3 7.3 %all-to-all-start = ((bf16[32,24,2048]{2,1,0:T(8,128)(2,1)}), bf16[32,24,2048]{2,1,0:T(8,128)(2,1)S(1)}, u32[]{:S(2)}, u32[]{:S(2)}) async-start(bf16[32,24,2048]{2,1,0:T(8,128)(2,1)} %bitcast.15), calls=%async_computation | async-start | bytes 6291456 | tf_op jit(solution)/shard_map/all_to_all | solution.py:102
  18.2 5.6 %copy.118 = bf16[128,8,16,128]{3,2,1,0:T(8,128)(2,1)} copy(bf16[128,8,16,128]{3,1,2,0:T(8,128)(2,1)} %bitcast.167) | data formatting | bytes 8388608
  26.2 4.7 %fusion.27 = (f32[32,16]{0,1:T(8,128)S(1)}, f32[16,4,256,32]{2,3,1,0:T(8,128)S(1)}) fusion(pred[4,32,256]{2,1,0:T(8,128)(4,1)S(1)} %broadcast_and_fusion, bf16[32,16,128,1]{2,1,0,3:T(8,128)(2,1)S(1)} %bitcast.178, bf16[4,256,16,128]{3,2,1,0:T(8,128)(2,1)} %bitcast.169), kind=kOutput, calls=%fused_computation.27 | convolution fusion | flops 135790080 | bytes 6457344 | tf_op jit(solution)/shard_map/rhd,gjhd->grhj/dot_general | solution.py:34
  34.7 3.7 %copy.121 = bf16[128,8,16,128]{3,2,1,0:T(8,128)(2,1)S(1)} copy(bf16[128,8,16,128]{3,1,2,0:T(8,128)(2,1)} %bitcast.168) | data formatting | bytes 8388608
  38.5 2.4 fusion.33
  41.8 1.9 reshape.302
  45.8 2.5 pad_maximum_fusion.1
  48.2 39.8 %all-to-all-done = bf16[32,24,2048]{2,1,0:T(8,128)(2,1)S(1)} async-done(((bf16[32,24,2048]{2,1,0:T(8,128)(2,1)}), bf16[32,24,2048]{2,1,0:T(8,128)(2,1)S(1)}, u32[]{:S(2)}, u32[]{:S(2)}) %all-to-all-start) | async-done | bytes 3145760 | tf_op jit(solution)/shard_map/all_to_all | solution.py:102
  88.0 2.5 copy.99
  90.6 4.1 %all-to-all-start.1 = ((f32[32,32,66]{2,1,0:T(8,128)}), f32[32,32,66]{2,1,0:T(8,128)S(1)}, u32[]{:S(2)}, u32[]{:S(2)}) async-start(f32[32,32,66]{2,1,0:T(8,128)} %copy.99), calls=%async_computation.1 | async-start | bytes 1048576 | tf_op jit(solution)/shard_map/all_to_all | solution.py:156
  94.7 8.3 %fusion.6 = f32[768,1024]{1,0:T(8,128)} fusion(bf16[768,2048]{1,0:T(8,128)(2,1)} %bitcast.171, bf16[1,2048,1024]{2,1,0:T(8,128)(2,1)} %param.30), kind=kOutput, calls=%fused_computation.9 | convolution fusion | flops 3221225472 | bytes 10485760 | tf_op jit(solution)/shard_map/dot_general | solution.py:15
  102.9 7.1 %all-to-all-done.1 = f32[32,32,66]{2,1,0:T(8,128)S(1)} async-done(((f32[32,32,66]{2,1,0:T(8,128)}), f32[32,32,66]{2,1,0:T(8,128)S(1)}, u32[]{:S(2)}, u32[]{:S(2)}) %all-to-all-start.1) | async-done | bytes 270368 | tf_op jit(solution)/shard_map/all_to_all | solution.py:156
  113.2 3.1 %all-to-all-start.2 = ((f32[32,1,2048]{2,1,0:T(1,128)}), f32[32,1,2048]{2,1,0:T(1,128)S(1)}, u32[]{:S(2)}, u32[]{:S(2)}) async-start(f32[32,1,2048]{2,1,0:T(1,128)} %copy.102), calls=%async_computation.2 | async-start | bytes 524288 | tf_op jit(solution)/shard_map/all_to_all | solution.py:80
  116.3 9.0 %multiply_convert_fusion = bf16[768,1024]{1,0:T(8,128)(2,1)} fusion(f32[768,1024]{1,0:T(8,128)} %fusion.6, bf16[768,2048]{1,0:T(8,128)(2,1)} %bitcast.172, bf16[1,2048,1024]{2,1,0:T(8,128)(2,1)} %param.29), kind=kOutput, calls=%fused_computation.21 | convolution fusion | flops 3225944064 | bytes 12058624 | tf_op jit(solution)/shard_map/dot_general | solution.py:14
  130.4 4.5 %all-to-all-start.3 = ((bf16[32,2,1024]{2,1,0:T(2,128)(2,1)}), bf16[32,2,1024]{2,1,0:T(2,128)(2,1)S(1)}, u32[]{:S(2)}, u32[]{:S(2)}) async-start(bf16[32,2,1024]{2,1,0:T(2,128)(2,1)} %reshape.334), calls=%async_computation.3 | async-start | bytes 262144 | tf_op jit(solution)/shard_map/all_to_all | solution.py:102
  134.9 6.1 %fusion.16 = bf16[32,24,2048]{2,1,0:T(8,128)(2,1)S(1)} fusion(bf16[32,24,1024]{2,1,0:T(8,128)(2,1)} %bitcast.188, bf16[1,1024,2048]{2,1,0:T(8,128)(2,1)} %param.31), kind=kOutput, calls=%fused_computation.19 | convolution fusion | flops 3222798336 | bytes 8912896 | tf_op jit(solution)/shard_map/dot_general | solution.py:17
  143.0 3.6 %fusion.8 = f32[32,1024]{1,0:T(8,128)} fusion(bf16[1,2048,1024]{2,1,0:T(8,128)(2,1)} %param.29, bf16[32,1,2048]{2,1,0:T(2,128)(2,1)S(1)} %reshape.335), kind=kOutput, calls=%fused_computation.11 | convolution fusion | flops 134217728 | bytes 4456448 | tf_op jit(solution)/shard_map/dot_general | solution.py:14
  146.6 5.0 %fusion.22 = bf16[32,1,2048]{2,0,1:T(8,128)(2,1)S(1)} fusion(bf16[1,1024,2048]{2,1,0:T(8,128)(2,1)} %param.31, bf16[1,2048,1024]{2,1,0:T(8,128)(2,1)} %param.30, f32[32,1024]{1,0:T(8,128)} %fusion.8, bf16[32,1,2048]{2,1,0:T(2,128)(2,1)S(1)} %reshape.335), kind=kOutput, calls=%fused_computation.24 | convolution fusion | flops 268697600 | bytes 8781824 | tf_op jit(solution)/shard_map/dot_general | solution.py:17
  151.9 2.5 pad_maximum_fusion
  154.4 3.9 %all-to-all-start.4 = ((bf16[32,25,2048]{2,1,0:T(8,128)(2,1)}), bf16[32,25,2048]{2,1,0:T(8,128)(2,1)}, u32[]{:S(2)}, u32[]{:S(2)}) async-start(bf16[32,25,2048]{2,1,0:T(8,128)(2,1)} %pad_maximum_fusion), calls=%async_computation.4 | async-start | bytes 8388608 | tf_op jit(solution)/shard_map/all_to_all | solution.py:164
  160.7 91.4 %all-to-all-done.4 = bf16[32,25,2048]{2,1,0:T(8,128)(2,1)} async-done(((bf16[32,25,2048]{2,1,0:T(8,128)(2,1)}), bf16[32,25,2048]{2,1,0:T(8,128)(2,1)}, u32[]{:S(2)}, u32[]{:S(2)}) %all-to-all-start.4) | async-done | bytes 3276832 | tf_op jit(solution)/shard_map/all_to_all | solution.py:164
  252.1 3.4 %reshape.309 = bf16[800,2048]{1,0:T(8,128)(2,1)S(1)} reshape(bf16[32,25,2048]{2,1,0:T(8,128)(2,1)} %all-to-all-done.4) | data formatting | bytes 6553600 | tf_op jit(solution)/shard_map/reshape | solution.py:170
  255.6 2.1 fusion.52
  (105 shorter events, 29.2 us)
Async XLA Ops:
  0.6 110.7 %copy-start = (bf16[64,2048]{1,0:T(8,128)(2,1)S(1)}, bf16[64,2048]{1,0:T(8,128)(2,1)}, u32[]{:S(2)}) copy-start(bf16[64,2048]{1,0:T(8,128)(2,1)} %param.24) | copy-start | bytes 786436
  9.3 7.3 %copy-start.15 = (s32[65,8]{0,1:T(8,128)S(1)}, s32[65,8]{0,1:T(8,128)}, u32[]{:S(2)}) copy-start(s32[65,8]{0,1:T(8,128)} %param.27) | copy-start | bytes 6244
  9.3 78.8 %all-to-all-start = ((bf16[32,24,2048]{2,1,0:T(8,128)(2,1)}), bf16[32,24,2048]{2,1,0:T(8,128)(2,1)S(1)}, u32[]{:S(2)}, u32[]{:S(2)}) async-start(bf16[32,24,2048]{2,1,0:T(8,128)(2,1)} %bitcast.15), calls=%async_computation | async-start | bytes 6291456 | tf_op jit(solution)/shard_map/all_to_all | solution.py:102
  18.2 5.6 %copy-start.9 = (bf16[1,32,2048]{2,1,0:T(8,128)(2,1)S(1)}, bf16[1,32,2048]{2,1,0:T(8,128)(2,1)}, u32[]{:S(2)}) copy-start(bf16[1,32,2048]{2,1,0:T(8,128)(2,1)} %param.17) | copy-start | bytes 393220
  26.2 4.7 %copy-start.7 = (pred[4,32,256]{2,1,0:T(8,128)(4,1)}, pred[4,32,256]{2,1,0:T(8,128)(4,1)S(1)}, u32[]{:S(2)}) copy-start(pred[4,32,256]{2,1,0:T(8,128)(4,1)S(1)} %broadcast_and_fusion) | copy-start | bytes 98308
  26.2 4.7 %copy-start.14 = (f32[32,16]{0,1:T(8,128)S(1)}, f32[32,16]{0,1:T(8,128)}, u32[]{:S(2)}) copy-start(f32[32,16]{0,1:T(8,128)} %copy.92) | copy-start | bytes 6148
  30.9 1.4 copy-start.5
  34.7 3.7 %copy-start.6 = (f32[16,4,256,32]{2,3,1,0:T(8,128)S(1)}, f32[16,4,256,32]{2,3,1,0:T(8,128)}, u32[]{:S(2)}) copy-start(f32[16,4,256,32]{2,3,1,0:T(8,128)} %copy-done.5) | copy-start | bytes 6291460
  34.7 3.8 %copy-start.8 = (pred[4,32,256]{2,1,0:T(8,128)(4,1)S(1)}, pred[4,32,256]{2,1,0:T(8,128)(4,1)}, u32[]{:S(2)}) copy-start(pred[4,32,256]{2,1,0:T(8,128)(4,1)} %copy-done.7) | copy-start | bytes 98308
  38.5 7.0 %copy-start.12 = (bf16[1,1,2048]{2,1,0:T(2,128)(2,1)S(1)}, bf16[1,1,2048]{2,1,0:T(2,128)(2,1)}, u32[]{:S(2)}) copy-start(bf16[1,1,2048]{2,1,0:T(2,128)(2,1)} %param.23) | copy-start | bytes 12292
  38.5 7.0 %copy-start.16 = (s32[1,8]{0,1:T(8,128)S(1)}, s32[1,8]{0,1:T(8,128)}, u32[]{:S(2)}) copy-start(s32[1,8]{0,1:T(8,128)} %slice.47) | copy-start | bytes 100
  88.0 2.5 copy-start.2
  90.6 19.5 %all-to-all-start.1 = ((f32[32,32,66]{2,1,0:T(8,128)}), f32[32,32,66]{2,1,0:T(8,128)S(1)}, u32[]{:S(2)}, u32[]{:S(2)}) async-start(f32[32,32,66]{2,1,0:T(8,128)} %copy.99), calls=%async_computation.1 | async-start | bytes 1048576 | tf_op jit(solution)/shard_map/all_to_all | solution.py:156
  113.2 13.7 %all-to-all-start.2 = ((f32[32,1,2048]{2,1,0:T(1,128)}), f32[32,1,2048]{2,1,0:T(1,128)S(1)}, u32[]{:S(2)}, u32[]{:S(2)}) async-start(f32[32,1,2048]{2,1,0:T(1,128)} %copy.102), calls=%async_computation.2 | async-start | bytes 524288 | tf_op jit(solution)/shard_map/all_to_all | solution.py:80
  116.3 12.1 %copy-start.11 = (f32[2048]{0:T(1024)S(1)}, f32[2048]{0:T(1024)}, u32[]{:S(2)}) copy-start(f32[2048]{0:T(1024)} %param.26) | copy-start | bytes 24580
  130.4 12.5 %all-to-all-start.3 = ((bf16[32,2,1024]{2,1,0:T(2,128)(2,1)}), bf16[32,2,1024]{2,1,0:T(2,128)(2,1)S(1)}, u32[]{:S(2)}, u32[]{:S(2)}) async-start(bf16[32,2,1024]{2,1,0:T(2,128)(2,1)} %reshape.334), calls=%async_computation.3 | async-start | bytes 262144 | tf_op jit(solution)/shard_map/all_to_all | solution.py:102
  154.4 3.9 %copy-start.3 = (bf16[64,2048]{1,0:T(8,128)(2,1)S(1)}, bf16[64,2048]{1,0:T(8,128)(2,1)}, u32[]{:S(2)}) copy-start(bf16[64,2048]{1,0:T(8,128)(2,1)} %param.25) | copy-start | bytes 786436
  154.4 4.8 %copy-start.17 = (f32[65,8]{0,1:T(8,128)S(1)}, f32[65,8]{0,1:T(8,128)}, u32[]{:S(2)}) copy-start(f32[65,8]{0,1:T(8,128)} %param.28) | copy-start | bytes 6244
  154.4 4.9 %copy-start.10 = (s32[64,8]{1,0:T(8,128)S(1)}, s32[64,8]{1,0:T(8,128)}, u32[]{:S(2)}) copy-start(s32[64,8]{1,0:T(8,128)} %get-tuple-element.14) | copy-start | bytes 6148
  154.4 6.3 %copy-start.13 = (bf16[1,1,2048]{2,1,0:T(2,128)(2,1)S(1)}, bf16[1,1,2048]{2,1,0:T(2,128)(2,1)}, u32[]{:S(2)}) copy-start(bf16[1,1,2048]{2,1,0:T(2,128)(2,1)} %param.23) | copy-start | bytes 12292
  154.4 97.7 %all-to-all-start.4 = ((bf16[32,25,2048]{2,1,0:T(8,128)(2,1)}), bf16[32,25,2048]{2,1,0:T(8,128)(2,1)}, u32[]{:S(2)}, u32[]{:S(2)}) async-start(bf16[32,25,2048]{2,1,0:T(8,128)(2,1)} %pad_maximum_fusion), calls=%async_computation.4 | async-start | bytes 8388608 | tf_op jit(solution)/shard_map/all_to_all | solution.py:164
  255.6 2.1 copy-start.4
  255.6 3.6 %copy-start.1 = (bf16[64,2048]{1,0:T(8,128)(2,1)S(1)}, bf16[64,2048]{1,0:T(8,128)(2,1)}, u32[]{:S(2)}) copy-start(bf16[64,2048]{1,0:T(8,128)(2,1)} %param.24) | copy-start | bytes 786436

commit v3 on v1

--- a/solution.py
+++ b/solution.py
@@ -60,13 +60,13 @@
     head_of = (jnp.arange(tensor_count, dtype=jnp.int32) * width) // HEAD_DIM
     peak_to = local_peak.T[head_of]
     totals_to = local_totals.T[head_of]
-    payload = jnp.concatenate(
-        [jnp.transpose(mixture, (1, 0, 2)), peak_to[:, :, None], totals_to[:, :, None]], axis=2
-    )
+    flat_mix = jnp.transpose(mixture, (1, 0, 2)).reshape(tensor_count, requests * width)
+    payload = jnp.concatenate([flat_mix, peak_to, totals_to], axis=1)
     received = lax.all_to_all(payload, "tensor", 0, 0, tiled=True)
-    part_mix = received[:, :, :width]
-    part_peak = received[:, :, width]
-    part_totals = received[:, :, width + 1]
+    mixed_width = requests * width
+    part_mix = received[:, :mixed_width].reshape(tensor_count, requests, width)
+    part_peak = received[:, mixed_width:mixed_width + requests]
+    part_totals = received[:, mixed_width + requests:]
     peak = jnp.max(part_peak, axis=0)
     scale = jnp.exp(part_peak - peak[None, :])
     my_head = (tensor_rank * width) // HEAD_DIM
@@ -158,16 +158,32 @@
         concat_axis=0,
         tiled=True,
     )
-    gathered = returned.reshape(tensor_count * capacity, model_width)[slot_index].astype(
-        jnp.float32
-    )
-    weighted = jnp.sum(
-        (gathered * route_weights.reshape(-1)[:, None]).reshape(row_count, top_count, model_width),
+    returned = returned.reshape(tensor_count * capacity, model_width)
+    columns = jnp.arange(tensor_count * capacity, dtype=jnp.int32)
+    mixing = jnp.sum(
+        jnp.where(
+            slot_index.reshape(row_count, top_count)[:, :, None] == columns[None, None, :],
+            route_weights[:, :, None],
+            0.0,
+        ),
         axis=1,
     )
-    mixed_rows = (row_float + weighted).astype(jnp.bfloat16)
+    high = mixing.astype(jnp.bfloat16)
+    rest = mixing - high.astype(jnp.float32)
+    middle = rest.astype(jnp.bfloat16)
+    low = (rest - middle.astype(jnp.float32)).astype(jnp.bfloat16)
     prefill_count = prefill_states.shape[0]
-    return (mixed_rows[:prefill_count], mixed_rows[prefill_count:][None])
+
+    def combined(lo, hi):
+        parts = jnp.dot(
+            jnp.concatenate([high[lo:hi], middle[lo:hi], low[lo:hi]], axis=0),
+            returned,
+            preferred_element_type=jnp.float32,
+        ).reshape(3, hi - lo, model_width)
+        weighted = (parts[0] + parts[1]) + parts[2]
+        return (row_float[lo:hi] + weighted).astype(jnp.bfloat16)
+
+    return (combined(0, prefill_count), combined(prefill_count, row_count)[None])
 
 
 def solution(mesh):

time: 232 us -> 221 us (0.953)
  waiting for transfers between devices: 94.4 us -> 86.2 us
  other arithmetic: 10.6 us -> 8.21 us
    all_to_all x1, waiting for transfers between devices: 13.5 us -> 9.1 us  [attention_rows(): received = lax.all_to_all(payload, 'tensor', 0, 0, tiled=True)]
    gather x1 -> x0, local copies, waits for them, and re-layouts: 3.88 us -> none  [per_device(): returned.reshape(tensor_count * capacity, model_width)[slot_index]]
    all_to_all x1, waiting for transfers between devices: 71.2 us -> 67.6 us  [per_device(): lax.all_to_all(lax.psum_scatter(expert_mlp(block, w_gate[0], w_up[0], w_d...]
    reduce_sum x1, other arithmetic: 3.43 us -> 0.55 us  [per_device(): jnp.sum(jnp.where(slot_index.reshape(row_count, top_count)[:, :, None] ==...]
    unnamed x28 -> x37, local copies, waits for them, and re-layouts: 8.92 us -> 11.1 us
  transfers between devices with their start and end apart: 3 -> 3, of which waited for: 3 -> 3; matrix products, arithmetic and copies ran while one was open for 1% -> 3% of each run, Pallas kernels for 0% -> 0%
where the time goes in v3:
time: 221 us; the launch traced here: 220 us
  waiting for transfers between devices  86.2 us (39%)
  blocking collectives  73.3 us (33%)
  matrix products  20.2 us (9%)
  local copies, waits for them, and re-layouts  17.5 us (8%)
  starting transfers between devices  13.7 us (6%)
  other arithmetic  8.21 us (4%)
    all_to_all x1, blocking collectives, per_device(): lax.all_to_all(outgoing, 'tensor', split_axis=0, concat_axis=0, tiled=True)  73.3 us
    all_to_all x1, waiting for transfers between devices, per_device(): lax.all_to_all(lax.psum_scatter(expert_mlp(block, w_gate[0], w_up[0], w_d...  67.6 us
    unnamed x37, local copies, waits for them, and re-layouts  11.1 us
    all_to_all x1, waiting for transfers between devices, attention_rows(): lax.all_to_all(partial.reshape(tensor_count, per_device, model_width), 't...  9.47 us
    all_to_all x1, waiting for transfers between devices, attention_rows(): received = lax.all_to_all(payload, 'tensor', 0, 0, tiled=True)  9.1 us
    all_to_all x1, starting transfers between devices, attention_rows(): received = lax.all_to_all(payload, 'tensor', 0, 0, tiled=True)  7.3 us
    dot_general x1, matrix products, expert_mlp(): return jnp.dot(active, down_w, preferred_element_type=jnp.float32)  4.81 us
  transfers between devices with their start and end apart: 3, of which 3 were waited for; matrix products, arithmetic and copies ran while one was open for 3% of the time, Pallas kernels for 0%

profile of v3, /device:TPU:0, one launch (start us, length us, event | category | flops | bytes accessed | tf_op | source)
XLA Modules:
  0.0 220.2 jit_solution(18312344146634356099)
XLA Ops:
  0.7 0.7 iota_compare_fusion.4
  1.4 0.9 copy.86
  2.3 5.6 %copy.85 = bf16[128,8,16,128]{3,2,1,0:T(8,128)(2,1)} copy(bf16[128,8,16,128]{3,1,2,0:T(8,128)(2,1)} %bitcast.124) | data formatting | bytes 8388608
  8.2 3.7 %copy.88 = bf16[128,8,16,128]{3,2,1,0:T(8,128)(2,1)S(1)} copy(bf16[128,8,16,128]{3,1,2,0:T(8,128)(2,1)} %bitcast.125) | data formatting | bytes 8388608
  12.1 2.5 %fusion.15 = (f32[32,16]{0,1:T(8,128)S(1)}, f32[16,4,256,32]{2,3,1,0:T(8,128)S(1)}) fusion(pred[4,32,256]{2,1,0:T(8,128)(4,1)S(1)} %broadcast_and_fusion, bf16[32,16,128,1]{2,1,0,3:T(8,128)(2,1)S(1)} %bitcast.139, bf16[4,256,16,128]{3,2,1,0:T(8,128)(2,1)S(1)} %bitcast.126), kind=kOutput, calls=%fused_computation.18 | convolution fusion | flops 135790080 | bytes 6457344 | tf_op jit(solution)/shard_map/rhd,gjhd->grhj/dot_general | solution.py:44
  15.3 2.4 %fusion.21 = f32[32,16,128]{2,0,1:T(8,128)S(1)} fusion(bf16[4,256,16,128]{3,2,1,0:T(8,128)(2,1)S(1)} %bitcast.127, f32[16,4,256,32]{2,3,1,0:T(8,128)S(1)} %get-tuple-element.10, f32[32,16]{0,1:T(8,128)S(1)} %get-tuple-element.8, pred[4,32,256]{2,1,0:T(8,128)(4,1)S(1)} %broadcast_and_fusion), kind=kOutput, calls=%fused_computation.27 | convolution fusion | flops 136314880 | bytes 6588416 | tf_op jit(solution)/shard_map/grhj,gjhd->rhd/dot_general | solution.py:57
  19.8 1.0 copy.69
  20.7 7.3 %all-to-all-start = ((f32[32,1,2112]{2,1,0:T(1,128)}), f32[32,1,2112]{2,1,0:T(1,128)S(1)}, u32[]{:S(2)}, u32[]{:S(2)}) async-start(f32[32,1,2112]{2,1,0:T(1,128)} %copy.69), calls=%async_computation | async-start | bytes 557056 | tf_op jit(solution)/shard_map/all_to_all | solution.py:65
  28.3 1.5 reduce-window.6
  30.0 9.1 %all-to-all-done = f32[32,1,2112]{2,1,0:T(1,128)S(1)} async-done(((f32[32,1,2112]{2,1,0:T(1,128)}), f32[32,1,2112]{2,1,0:T(1,128)S(1)}, u32[]{:S(2)}, u32[]{:S(2)}) %all-to-all-start) | async-done | bytes 270368 | tf_op jit(solution)/shard_map/all_to_all | solution.py:65
  39.8 0.9 convolution_bitcast_fusion
  40.8 1.0 copy.70
  41.8 2.8 %all-to-all-start.1 = ((f32[32,1,2048]{2,1,0:T(1,128)}), f32[32,1,2048]{2,1,0:T(1,128)S(1)}, u32[]{:S(2)}, u32[]{:S(2)}) async-start(f32[32,1,2048]{2,1,0:T(1,128)} %copy.70), calls=%async_computation.1 | async-start | bytes 524288 | tf_op jit(solution)/shard_map/all_to_all | solution.py:83
  45.5 9.5 %all-to-all-done.1 = f32[32,1,2048]{2,1,0:T(1,128)S(1)} async-done(((f32[32,1,2048]{2,1,0:T(1,128)}), f32[32,1,2048]{2,1,0:T(1,128)S(1)}, u32[]{:S(2)}, u32[]{:S(2)}) %all-to-all-start.1) | async-done | bytes 262176 | tf_op jit(solution)/shard_map/all_to_all | solution.py:83
  55.3 1.1 convolution_convert_fusion
  56.4 73.3 %all_to_all.27 = bf16[32,24,2048]{2,1,0:T(8,128)(2,1)S(1)} all-to-all(bf16[32,24,2048]{2,1,0:T(8,128)(2,1)S(1)} %bitcast.123), channel_id=1, replica_groups=mesh['dp'=1,'tensor'=32] {'tensor'}, dimensions={0} | all-to-all | bytes 6291456 | tf_op jit(solution)/shard_map/all_to_all | solution.py:141
  129.7 3.4 %fusion.2 = f32[768,1024]{1,0:T(8,128)S(1)} fusion(bf16[768,2048]{1,0:T(8,128)(2,1)S(1)} %bitcast.128, bf16[1,2048,1024]{2,1,0:T(8,128)(2,1)S(1)} %copy-done.12), kind=kOutput, calls=%fused_computation.4 | convolution fusion | flops 3221225472 | bytes 10485760 | tf_op jit(solution)/shard_map/dot_general | solution.py:15
  133.2 3.8 %multiply_convert_fusion = bf16[768,1024]{1,0:T(8,128)(2,1)S(1)} fusion(f32[768,1024]{1,0:T(8,128)S(1)} %fusion.2, bf16[768,2048]{1,0:T(8,128)(2,1)S(1)} %bitcast.129, bf16[1,2048,1024]{2,1,0:T(8,128)(2,1)S(1)} %copy-done.13), kind=kOutput, calls=%fused_computation.14 | convolution fusion | flops 3225944064 | bytes 12058624 | tf_op jit(solution)/shard_map/dot_general | solution.py:14
  136.9 4.8 %fusion.10 = bf16[32,24,2048]{2,1,0:T(8,128)(2,1)} fusion(bf16[32,24,1024]{2,1,0:T(8,128)(2,1)S(1)} %bitcast.145, bf16[1,1024,2048]{2,1,0:T(8,128)(2,1)S(1)} %copy-done.14), kind=kOutput, calls=%fused_computation.12 | convolution fusion | flops 3222798336 | bytes 8912896 | tf_op jit(solution)/shard_map/dot_general | solution.py:17
  141.8 3.7 %all-to-all-start.3 = ((bf16[32,24,2048]{2,1,0:T(8,128)(2,1)}), bf16[32,24,2048]{2,1,0:T(8,128)(2,1)S(1)}, u32[]{:S(2)}, u32[]{:S(2)}) async-start(bf16[32,24,2048]{2,1,0:T(8,128)(2,1)} %fusion.10), calls=%async_computation.3 | async-start | bytes 6291456 | tf_op jit(solution)/shard_map/all_to_all | solution.py:147
  147.5 1.8 maximum_convert_fusion
  149.3 67.6 %all-to-all-done.3 = bf16[32,24,2048]{2,1,0:T(8,128)(2,1)S(1)} async-done(((bf16[32,24,2048]{2,1,0:T(8,128)(2,1)}), bf16[32,24,2048]{2,1,0:T(8,128)(2,1)S(1)}, u32[]{:S(2)}, u32[]{:S(2)}) %all-to-all-start.3) | async-done | bytes 3145760 | tf_op jit(solution)/shard_map/all_to_all | solution.py:147
  218.6 0.8 fusion.31
  219.4 0.8 fusion.30
  (86 shorter events, 9.3 us)
Async XLA Ops:
  0.6 39.2 %copy-start = (bf16[64,2048]{1,0:T(8,128)(2,1)S(1)}, bf16[64,2048]{1,0:T(8,128)(2,1)}, u32[]{:S(2)}) copy-start(bf16[64,2048]{1,0:T(8,128)(2,1)} %param.24) | copy-start | bytes 786436
  2.3 5.6 %copy-start.6 = (bf16[1,32,2048]{2,1,0:T(8,128)(2,1)S(1)}, bf16[1,32,2048]{2,1,0:T(8,128)(2,1)}, u32[]{:S(2)}) copy-start(bf16[1,32,2048]{2,1,0:T(8,128)(2,1)} %param.17) | copy-start | bytes 393220
  8.2 3.8 %copy-start.11 = (s32[1,4]{1,0:T(1,128)S(1)}, s32[1,4]{1,0:T(1,128)}, u32[]{:S(2)}) copy-start(s32[1,4]{1,0:T(1,128)} %param.22) | copy-start | bytes 52
  8.2 3.9 %copy-start.1 = (bf16[128,8,16,128]{3,2,1,0:T(8,128)(2,1)S(1)}, bf16[128,8,16,128]{3,2,1,0:T(8,128)(2,1)}, u32[]{:S(2)}) copy-start(bf16[128,8,16,128]{3,2,1,0:T(8,128)(2,1)} %copy.85) | copy-start | bytes 12582916
  17.7 10.4 %copy-start.7 = (s32[65,8]{0,1:T(8,128)S(1)}, s32[65,8]{0,1:T(8,128)}, u32[]{:S(2)}) copy-start(s32[65,8]{0,1:T(8,128)} %param.27) | copy-start | bytes 6244
  19.7 35.4 %copy-start.9 = (bf16[1,1,2048]{2,1,0:T(2,128)(2,1)S(1)}, bf16[1,1,2048]{2,1,0:T(2,128)(2,1)}, u32[]{:S(2)}) copy-start(bf16[1,1,2048]{2,1,0:T(2,128)(2,1)} %param.23) | copy-start | bytes 12292
  19.8 35.4 %copy-start.2 = (bf16[64,2048]{1,0:T(8,128)(2,1)S(1)}, bf16[64,2048]{1,0:T(8,128)(2,1)}, u32[]{:S(2)}) copy-start(bf16[64,2048]{1,0:T(8,128)(2,1)} %param.25) | copy-start | bytes 786436
  20.7 34.6 %copy-start.8 = (f32[2048]{0:T(1024)S(1)}, f32[2048]{0:T(1024)}, u32[]{:S(2)}) copy-start(f32[2048]{0:T(1024)} %param.26) | copy-start | bytes 24580
  20.7 18.4 %all-to-all-start = ((f32[32,1,2112]{2,1,0:T(1,128)}), f32[32,1,2112]{2,1,0:T(1,128)S(1)}, u32[]{:S(2)}, u32[]{:S(2)}) async-start(f32[32,1,2112]{2,1,0:T(1,128)} %copy.69), calls=%async_computation | async-start | bytes 557056 | tf_op jit(solution)/shard_map/all_to_all | solution.py:65
  41.8 13.2 %all-to-all-start.1 = ((f32[32,1,2048]{2,1,0:T(1,128)}), f32[32,1,2048]{2,1,0:T(1,128)S(1)}, u32[]{:S(2)}, u32[]{:S(2)}) async-start(f32[32,1,2048]{2,1,0:T(1,128)} %copy.70), calls=%async_computation.1 | async-start | bytes 524288 | tf_op jit(solution)/shard_map/all_to_all | solution.py:83
  56.4 73.3 %copy-start.12 = (bf16[1,2048,1024]{2,1,0:T(8,128)(2,1)S(1)}, bf16[1,2048,1024]{2,1,0:T(8,128)(2,1)}, u32[]{:S(2)}) copy-start(bf16[1,2048,1024]{2,1,0:T(8,128)(2,1)} %param.30) | copy-start | bytes 12582916
  129.7 3.4 %copy-start.13 = (bf16[1,2048,1024]{2,1,0:T(8,128)(2,1)S(1)}, bf16[1,2048,1024]{2,1,0:T(8,128)(2,1)}, u32[]{:S(2)}) copy-start(bf16[1,2048,1024]{2,1,0:T(8,128)(2,1)} %param.29) | copy-start | bytes 12582916
  133.1 3.8 %copy-start.14 = (bf16[1,1024,2048]{2,1,0:T(8,128)(2,1)S(1)}, bf16[1,1024,2048]{2,1,0:T(8,128)(2,1)}, u32[]{:S(2)}) copy-start(bf16[1,1024,2048]{2,1,0:T(8,128)(2,1)} %param.31) | copy-start | bytes 12582916
  141.8 3.7 %copy-start.10 = (f32[65,8]{0,1:T(8,128)S(1)}, f32[65,8]{0,1:T(8,128)}, u32[]{:S(2)}) copy-start(f32[65,8]{0,1:T(8,128)} %param.28) | copy-start | bytes 6244
  141.8 75.1 %all-to-all-start.3 = ((bf16[32,24,2048]{2,1,0:T(8,128)(2,1)}), bf16[32,24,2048]{2,1,0:T(8,128)(2,1)S(1)}, u32[]{:S(2)}, u32[]{:S(2)}) async-start(bf16[32,24,2048]{2,1,0:T(8,128)(2,1)} %fusion.10), calls=%async_computation.3 | async-start | bytes 6291456 | tf_op jit(solution)/shard_map/all_to_all | solution.py:147
  216.9 1.1 copy-start.3
  216.9 1.7 copy-start.4
  216.9 1.7 copy-start.5

commit v4 on v3

--- a/solution.py
+++ b/solution.py
@@ -38,24 +38,33 @@
     assert HEAD_DIM % width == 0
     factor = 1.0 / math.sqrt(HEAD_DIM)
     query_heads = decode_queries[0].reshape(requests, HEADS, HEAD_DIM)
-    key_table = cache_keys[0].reshape(groups, reach, HEADS, HEAD_DIM)
-    value_table = cache_values[0].reshape(groups, reach, HEADS, HEAD_DIM)
+    diagonal = jnp.arange(HEADS, dtype=jnp.int32)[:, None] == jnp.arange(HEADS, dtype=jnp.int32)[None, :]
+    query_blocks = jnp.where(
+        diagonal[None, :, :, None], query_heads[:, :, None, :], jnp.zeros((), query_heads.dtype)
+    ).reshape(requests * HEADS, HEADS * HEAD_DIM)
+    key_rows = cache_keys[0].reshape(groups * reach, HEADS * HEAD_DIM)
+    value_rows = cache_values[0].reshape(groups * reach, HEADS * HEAD_DIM)
     scores = (
-        jnp.einsum("rhd,gjhd->grhj", query_heads, key_table, preferred_element_type=jnp.float32)
+        lax.dot_general(
+            query_blocks, key_rows, (((1,), (1,)), ((), ())), preferred_element_type=jnp.float32
+        ).reshape(requests, HEADS, groups, reach)
         * factor
     )
     positions = tensor_rank * reach + jnp.arange(reach, dtype=jnp.int32)
-    member = group_of[0][None, :] == jnp.arange(groups, dtype=jnp.int32)[:, None]
+    member = group_of[0][:, None] == jnp.arange(groups, dtype=jnp.int32)[None, :]
     within = positions[None, :] < cache_lengths[0][:, None]
-    visible = (member[:, :, None] & within[:, None, :])[:, :, None, :]
+    visible = (member[:, :, None] & within[None, :, :])[:, None, :, :]
     own_keys = new_keys[0].astype(jnp.float32).reshape(requests, HEADS, HEAD_DIM)
     own_score = jnp.sum(query_heads.astype(jnp.float32) * own_keys, axis=2) * factor
-    local_peak = jnp.maximum(jnp.max(jnp.where(visible, scores, -jnp.inf), axis=(0, 3)), own_score)
-    expon = jnp.where(visible, jnp.exp(scores - local_peak[None, :, :, None]), 0.0)
-    probs = expon.astype(jnp.bfloat16)
-    local_totals = jnp.sum(expon, axis=(0, 3))
-    mixture = jnp.einsum(
-        "grhj,gjhd->rhd", probs, value_table, preferred_element_type=jnp.float32
+    local_peak = jnp.maximum(jnp.max(jnp.where(visible, scores, -jnp.inf), axis=(2, 3)), own_score)
+    expon = jnp.where(visible, jnp.exp(scores - local_peak[:, :, None, None]), 0.0)
+    probs = expon.astype(jnp.bfloat16).reshape(requests * HEADS, groups * reach)
+    local_totals = jnp.sum(expon, axis=(2, 3))
+    every_head = jnp.dot(probs, value_rows, preferred_element_type=jnp.float32).reshape(
+        requests, HEADS, HEADS, HEAD_DIM
+    )
+    mixture = jnp.sum(
+        jnp.where(diagonal[None, :, :, None], every_head, 0.0), axis=2
     ).reshape(requests, tensor_count, width)
     head_of = (jnp.arange(tensor_count, dtype=jnp.int32) * width) // HEAD_DIM
     peak_to = local_peak.T[head_of]

time: 221 us -> 227 us (1.027)
  matrix products: 20.2 us -> 25.5 us
    unnamed x37 -> x35, local copies, waits for them, and re-layouts: 11.1 us -> 1.84 us
    dot_general x0 -> x2, local copies, waits for them, and re-layouts: none -> 7.17 us  [attention_rows(): jnp.dot(probs, value_rows, preferred_element_type=jnp.float32)]
    dot_general x2, matrix products: 4.89 us -> 10.2 us  [the longest x1 5.38 us: attention_rows(): lax.dot_general(query_blocks, key_rows, (((1,), (1,)), ((), ())), preferr...]
    select_n x0 -> x2, local copies, waits for them, and re-layouts: none -> 2.87 us  [attention_rows(): jnp.where(diagonal[None, :, :, None], query_heads[:, :, None, :], jnp.zer...]
where the time goes in v4:
time: 227 us
  waiting for transfers between devices  86.4 us (38%)
  blocking collectives  73.3 us (32%)
  matrix products  25.5 us (11%)
  local copies, waits for them, and re-layouts  18.9 us (8%)
  starting transfers between devices  13.5 us (6%)
  other arithmetic  7.89 us (3%)
    all_to_all x1, blocking collectives, per_device(): lax.all_to_all(outgoing, 'tensor', split_axis=0, concat_axis=0, tiled=True)  73.3 us
    all_to_all x1, waiting for transfers between devices, per_device(): lax.all_to_all(lax.psum_scatter(expert_mlp(block, w_gate[0], w_up[0], w_d...  67.6 us
    all_to_all x1, waiting for transfers between devices, attention_rows(): lax.all_to_all(partial.reshape(tensor_count, per_device, model_width), 't...  9.65 us
    all_to_all x1, waiting for transfers between devices, attention_rows(): received = lax.all_to_all(payload, 'tensor', 0, 0, tiled=True)  9.1 us
    all_to_all x1, starting transfers between devices, attention_rows(): received = lax.all_to_all(payload, 'tensor', 0, 0, tiled=True)  7.29 us
    dot_general x2, local copies, waits for them, and re-layouts, attention_rows(): jnp.dot(probs, value_rows, preferred_element_type=jnp.float32)  7.17 us
    dot_general x1, matrix products, attention_rows(): lax.dot_general(query_blocks, key_rows, (((1,), (1,)), ((), ())), preferr...  5.38 us
    dot_general x1, matrix products, expert_mlp(): return jnp.dot(active, down_w, preferred_element_type=jnp.float32)  4.83 us
  transfers between devices with their start and end apart: 3, of which 3 were waited for; matrix products, arithmetic and copies ran while one was open for 3% of the time, Pallas kernels for 0%

profile of v4, /device:TPU:0, one launch (start us, length us, event | category | flops | bytes accessed | tf_op | source)
XLA Modules:
  0.0 226.6 jit_solution(16867558483671347945)
XLA Ops:
  0.7 1.0 copy.98
  2.4 2.3 %reshape.319 = bf16[32,16,2048,1]{2,1,0,3:T(8,128)(2,1)} reshape(bf16[32,16,16,128]{3,2,1,0:T(8,128)(2,1)S(1)} %copy.76) | data formatting | bytes 4194304 | tf_op jit(solution)/shard_map/jit(_where)/select_n | solution.py:42
  5.1 5.4 %select_reduce_fusion.1 = (f32[32,16]{1,0:T(8,128)S(1)}, f32[32,16,4,256]{3,1,2,0:T(8,128)S(1)}) fusion(pred[32,4,256]{2,1,0:T(4,128)(4,1)S(1)} %broadcast_and_fusion, bf16[1,4,256,2048]{3,2,1,0:T(8,128)(2,1)} %param.19, bf16[32,16,2048,1]{2,1,0,3:T(8,128)(2,1)} %reshape.319), kind=kOutput, calls=%fused_computation.17 | convolution fusion | flops 2149056000 | bytes 8423424 | tf_op jit(solution)/shard_map/dot_general | solution.py:48
  12.2 0.8 reshape.321
  12.9 6.4 %copy.81 = bf16[2048,1024]{1,0:T(8,128)(2,1)} copy(bf16[2048,1024]{0,1:T(8,128)(2,1)} %bitcast.116) | data formatting | bytes 8388608 | tf_op jit(solution)/shard_map/dot_general | solution.py:63
  19.3 4.8 %select_reduce_fusion = f32[32,16,128]{2,1,0:T(8,128)S(1)} fusion(pred[16,16]{0,1:T(8,128)(4,1)S(1)} %iota_compare_fusion.5, bf16[16,128,1024,1]{2,1,0,3:T(8,128)(2,1)} %bitcast.117, bf16[32,16,1024,1]{2,1,0,3:T(8,128)(2,1)S(1)} %reshape.321), kind=kOutput, calls=%fused_computation.10 | convolution fusion | flops 2149515264 | bytes 5505280 | tf_op jit(solution)/shard_map/dot_general | solution.py:63
  26.1 1.0 copy.84
  27.1 7.3 %all-to-all-start = ((f32[32,1,2112]{2,1,0:T(1,128)}), f32[32,1,2112]{2,1,0:T(1,128)S(1)}, u32[]{:S(2)}, u32[]{:S(2)}) async-start(f32[32,1,2112]{2,1,0:T(1,128)} %copy.84), calls=%async_computation | async-start | bytes 557056 | tf_op jit(solution)/shard_map/all_to_all | solution.py:74
  34.7 1.5 reduce-window.6
  36.4 9.1 %all-to-all-done = f32[32,1,2112]{2,1,0:T(1,128)S(1)} async-done(((f32[32,1,2112]{2,1,0:T(1,128)}), f32[32,1,2112]{2,1,0:T(1,128)S(1)}, u32[]{:S(2)}, u32[]{:S(2)}) %all-to-all-start) | async-done | bytes 270368 | tf_op jit(solution)/shard_map/all_to_all | solution.py:74
  46.2 0.9 convolution_bitcast_fusion
  47.2 1.0 copy.85
  48.1 2.6 %all-to-all-start.1 = ((f32[32,1,2048]{2,1,0:T(1,128)}), f32[32,1,2048]{2,1,0:T(1,128)S(1)}, u32[]{:S(2)}, u32[]{:S(2)}) async-start(f32[32,1,2048]{2,1,0:T(1,128)} %copy.85), calls=%async_computation.1 | async-start | bytes 524288 | tf_op jit(solution)/shard_map/all_to_all | solution.py:92
  51.7 9.6 %all-to-all-done.1 = f32[32,1,2048]{2,1,0:T(1,128)S(1)} async-done(((f32[32,1,2048]{2,1,0:T(1,128)}), f32[32,1,2048]{2,1,0:T(1,128)S(1)}, u32[]{:S(2)}, u32[]{:S(2)}) %all-to-all-start.1) | async-done | bytes 262176 | tf_op jit(solution)/shard_map/all_to_all | solution.py:92
  61.7 1.1 convolution_convert_fusion
  62.8 73.3 %all_to_all.27 = bf16[32,24,2048]{2,1,0:T(8,128)(2,1)S(1)} all-to-all(bf16[32,24,2048]{2,1,0:T(8,128)(2,1)S(1)} %bitcast.115), channel_id=1, replica_groups=mesh['dp'=1,'tensor'=32] {'tensor'}, dimensions={0} | all-to-all | bytes 6291456 | tf_op jit(solution)/shard_map/all_to_all | solution.py:150
  136.1 3.4 %fusion.2 = f32[768,1024]{1,0:T(8,128)S(1)} fusion(bf16[768,2048]{1,0:T(8,128)(2,1)S(1)} %bitcast.118, bf16[1,2048,1024]{2,1,0:T(8,128)(2,1)S(1)} %copy-done.12), kind=kOutput, calls=%fused_computation.4 | convolution fusion | flops 3221225472 | bytes 10485760 | tf_op jit(solution)/shard_map/dot_general | solution.py:15
  139.5 3.8 %multiply_convert_fusion = bf16[768,1024]{1,0:T(8,128)(2,1)S(1)} fusion(f32[768,1024]{1,0:T(8,128)S(1)} %fusion.2, bf16[768,2048]{1,0:T(8,128)(2,1)S(1)} %bitcast.119, bf16[1,2048,1024]{2,1,0:T(8,128)(2,1)S(1)} %copy-done.13), kind=kOutput, calls=%fused_computation.13 | convolution fusion | flops 3225944064 | bytes 12058624 | tf_op jit(solution)/shard_map/dot_general | solution.py:14
  143.3 4.8 %fusion.8 = bf16[32,24,2048]{2,1,0:T(8,128)(2,1)} fusion(bf16[32,24,1024]{2,1,0:T(8,128)(2,1)S(1)} %bitcast.135, bf16[1,1024,2048]{2,1,0:T(8,128)(2,1)S(1)} %copy-done.14), kind=kOutput, calls=%fused_computation.11 | convolution fusion | flops 3222798336 | bytes 8912896 | tf_op jit(solution)/shard_map/dot_general | solution.py:17
  148.1 3.7 %all-to-all-start.3 = ((bf16[32,24,2048]{2,1,0:T(8,128)(2,1)}), bf16[32,24,2048]{2,1,0:T(8,128)(2,1)S(1)}, u32[]{:S(2)}, u32[]{:S(2)}) async-start(bf16[32,24,2048]{2,1,0:T(8,128)(2,1)} %fusion.8), calls=%async_computation.3 | async-start | bytes 6291456 | tf_op jit(solution)/shard_map/all_to_all | solution.py:156
  153.9 1.8 maximum_convert_fusion
  155.7 67.6 %all-to-all-done.3 = bf16[32,24,2048]{2,1,0:T(8,128)(2,1)S(1)} async-done(((bf16[32,24,2048]{2,1,0:T(8,128)(2,1)}), bf16[32,24,2048]{2,1,0:T(8,128)(2,1)S(1)}, u32[]{:S(2)}, u32[]{:S(2)}) %all-to-all-start.3) | async-done | bytes 3145760 | tf_op jit(solution)/shard_map/all_to_all | solution.py:156
  225.0 0.8 fusion.20
  225.8 0.8 fusion.19
  (93 shorter events, 10.8 us)
Async XLA Ops:
  0.6 45.6 %copy-start = (bf16[64,2048]{1,0:T(8,128)(2,1)S(1)}, bf16[64,2048]{1,0:T(8,128)(2,1)}, u32[]{:S(2)}) copy-start(bf16[64,2048]{1,0:T(8,128)(2,1)} %param.24) | copy-start | bytes 786436
  2.4 2.4 %copy-start.10 = (s32[1,32]{1,0:T(1,128)S(1)}, s32[1,32]{1,0:T(1,128)}, u32[]{:S(2)}) copy-start(s32[1,32]{1,0:T(1,128)} %param.21) | copy-start | bytes 388
  2.4 2.4 %copy-start.11 = (s32[1,4]{1,0:T(1,128)S(1)}, s32[1,4]{1,0:T(1,128)}, u32[]{:S(2)}) copy-start(s32[1,4]{1,0:T(1,128)} %param.22) | copy-start | bytes 52
  5.0 5.5 %copy-start.5 = (bf16[1,32,2048]{2,1,0:T(8,128)(2,1)S(1)}, bf16[1,32,2048]{2,1,0:T(8,128)(2,1)}, u32[]{:S(2)}) copy-start(bf16[1,32,2048]{2,1,0:T(8,128)(2,1)} %param.17) | copy-start | bytes 393220
  24.1 10.3 %copy-start.6 = (s32[65,8]{0,1:T(8,128)S(1)}, s32[65,8]{0,1:T(8,128)}, u32[]{:S(2)}) copy-start(s32[65,8]{0,1:T(8,128)} %param.27) | copy-start | bytes 6244
  26.1 35.4 %copy-start.8 = (bf16[1,1,2048]{2,1,0:T(2,128)(2,1)S(1)}, bf16[1,1,2048]{2,1,0:T(2,128)(2,1)}, u32[]{:S(2)}) copy-start(bf16[1,1,2048]{2,1,0:T(2,128)(2,1)} %param.23) | copy-start | bytes 12292
  26.1 35.4 %copy-start.1 = (bf16[64,2048]{1,0:T(8,128)(2,1)S(1)}, bf16[64,2048]{1,0:T(8,128)(2,1)}, u32[]{:S(2)}) copy-start(bf16[64,2048]{1,0:T(8,128)(2,1)} %param.25) | copy-start | bytes 786436
  27.1 34.6 %copy-start.7 = (f32[2048]{0:T(1024)S(1)}, f32[2048]{0:T(1024)}, u32[]{:S(2)}) copy-start(f32[2048]{0:T(1024)} %param.26) | copy-start | bytes 24580
  27.1 18.4 %all-to-all-start = ((f32[32,1,2112]{2,1,0:T(1,128)}), f32[32,1,2112]{2,1,0:T(1,128)S(1)}, u32[]{:S(2)}, u32[]{:S(2)}) async-start(f32[32,1,2112]{2,1,0:T(1,128)} %copy.84), calls=%async_computation | async-start | bytes 557056 | tf_op jit(solution)/shard_map/all_to_all | solution.py:74
  48.1 13.2 %all-to-all-start.1 = ((f32[32,1,2048]{2,1,0:T(1,128)}), f32[32,1,2048]{2,1,0:T(1,128)S(1)}, u32[]{:S(2)}, u32[]{:S(2)}) async-start(f32[32,1,2048]{2,1,0:T(1,128)} %copy.85), calls=%async_computation.1 | async-start | bytes 524288 | tf_op jit(solution)/shard_map/all_to_all | solution.py:92
  62.8 73.3 %copy-start.12 = (bf16[1,2048,1024]{2,1,0:T(8,128)(2,1)S(1)}, bf16[1,2048,1024]{2,1,0:T(8,128)(2,1)}, u32[]{:S(2)}) copy-start(bf16[1,2048,1024]{2,1,0:T(8,128)(2,1)} %param.30) | copy-start | bytes 12582916
  136.1 3.4 %copy-start.13 = (bf16[1,2048,1024]{2,1,0:T(8,128)(2,1)S(1)}, bf16[1,2048,1024]{2,1,0:T(8,128)(2,1)}, u32[]{:S(2)}) copy-start(bf16[1,2048,1024]{2,1,0:T(8,128)(2,1)} %param.29) | copy-start | bytes 12582916
  139.5 3.8 %copy-start.14 = (bf16[1,1024,2048]{2,1,0:T(8,128)(2,1)S(1)}, bf16[1,1024,2048]{2,1,0:T(8,128)(2,1)}, u32[]{:S(2)}) copy-start(bf16[1,1024,2048]{2,1,0:T(8,128)(2,1)} %param.31) | copy-start | bytes 12582916
  148.1 3.7 %copy-start.9 = (f32[65,8]{0,1:T(8,128)S(1)}, f32[65,8]{0,1:T(8,128)}, u32[]{:S(2)}) copy-start(f32[65,8]{0,1:T(8,128)} %param.28) | copy-start | bytes 6244
  148.1 75.1 %all-to-all-start.3 = ((bf16[32,24,2048]{2,1,0:T(8,128)(2,1)}), bf16[32,24,2048]{2,1,0:T(8,128)(2,1)S(1)}, u32[]{:S(2)}, u32[]{:S(2)}) async-start(bf16[32,24,2048]{2,1,0:T(8,128)(2,1)} %fusion.8), calls=%async_computation.3 | async-start | bytes 6291456 | tf_op jit(solution)/shard_map/all_to_all | solution.py:156
  223.3 1.1 copy-start.2
  223.3 1.7 copy-start.3
  223.3 1.7 copy-start.4

commit v5 on v2

--- a/solution.py
+++ b/solution.py
@@ -25,6 +25,7 @@
     requests = decode_queries.shape[1]
     groups = cache_keys.shape[1]
     reach = cache_keys.shape[2]
+    model_width = decode_queries.shape[2]
     assert HEAD_DIM % width == 0
     factor = 1.0 / math.sqrt(HEAD_DIM)
     query_heads = decode_queries[0].reshape(requests, HEADS, HEAD_DIM)
@@ -50,20 +51,21 @@
     head_of = (jnp.arange(tensor_count, dtype=jnp.int32) * width) // HEAD_DIM
     peak_to = local_peak.T[head_of]
     totals_to = local_totals.T[head_of]
-    payload = jnp.concatenate(
-        [jnp.transpose(mixture, (1, 0, 2)), peak_to[:, :, None], totals_to[:, :, None]], axis=2
-    )
+    flat_mix = jnp.transpose(mixture, (1, 0, 2)).reshape(tensor_count, requests * width)
+    payload = jnp.concatenate([flat_mix, peak_to, totals_to], axis=1)
     return payload, own_score
 
 
-def attention_finish(received, own_score, new_values, decode_residual, out_weight):
+def attention_finish(payload, own_score, new_values, decode_residual, out_weight):
     tensor_count = lax.axis_size("tensor")
     tensor_rank = lax.axis_index("tensor")
     requests, model_width = new_values.shape[1], new_values.shape[2]
     width = out_weight.shape[0]
-    part_mix = received[:, :, :width]
-    part_peak = received[:, :, width]
-    part_totals = received[:, :, width + 1]
+    received = lax.all_to_all(payload, "tensor", 0, 0, tiled=True)
+    mixed_width = requests * width
+    part_mix = received[:, :mixed_width].reshape(tensor_count, requests, width)
+    part_peak = received[:, mixed_width:mixed_width + requests]
+    part_totals = received[:, mixed_width + requests:]
     peak = jnp.max(part_peak, axis=0)
     scale = jnp.exp(part_peak - peak[None, :])
     my_head = (tensor_rank * width) // HEAD_DIM
@@ -112,7 +114,7 @@
         jnp.int32
     )
     earlier = jnp.cumsum(one_hot, axis=0) - one_hot
-    return jnp.sum(earlier * one_hot, axis=1)
+    return jnp.sum(earlier * one_hot, axis=1), jnp.sum(one_hot, axis=0)
 
 
 def per_device(
@@ -139,28 +141,42 @@
     row_count, top_count = routes.shape
     decode_count = row_count - prefill_count
     capacity = max(8, (row_count * top_count * 3 // (2 * tensor_count) + 7) // 8 * 8)
-    stride = capacity + decode_count
+    early = max(8, capacity * 2 // 3 // 8 * 8)
+    late = max(capacity - early, decode_count)
+    stride = early + late
     experts = (w_gate[0], w_up[0], w_down[0])
     prefill_routes = routes[:prefill_count].reshape(-1)
-    decode_routes = routes[prefill_count:]
-    prefill_rank = rank_in_expert(prefill_routes, tensor_count)
+    decode_routes = routes[prefill_count:].reshape(-1)
+    prefill_rank, prefill_counts = rank_in_expert(prefill_routes, tensor_count)
+    decode_rank, _ = rank_in_expert(decode_routes, tensor_count)
+    overflow = jnp.maximum(prefill_counts - early, 0)
     prefill_float, prefill_normed = rms_normed(prefill_states, norm_gain)
-    prefill_in = dispatch(
-        prefill_normed, prefill_routes * capacity + prefill_rank, tensor_count * capacity
+    first_in = dispatch(
+        prefill_normed,
+        jnp.where(prefill_rank < early, prefill_routes * early + prefill_rank, -1),
+        tensor_count * early,
     )
     payload, own_score = attention_partials(
         decode_queries, new_keys, cache_keys, cache_values, group_of, cache_lengths,
         out_weight.shape[0],
     )
-    payload, prefill_in = lax.optimization_barrier((payload, prefill_in))
-    received = lax.all_to_all(payload, "tensor", 0, 0, tiled=True)
-    prefill_done = experts_on(prefill_in, experts)
-    decode_hidden = attention_finish(received, own_score, new_values, decode_residual, out_weight)
+    payload, first_in = lax.optimization_barrier((payload, first_in))
+    first_done = experts_on(first_in, experts)
+    decode_hidden = attention_finish(payload, own_score, new_values, decode_residual, out_weight)
     decode_float, decode_normed = rms_normed(decode_hidden, norm_gain)
-    decode_slot = decode_routes * decode_count + jnp.arange(decode_count, dtype=jnp.int32)[:, None]
-    decode_in = dispatch(decode_normed, decode_slot.reshape(-1), tensor_count * decode_count)
-    decode_done = experts_on(decode_in, experts)
-    merged = jnp.concatenate([prefill_done, decode_done], axis=1)
+    late_slot = jnp.concatenate(
+        [
+            jnp.where(
+                prefill_rank >= early, prefill_routes * late + prefill_rank - early, -1
+            ),
+            decode_routes * late + overflow[decode_routes] + decode_rank,
+        ]
+    )
+    second_in = dispatch(
+        jnp.concatenate([prefill_normed, decode_normed], axis=0), late_slot, tensor_count * late
+    )
+    second_done = experts_on(second_in, experts)
+    merged = jnp.concatenate([first_done, second_done], axis=1)
     returned = lax.all_to_all(
         lax.psum_scatter(merged, "dp", scatter_dimension=0, tiled=True),
         "tensor",
@@ -170,13 +186,10 @@
     ).reshape(tensor_count * stride, model_width)
     place = jnp.concatenate(
         [
-            prefill_routes.reshape(prefill_count, top_count) * stride
-            + prefill_rank.reshape(prefill_count, top_count),
-            decode_routes * stride + capacity
-            + jnp.arange(decode_count, dtype=jnp.int32)[:, None],
-        ],
-        axis=0,
-    )
+            prefill_routes * stride + prefill_rank,
+            decode_routes * stride + early + overflow[decode_routes] + decode_rank,
+        ]
+    ).reshape(row_count, top_count)
     columns = jnp.arange(tensor_count * stride, dtype=jnp.int32)
     mixing = jnp.sum(
         jnp.where(place[:, :, None] == columns[None, None, :], route_weights[:, :, None], 0.0),
@@ -186,13 +199,20 @@
     rest = mixing - high.astype(jnp.float32)
     middle = rest.astype(jnp.bfloat16)
     low = (rest - middle.astype(jnp.float32)).astype(jnp.bfloat16)
-    parts = jnp.dot(
-        jnp.concatenate([high, middle, low], axis=0), returned, preferred_element_type=jnp.float32
-    ).reshape(3, row_count, model_width)
-    weighted = (parts[0] + parts[1]) + parts[2]
-    row_float = jnp.concatenate([prefill_float, decode_float], axis=0)
-    mixed_rows = (row_float + weighted).astype(jnp.bfloat16)
-    return (mixed_rows[:prefill_count], mixed_rows[prefill_count:][None])
+
+    def combined(lo, hi, row_float):
+        parts = jnp.dot(
+            jnp.concatenate([high[lo:hi], middle[lo:hi], low[lo:hi]], axis=0),
+            returned,
+            preferred_element_type=jnp.float32,
+        ).reshape(3, hi - lo, model_width)
+        weighted = (parts[0] + parts[1]) + parts[2]
+        return (row_float + weighted).astype(jnp.bfloat16)
+
+    return (
+        combined(0, prefill_count, prefill_float),
+        combined(prefill_count, row_count, decode_float)[None],
+    )
 
 
 def solution(mesh):

time: 260 us -> 223 us (0.86)
  waiting for transfers between devices: 142 us -> 130 us
  matrix products: 45.9 us -> 35 us
  local copies, waits for them, and re-layouts: 31.3 us -> 22.1 us
  other arithmetic: 15.7 us -> 12.9 us
    all_to_all x1, waiting for transfers between devices: 91.4 us -> 69.3 us  [per_device(): lax.all_to_all(lax.psum_scatter(merged, 'dp', scatter_dimension=0, tiled=...]
    all_to_all x1, waiting for transfers between devices: 1.6 us -> 10 us  [attention_finish(): lax.all_to_all(partial.reshape(tensor_count, per_device, model_width), 't...]
    dot_general x1, matrix products: 8.26 us -> 2.54 us  [expert_mlp(): upper = jnp.dot(flat_rows, up_w, preferred_element_type=jnp.float32)]
    dot_general x2, matrix products: 12.6 us -> 9.46 us  [expert_mlp(): gate = jnp.dot(flat_rows, gate_w, preferred_element_type=jnp.float32)]
    broadcast_in_dim x3 -> x0, local copies, waits for them, and re-layouts: 3.15 us -> none  [the longest x1 1.28 us: attention_partials(): totals_to[:, :, None]]
    concatenate x3 -> x2, other arithmetic: 5 us -> 1.9 us  [the longest x1 1.89 us: per_device(): merged = jnp.concatenate([first_done, second_done], axis=1)]
    all_to_all x1, waiting for transfers between devices: 7.11 us -> 10.2 us  [attention_finish(): received = lax.all_to_all(payload, 'tensor', 0, 0, tiled=True)]
    reshape x2, local copies, waits for them, and re-layouts: 3.94 us -> 1.33 us  [the longest x1 1.24 us: attention_partials(): jnp.transpose(mixture, (1, 0, 2)).reshape(tensor_count, requests * width)]
  transfers between devices with their start and end apart: 5 -> 5, of which waited for: 5 -> 5; matrix products, arithmetic and copies ran while one was open for 22% -> 17% of each run, Pallas kernels for 0% -> 0%
where the time goes in v5:
time: 223 us; the launch traced here: 222 us
  waiting for transfers between devices  130 us (58%)
  matrix products  35 us (16%)
  local copies, waits for them, and re-layouts  22.1 us (10%)
  starting transfers between devices  21 us (9%)
  other arithmetic  12.9 us (6%)
    all_to_all x1, waiting for transfers between devices, per_device(): lax.all_to_all(lax.psum_scatter(merged, 'dp', scatter_dimension=0, tiled=...  69.3 us
    all_to_all x2, waiting for transfers between devices, dispatch(): lax.all_to_all(outgoing, 'tensor', split_axis=0, concat_axis=0, tiled=True)  40 us
    unnamed x35, local copies, waits for them, and re-layouts  12.2 us
    all_to_all x2, starting transfers between devices, dispatch(): lax.all_to_all(outgoing, 'tensor', split_axis=0, concat_axis=0, tiled=True)  10.7 us
    all_to_all x1, waiting for transfers between devices, attention_finish(): received = lax.all_to_all(payload, 'tensor', 0, 0, tiled=True)  10.2 us
    all_to_all x1, waiting for transfers between devices, attention_finish(): lax.all_to_all(partial.reshape(tensor_count, per_device, model_width), 't...  10 us
    dot_general x2, matrix products, expert_mlp(): gate = jnp.dot(flat_rows, gate_w, preferred_element_type=jnp.float32)  9.46 us
    dot_general x2, matrix products, expert_mlp(): return jnp.dot(active, down_w, preferred_element_type=jnp.float32)  8.79 us
  transfers between devices with their start and end apart: 5, of which 5 were waited for; matrix products, arithmetic and copies ran while one was open for 17% of the time, Pallas kernels for 0%

profile of v5, /device:TPU:0, one launch (start us, length us, event | category | flops | bytes accessed | tf_op | source)
XLA Modules:
  0.0 222.3 jit_solution(18298131986345227674)
XLA Ops:
  6.0 2.2 convolution_convert_fusion
  8.1 7.3 %all-to-all-start = ((bf16[32,16,2048]{2,1,0:T(8,128)(2,1)}), bf16[32,16,2048]{2,1,0:T(8,128)(2,1)S(1)}, u32[]{:S(2)}, u32[]{:S(2)}) async-start(bf16[32,16,2048]{2,1,0:T(8,128)(2,1)} %bitcast.13), calls=%async_computation | async-start | bytes 4194304 | tf_op jit(solution)/shard_map/all_to_all | solution.py:104
  15.5 5.6 %copy.60 = bf16[128,8,16,128]{3,2,1,0:T(8,128)(2,1)} copy(bf16[128,8,16,128]{3,1,2,0:T(8,128)(2,1)} %bitcast.165) | data formatting | bytes 8388608
  21.4 5.6 %copy.63 = bf16[128,8,16,128]{3,2,1,0:T(8,128)(2,1)} copy(bf16[128,8,16,128]{3,1,2,0:T(8,128)(2,1)} %bitcast.166) | data formatting | bytes 8388608
  27.2 4.8 %fusion.23 = (f32[32,16]{0,1:T(8,128)S(1)}, f32[16,4,256,32]{2,3,1,0:T(8,128)S(1)}) fusion(pred[4,32,256]{2,1,0:T(8,128)(4,1)S(1)} %broadcast_and_fusion, bf16[32,16,128,1]{2,1,0,3:T(8,128)(2,1)S(1)} %bitcast.180, bf16[4,256,16,128]{3,2,1,0:T(8,128)(2,1)} %bitcast.167), kind=kOutput, calls=%fused_computation.28 | convolution fusion | flops 135790080 | bytes 6457344 | tf_op jit(solution)/shard_map/rhd,gjhd->grhj/dot_general | solution.py:35
  32.0 2.4 %fusion.39 = f32[32,16,128]{2,0,1:T(8,128)S(1)} fusion(bf16[4,256,16,128]{3,2,1,0:T(8,128)(2,1)S(1)} %bitcast.168, f32[16,4,256,32]{2,3,1,0:T(8,128)S(1)} %get-tuple-element.22, f32[32,16]{0,1:T(8,128)S(1)} %get-tuple-element.16, pred[4,32,256]{2,1,0:T(8,128)(4,1)S(1)} %broadcast_and_fusion), kind=kOutput, calls=%fused_computation.39 | convolution fusion | flops 136314880 | bytes 6588416 | tf_op jit(solution)/shard_map/grhj,gjhd->rhd/dot_general | solution.py:48
  37.2 2.2 fusion.28
  40.9 23.4 %all-to-all-done = bf16[32,16,2048]{2,1,0:T(8,128)(2,1)S(1)} async-done(((bf16[32,16,2048]{2,1,0:T(8,128)(2,1)}), bf16[32,16,2048]{2,1,0:T(8,128)(2,1)S(1)}, u32[]{:S(2)}, u32[]{:S(2)}) %all-to-all-start) | async-done | bytes 2097184 | tf_op jit(solution)/shard_map/all_to_all | solution.py:104
  65.3 4.0 %all-to-all-start.1 = ((f32[32,1,2112]{2,1,0:T(1,128)}), f32[32,1,2112]{2,1,0:T(1,128)S(1)}, u32[]{:S(2)}, u32[]{:S(2)}) async-start(f32[32,1,2112]{2,1,0:T(1,128)} %copy.51), calls=%async_computation.1 | async-start | bytes 557056 | tf_op jit(solution)/shard_map/all_to_all | solution.py:64
  70.2 10.2 %all-to-all-done.1 = f32[32,1,2112]{2,1,0:T(1,128)S(1)} async-done(((f32[32,1,2112]{2,1,0:T(1,128)}), f32[32,1,2112]{2,1,0:T(1,128)S(1)}, u32[]{:S(2)}, u32[]{:S(2)}) %all-to-all-start.1) | async-done | bytes 270368 | tf_op jit(solution)/shard_map/all_to_all | solution.py:64
  84.7 2.8 %all-to-all-start.2 = ((f32[32,1,2048]{2,1,0:T(1,128)}), f32[32,1,2048]{2,1,0:T(1,128)S(1)}, u32[]{:S(2)}, u32[]{:S(2)}) async-start(f32[32,1,2048]{2,1,0:T(1,128)} %copy.52), calls=%async_computation.2 | async-start | bytes 524288 | tf_op jit(solution)/shard_map/all_to_all | solution.py:82
  87.9 10.0 %all-to-all-done.2 = f32[32,1,2048]{2,1,0:T(1,128)S(1)} async-done(((f32[32,1,2048]{2,1,0:T(1,128)}), f32[32,1,2048]{2,1,0:T(1,128)S(1)}, u32[]{:S(2)}, u32[]{:S(2)}) %all-to-all-start.2) | async-done | bytes 262176 | tf_op jit(solution)/shard_map/all_to_all | solution.py:82
  99.4 1.5 fusion.22
  100.9 3.4 %all-to-all-start.3 = ((bf16[32,8,2048]{2,1,0:T(8,128)(2,1)}), bf16[32,8,2048]{2,1,0:T(8,128)(2,1)}, u32[]{:S(2)}, u32[]{:S(2)}) async-start(bf16[32,8,2048]{2,1,0:T(8,128)(2,1)} %fusion.22), calls=%async_computation.3 | async-start | bytes 2097152 | tf_op jit(solution)/shard_map/all_to_all | solution.py:104
  104.3 4.7 %fusion.10 = f32[512,1024]{1,0:T(8,128)S(1)} fusion(bf16[512,2048]{1,0:T(8,128)(2,1)S(1)} %bitcast.171, bf16[1,2048,1024]{2,1,0:T(8,128)(2,1)} %param.29), kind=kOutput, calls=%fused_computation.13 | convolution fusion | flops 2147483648 | bytes 8388608 | tf_op jit(solution)/shard_map/dot_general | solution.py:14
  109.0 2.5 %multiply_convert_fusion = bf16[512,1024]{1,0:T(8,128)(2,1)S(1)} fusion(f32[512,1024]{1,0:T(8,128)S(1)} %fusion.10, bf16[512,2048]{1,0:T(8,128)(2,1)S(1)} %bitcast.172, bf16[1,2048,1024]{2,1,0:T(8,128)(2,1)S(1)} %copy-done.12), kind=kOutput, calls=%fused_computation.31 | convolution fusion | flops 2150629376 | bytes 9437184 | tf_op jit(solution)/shard_map/dot_general | solution.py:15
  111.5 2.4 %fusion.16 = bf16[32,16,2048]{2,1,0:T(8,128)(2,1)S(1)} fusion(bf16[32,16,1024]{2,1,0:T(8,128)(2,1)S(1)} %bitcast.187, bf16[1,1024,2048]{2,1,0:T(8,128)(2,1)S(1)} %copy-done.11), kind=kOutput, calls=%fused_computation.20 | convolution fusion | flops 2148532224 | bytes 7340032 | tf_op jit(solution)/shard_map/dot_general | solution.py:17
  113.9 16.6 %all-to-all-done.3 = bf16[32,8,2048]{2,1,0:T(8,128)(2,1)} async-done(((bf16[32,8,2048]{2,1,0:T(8,128)(2,1)}), bf16[32,8,2048]{2,1,0:T(8,128)(2,1)}, u32[]{:S(2)}, u32[]{:S(2)}) %all-to-all-start.3) | async-done | bytes 1048608 | tf_op jit(solution)/shard_map/all_to_all | solution.py:104
  130.5 4.8 %fusion.8 = f32[256,1024]{1,0:T(8,128)} fusion(bf16[1,2048,1024]{2,1,0:T(8,128)(2,1)} %param.29, bf16[32,8,2048]{2,1,0:T(8,128)(2,1)} %all-to-all-done.3), kind=kOutput, calls=%fused_computation.11 | convolution fusion | flops 1073741824 | bytes 6291456 | tf_op jit(solution)/shard_map/dot_general | solution.py:14
  135.3 6.4 %fusion.19 = bf16[32,8,2048]{2,1,0:T(8,128)(2,1)S(1)} fusion(bf16[1,1024,2048]{2,1,0:T(8,128)(2,1)} %param.31, bf16[1,2048,1024]{2,1,0:T(8,128)(2,1)} %param.30, bf16[32,8,2048]{2,1,0:T(8,128)(2,1)} %all-to-all-done.3, f32[256,1024]{1,0:T(8,128)} %fusion.8), kind=kOutput, calls=%fused_computation.22 | convolution fusion | flops 2149580800 | bytes 11534336 | tf_op jit(solution)/shard_map/dot_general | solution.py:17
  141.7 1.9 pad_maximum_fusion
  143.6 3.5 %all-to-all-start.4 = ((bf16[32,24,2048]{2,1,0:T(8,128)(2,1)}), bf16[32,24,2048]{2,1,0:T(8,128)(2,1)S(1)}, u32[]{:S(2)}, u32[]{:S(2)}) async-start(bf16[32,24,2048]{2,1,0:T(8,128)(2,1)} %pad_maximum_fusion), calls=%async_computation.4 | async-start | bytes 6291456 | tf_op jit(solution)/shard_map/all_to_all | solution.py:180
  149.3 69.3 %all-to-all-done.4 = bf16[32,24,2048]{2,1,0:T(8,128)(2,1)S(1)} async-done(((bf16[32,24,2048]{2,1,0:T(8,128)(2,1)}), bf16[32,24,2048]{2,1,0:T(8,128)(2,1)S(1)}, u32[]{:S(2)}, u32[]{:S(2)}) %all-to-all-start.4) | async-done | bytes 3145760 | tf_op jit(solution)/shard_map/all_to_all | solution.py:180
  218.6 1.8 fusion.60
  (106 shorter events, 21.2 us)
Async XLA Ops:
  0.6 82.1 %copy-start = (bf16[64,2048]{1,0:T(8,128)(2,1)S(1)}, bf16[64,2048]{1,0:T(8,128)(2,1)}, u32[]{:S(2)}) copy-start(bf16[64,2048]{1,0:T(8,128)(2,1)} %param.24) | copy-start | bytes 786436
  8.1 7.3 %copy-start.5 = (bf16[1,32,2048]{2,1,0:T(8,128)(2,1)S(1)}, bf16[1,32,2048]{2,1,0:T(8,128)(2,1)}, u32[]{:S(2)}) copy-start(bf16[1,32,2048]{2,1,0:T(8,128)(2,1)} %param.16) | copy-start | bytes 393220
  8.1 56.2 %all-to-all-start = ((bf16[32,16,2048]{2,1,0:T(8,128)(2,1)}), bf16[32,16,2048]{2,1,0:T(8,128)(2,1)S(1)}, u32[]{:S(2)}, u32[]{:S(2)}) async-start(bf16[32,16,2048]{2,1,0:T(8,128)(2,1)} %bitcast.13), calls=%async_computation | async-start | bytes 4194304 | tf_op jit(solution)/shard_map/all_to_all | solution.py:104
  15.5 5.6 %copy-start.4 = (bf16[1,32,2048]{2,1,0:T(8,128)(2,1)S(1)}, bf16[1,32,2048]{2,1,0:T(8,128)(2,1)}, u32[]{:S(2)}) copy-start(bf16[1,32,2048]{2,1,0:T(8,128)(2,1)} %param.17) | copy-start | bytes 393220
  21.4 5.6 %copy-start.13 = (s32[1,32]{1,0:T(1,128)S(1)}, s32[1,32]{1,0:T(1,128)}, u32[]{:S(2)}) copy-start(s32[1,32]{1,0:T(1,128)} %param.21) | copy-start | bytes 388
  21.4 5.6 %copy-start.10 = (s32[1,4]{1,0:T(1,128)S(1)}, s32[1,4]{1,0:T(1,128)}, u32[]{:S(2)}) copy-start(s32[1,4]{1,0:T(1,128)} %param.22) | copy-start | bytes 52
  27.1 4.9 %copy-start.1 = (bf16[128,8,16,128]{3,2,1,0:T(8,128)(2,1)S(1)}, bf16[128,8,16,128]{3,2,1,0:T(8,128)(2,1)}, u32[]{:S(2)}) copy-start(bf16[128,8,16,128]{3,2,1,0:T(8,128)(2,1)} %copy.63) | copy-start | bytes 12582916
  32.0 2.5 %copy-start.3 = (f32[16,4,256,32]{2,3,1,0:T(8,128)}, f32[16,4,256,32]{2,3,1,0:T(8,128)S(1)}, u32[]{:S(2)}) copy-start(f32[16,4,256,32]{2,3,1,0:T(8,128)S(1)} %get-tuple-element.22) | copy-start | bytes 6291460
  35.9 4.7 %copy-start.8 = (s32[65,8]{0,1:T(8,128)S(1)}, s32[65,8]{0,1:T(8,128)}, u32[]{:S(2)}) copy-start(s32[65,8]{0,1:T(8,128)} %param.27) | copy-start | bytes 6244
  65.3 15.1 %all-to-all-start.1 = ((f32[32,1,2112]{2,1,0:T(1,128)}), f32[32,1,2112]{2,1,0:T(1,128)S(1)}, u32[]{:S(2)}, u32[]{:S(2)}) async-start(f32[32,1,2112]{2,1,0:T(1,128)} %copy.51), calls=%async_computation.1 | async-start | bytes 557056 | tf_op jit(solution)/shard_map/all_to_all | solution.py:64
  70.0 17.4 %copy-start.7 = (bf16[1,1,2048]{2,1,0:T(2,128)(2,1)S(1)}, bf16[1,1,2048]{2,1,0:T(2,128)(2,1)}, u32[]{:S(2)}) copy-start(bf16[1,1,2048]{2,1,0:T(2,128)(2,1)} %param.23) | copy-start | bytes 12292
  80.4 18.9 %copy-start.6 = (f32[2048]{0:T(1024)S(1)}, f32[2048]{0:T(1024)}, u32[]{:S(2)}) copy-start(f32[2048]{0:T(1024)} %param.26) | copy-start | bytes 24580
  84.7 13.2 %all-to-all-start.2 = ((f32[32,1,2048]{2,1,0:T(1,128)}), f32[32,1,2048]{2,1,0:T(1,128)S(1)}, u32[]{:S(2)}, u32[]{:S(2)}) async-start(f32[32,1,2048]{2,1,0:T(1,128)} %copy.52), calls=%async_computation.2 | async-start | bytes 524288 | tf_op jit(solution)/shard_map/all_to_all | solution.py:82
  100.9 29.6 %all-to-all-start.3 = ((bf16[32,8,2048]{2,1,0:T(8,128)(2,1)}), bf16[32,8,2048]{2,1,0:T(8,128)(2,1)}, u32[]{:S(2)}, u32[]{:S(2)}) async-start(bf16[32,8,2048]{2,1,0:T(8,128)(2,1)} %fusion.22), calls=%async_computation.3 | async-start | bytes 2097152 | tf_op jit(solution)/shard_map/all_to_all | solution.py:104
  104.3 4.7 %copy-start.12 = (bf16[1,2048,1024]{2,1,0:T(8,128)(2,1)S(1)}, bf16[1,2048,1024]{2,1,0:T(8,128)(2,1)}, u32[]{:S(2)}) copy-start(bf16[1,2048,1024]{2,1,0:T(8,128)(2,1)} %param.30) | copy-start | bytes 12582916
  109.0 2.6 %copy-start.11 = (bf16[1,1024,2048]{2,1,0:T(8,128)(2,1)S(1)}, bf16[1,1024,2048]{2,1,0:T(8,128)(2,1)}, u32[]{:S(2)}) copy-start(bf16[1,1024,2048]{2,1,0:T(8,128)(2,1)} %param.31) | copy-start | bytes 12582916
  143.6 3.6 %copy-start.9 = (f32[65,8]{0,1:T(8,128)S(1)}, f32[65,8]{0,1:T(8,128)}, u32[]{:S(2)}) copy-start(f32[65,8]{0,1:T(8,128)} %param.28) | copy-start | bytes 6244
  143.6 75.0 %all-to-all-start.4 = ((bf16[32,24,2048]{2,1,0:T(8,128)(2,1)}), bf16[32,24,2048]{2,1,0:T(8,128)(2,1)S(1)}, u32[]{:S(2)}, u32[]{:S(2)}) async-start(bf16[32,24,2048]{2,1,0:T(8,128)(2,1)} %pad_maximum_fusion), calls=%async_computation.4 | async-start | bytes 6291456 | tf_op jit(solution)/shard_map/all_to_all | solution.py:180
  218.6 1.8 copy-start.2

commit v6 on v5

--- a/solution.py
+++ b/solution.py
@@ -117,6 +117,16 @@
     return jnp.sum(earlier * one_hot, axis=1), jnp.sum(one_hot, axis=0)
 
 
+def give_back(done):
+    return lax.all_to_all(
+        lax.psum_scatter(done, "dp", scatter_dimension=0, tiled=True),
+        "tensor",
+        split_axis=0,
+        concat_axis=0,
+        tiled=True,
+    )
+
+
 def per_device(
     decode_queries,
     new_keys,
@@ -175,15 +185,14 @@
     second_in = dispatch(
         jnp.concatenate([prefill_normed, decode_normed], axis=0), late_slot, tensor_count * late
     )
+    first_done, second_in = lax.optimization_barrier((first_done, second_in))
+    first_back = give_back(first_done)
     second_done = experts_on(second_in, experts)
-    merged = jnp.concatenate([first_done, second_done], axis=1)
-    returned = lax.all_to_all(
-        lax.psum_scatter(merged, "dp", scatter_dimension=0, tiled=True),
-        "tensor",
-        split_axis=0,
-        concat_axis=0,
-        tiled=True,
-    ).reshape(tensor_count * stride, model_width)
+    first_back, second_done = lax.optimization_barrier((first_back, second_done))
+    second_back = give_back(second_done)
+    returned = jnp.concatenate([first_back, second_back], axis=1).reshape(
+        tensor_count * stride, model_width
+    )
     place = jnp.concatenate(
         [
             prefill_routes * stride + prefill_rank,

time: 223 us -> 218 us (0.978)
  waiting for transfers between devices: 130 us -> 121 us
  starting transfers between devices: 21 us -> 25 us
    all_to_all x1 -> x2, waiting for transfers between devices: 69.3 us -> 62.1 us  [give_back(): lax.all_to_all(lax.psum_scatter(done, 'dp', scatter_dimension=0, tiled=Tr...]
    all_to_all x1 -> x2, starting transfers between devices: 3.54 us -> 7.55 us  [give_back(): lax.all_to_all(lax.psum_scatter(done, 'dp', scatter_dimension=0, tiled=Tr...]
    unnamed x35 -> x39, local copies, waits for them, and re-layouts: 12.2 us -> 13.1 us
  transfers between devices with their start and end apart: 5 -> 6, of which waited for: 5 -> 6; matrix products, arithmetic and copies ran while one was open for 17% -> 23% of each run, Pallas kernels for 0% -> 0%
where the time goes in v6:
time: 218 us; the launch traced here: 217 us
  waiting for transfers between devices  121 us (56%)
  matrix products  34.9 us (16%)
  starting transfers between devices  25 us (11%)
  local copies, waits for them, and re-layouts  23 us (11%)
  other arithmetic  11.2 us (5%)
    all_to_all x2, waiting for transfers between devices, give_back(): lax.all_to_all(lax.psum_scatter(done, 'dp', scatter_dimension=0, tiled=Tr...  62.1 us
    all_to_all x2, waiting for transfers between devices, dispatch(): lax.all_to_all(outgoing, 'tensor', split_axis=0, concat_axis=0, tiled=True)  38.6 us
    unnamed x39, local copies, waits for them, and re-layouts  13.1 us
    dot_general x2, matrix products, expert_mlp(): return jnp.dot(active, down_w, preferred_element_type=jnp.float32)  10.8 us
    all_to_all x2, starting transfers between devices, dispatch(): lax.all_to_all(outgoing, 'tensor', split_axis=0, concat_axis=0, tiled=True)  10.7 us
    all_to_all x1, waiting for transfers between devices, attention_finish(): received = lax.all_to_all(payload, 'tensor', 0, 0, tiled=True)  10.2 us
    all_to_all x1, waiting for transfers between devices, attention_finish(): lax.all_to_all(partial.reshape(tensor_count, per_device, model_width), 't...  10 us
    dot_general x2, matrix products, expert_mlp(): gate = jnp.dot(flat_rows, gate_w, preferred_element_type=jnp.float32)  8.42 us
  transfers between devices with their start and end apart: 6, of which 6 were waited for; matrix products, arithmetic and copies ran while one was open for 23% of the time, Pallas kernels for 0%

profile of v6, /device:TPU:0, one launch (start us, length us, event | category | flops | bytes accessed | tf_op | source)
XLA Modules:
  0.0 217.0 jit_solution(2655554201811927756)
XLA Ops:
  6.0 2.2 convolution_convert_fusion
  8.1 7.3 %all-to-all-start = ((bf16[32,16,2048]{2,1,0:T(8,128)(2,1)}), bf16[32,16,2048]{2,1,0:T(8,128)(2,1)S(1)}, u32[]{:S(2)}, u32[]{:S(2)}) async-start(bf16[32,16,2048]{2,1,0:T(8,128)(2,1)} %bitcast.13), calls=%async_computation | async-start | bytes 4194304 | tf_op jit(solution)/shard_map/all_to_all | solution.py:104
  15.5 5.6 %copy.60 = bf16[128,8,16,128]{3,2,1,0:T(8,128)(2,1)} copy(bf16[128,8,16,128]{3,1,2,0:T(8,128)(2,1)} %bitcast.165) | data formatting | bytes 8388608
  21.4 5.6 %copy.63 = bf16[128,8,16,128]{3,2,1,0:T(8,128)(2,1)} copy(bf16[128,8,16,128]{3,1,2,0:T(8,128)(2,1)} %bitcast.166) | data formatting | bytes 8388608
  27.2 4.8 %fusion.23 = (f32[32,16]{0,1:T(8,128)S(1)}, f32[16,4,256,32]{2,3,1,0:T(8,128)S(1)}) fusion(pred[4,32,256]{2,1,0:T(8,128)(4,1)S(1)} %broadcast_and_fusion, bf16[32,16,128,1]{2,1,0,3:T(8,128)(2,1)S(1)} %bitcast.180, bf16[4,256,16,128]{3,2,1,0:T(8,128)(2,1)} %bitcast.167), kind=kOutput, calls=%fused_computation.28 | convolution fusion | flops 135790080 | bytes 6457344 | tf_op jit(solution)/shard_map/rhd,gjhd->grhj/dot_general | solution.py:35
  32.0 2.4 %fusion.39 = f32[32,16,128]{2,0,1:T(8,128)S(1)} fusion(bf16[4,256,16,128]{3,2,1,0:T(8,128)(2,1)S(1)} %bitcast.168, f32[16,4,256,32]{2,3,1,0:T(8,128)S(1)} %get-tuple-element.30, f32[32,16]{0,1:T(8,128)S(1)} %get-tuple-element.24, pred[4,32,256]{2,1,0:T(8,128)(4,1)S(1)} %broadcast_and_fusion), kind=kOutput, calls=%fused_computation.39 | convolution fusion | flops 136314880 | bytes 6588416 | tf_op jit(solution)/shard_map/grhj,gjhd->rhd/dot_general | solution.py:48
  37.2 2.2 %fusion.28 = f32[32,16]{0,1:T(8,128)S(1)} fusion(f32[16,4,256,32]{2,3,1,0:T(8,128)} %copy-done.3, f32[32,16]{0,1:T(8,128)S(1)} %get-tuple-element.24, pred[4,32,256]{2,1,0:T(8,128)(4,1)S(1)} %broadcast_and_fusion), kind=kLoop, calls=%fused_computation.32 | loop fusion | flops 2096640 | bytes 2134016 | tf_op jit(solution)/shard_map/reduce_sum | solution.py:47
  40.9 23.4 %all-to-all-done = bf16[32,16,2048]{2,1,0:T(8,128)(2,1)S(1)} async-done(((bf16[32,16,2048]{2,1,0:T(8,128)(2,1)}), bf16[32,16,2048]{2,1,0:T(8,128)(2,1)S(1)}, u32[]{:S(2)}, u32[]{:S(2)}) %all-to-all-start) | async-done | bytes 2097184 | tf_op jit(solution)/shard_map/all_to_all | solution.py:104
  65.3 4.0 %all-to-all-start.1 = ((f32[32,1,2112]{2,1,0:T(1,128)}), f32[32,1,2112]{2,1,0:T(1,128)S(1)}, u32[]{:S(2)}, u32[]{:S(2)}) async-start(f32[32,1,2112]{2,1,0:T(1,128)} %copy.51), calls=%async_computation.1 | async-start | bytes 557056 | tf_op jit(solution)/shard_map/all_to_all | solution.py:64
  70.2 10.2 %all-to-all-done.1 = f32[32,1,2112]{2,1,0:T(1,128)S(1)} async-done(((f32[32,1,2112]{2,1,0:T(1,128)}), f32[32,1,2112]{2,1,0:T(1,128)S(1)}, u32[]{:S(2)}, u32[]{:S(2)}) %all-to-all-start.1) | async-done | bytes 270368 | tf_op jit(solution)/shard_map/all_to_all | solution.py:64
  84.7 2.8 %all-to-all-start.2 = ((f32[32,1,2048]{2,1,0:T(1,128)}), f32[32,1,2048]{2,1,0:T(1,128)S(1)}, u32[]{:S(2)}, u32[]{:S(2)}) async-start(f32[32,1,2048]{2,1,0:T(1,128)} %copy.52), calls=%async_computation.2 | async-start | bytes 524288 | tf_op jit(solution)/shard_map/all_to_all | solution.py:82
  87.9 10.0 %all-to-all-done.2 = f32[32,1,2048]{2,1,0:T(1,128)S(1)} async-done(((f32[32,1,2048]{2,1,0:T(1,128)}), f32[32,1,2048]{2,1,0:T(1,128)S(1)}, u32[]{:S(2)}, u32[]{:S(2)}) %all-to-all-start.2) | async-done | bytes 262176 | tf_op jit(solution)/shard_map/all_to_all | solution.py:82
  99.4 1.5 fusion.22
  100.8 3.4 %all-to-all-start.3 = ((bf16[32,8,2048]{2,1,0:T(8,128)(2,1)}), bf16[32,8,2048]{2,1,0:T(8,128)(2,1)}, u32[]{:S(2)}, u32[]{:S(2)}) async-start(bf16[32,8,2048]{2,1,0:T(8,128)(2,1)} %fusion.22), calls=%async_computation.3 | async-start | bytes 2097152 | tf_op jit(solution)/shard_map/all_to_all | solution.py:104
  104.2 4.7 %fusion.10 = f32[512,1024]{1,0:T(8,128)S(1)} fusion(bf16[512,2048]{1,0:T(8,128)(2,1)S(1)} %bitcast.171, bf16[1,2048,1024]{2,1,0:T(8,128)(2,1)} %param.29), kind=kOutput, calls=%fused_computation.13 | convolution fusion | flops 2147483648 | bytes 8388608 | tf_op jit(solution)/shard_map/dot_general | solution.py:14
  108.9 2.5 %multiply_convert_fusion = bf16[512,1024]{1,0:T(8,128)(2,1)S(1)} fusion(f32[512,1024]{1,0:T(8,128)S(1)} %fusion.10, bf16[512,2048]{1,0:T(8,128)(2,1)S(1)} %bitcast.172, bf16[1,2048,1024]{2,1,0:T(8,128)(2,1)S(1)} %copy-done.14), kind=kOutput, calls=%fused_computation.31 | convolution fusion | flops 2150629376 | bytes 9437184 | tf_op jit(solution)/shard_map/dot_general | solution.py:15
  111.5 3.7 %fusion.16 = bf16[32,16,2048]{2,1,0:T(8,128)(2,1)} fusion(bf16[32,16,1024]{2,1,0:T(8,128)(2,1)S(1)} %bitcast.187, bf16[1,1024,2048]{2,1,0:T(8,128)(2,1)S(1)} %copy-done.13), kind=kOutput, calls=%fused_computation.20 | convolution fusion | flops 2148532224 | bytes 7340032 | tf_op jit(solution)/shard_map/dot_general | solution.py:17
  115.2 15.2 %all-to-all-done.3 = bf16[32,8,2048]{2,1,0:T(8,128)(2,1)} async-done(((bf16[32,8,2048]{2,1,0:T(8,128)(2,1)}), bf16[32,8,2048]{2,1,0:T(8,128)(2,1)}, u32[]{:S(2)}, u32[]{:S(2)}) %all-to-all-start.3) | async-done | bytes 1048608 | tf_op jit(solution)/shard_map/all_to_all | solution.py:104
  130.4 3.5 %all-to-all-start.4 = ((bf16[32,16,2048]{2,1,0:T(8,128)(2,1)}), bf16[32,16,2048]{2,1,0:T(8,128)(2,1)S(1)}, u32[]{:S(2)}, u32[]{:S(2)}) async-start(bf16[32,16,2048]{2,1,0:T(8,128)(2,1)} %fusion.16), calls=%async_computation.4 | async-start | bytes 4194304 | tf_op jit(solution)/shard_map/all_to_all | solution.py:121
  134.0 3.8 %fusion.8 = f32[256,1024]{1,0:T(8,128)S(1)} fusion(bf16[1,2048,1024]{2,1,0:T(8,128)(2,1)} %param.29, bf16[32,8,2048]{2,1,0:T(8,128)(2,1)} %all-to-all-done.3), kind=kOutput, calls=%fused_computation.11 | convolution fusion | flops 1073741824 | bytes 6291456 | tf_op jit(solution)/shard_map/dot_general | solution.py:14
  137.7 7.1 %fusion.19 = bf16[32,8,2048]{2,1,0:T(8,128)(2,1)} fusion(bf16[1,1024,2048]{2,1,0:T(8,128)(2,1)} %param.31, bf16[1,2048,1024]{2,1,0:T(8,128)(2,1)} %param.30, bf16[32,8,2048]{2,1,0:T(8,128)(2,1)} %all-to-all-done.3, f32[256,1024]{1,0:T(8,128)S(1)} %fusion.8), kind=kOutput, calls=%fused_computation.22 | convolution fusion | flops 2149580800 | bytes 11534336 | tf_op jit(solution)/shard_map/dot_general | solution.py:17
  144.9 38.0 %all-to-all-done.4 = bf16[32,16,2048]{2,1,0:T(8,128)(2,1)S(1)} async-done(((bf16[32,16,2048]{2,1,0:T(8,128)(2,1)}), bf16[32,16,2048]{2,1,0:T(8,128)(2,1)S(1)}, u32[]{:S(2)}, u32[]{:S(2)}) %all-to-all-start.4) | async-done | bytes 2097184 | tf_op jit(solution)/shard_map/all_to_all | solution.py:121
  182.9 4.0 %all-to-all-start.5 = ((bf16[32,8,2048]{2,1,0:T(8,128)(2,1)}), bf16[32,8,2048]{2,1,0:T(8,128)(2,1)S(1)}, u32[]{:S(2)}, u32[]{:S(2)}) async-start(bf16[32,8,2048]{2,1,0:T(8,128)(2,1)} %fusion.19), calls=%async_computation.5 | async-start | bytes 2097152 | tf_op jit(solution)/shard_map/all_to_all | solution.py:121
  189.0 24.1 %all-to-all-done.5 = bf16[32,8,2048]{2,1,0:T(8,128)(2,1)S(1)} async-done(((bf16[32,8,2048]{2,1,0:T(8,128)(2,1)}), bf16[32,8,2048]{2,1,0:T(8,128)(2,1)S(1)}, u32[]{:S(2)}, u32[]{:S(2)}) %all-to-all-start.5) | async-done | bytes 1048608 | tf_op jit(solution)/shard_map/all_to_all | solution.py:121
  (112 shorter events, 23.1 us)
Async XLA Ops:
  0.6 82.1 %copy-start = (bf16[64,2048]{1,0:T(8,128)(2,1)S(1)}, bf16[64,2048]{1,0:T(8,128)(2,1)}, u32[]{:S(2)}) copy-start(bf16[64,2048]{1,0:T(8,128)(2,1)} %param.24) | copy-start | bytes 786436
  8.1 7.3 %copy-start.7 = (bf16[1,32,2048]{2,1,0:T(8,128)(2,1)S(1)}, bf16[1,32,2048]{2,1,0:T(8,128)(2,1)}, u32[]{:S(2)}) copy-start(bf16[1,32,2048]{2,1,0:T(8,128)(2,1)} %param.16) | copy-start | bytes 393220
  8.1 56.2 %all-to-all-start = ((bf16[32,16,2048]{2,1,0:T(8,128)(2,1)}), bf16[32,16,2048]{2,1,0:T(8,128)(2,1)S(1)}, u32[]{:S(2)}, u32[]{:S(2)}) async-start(bf16[32,16,2048]{2,1,0:T(8,128)(2,1)} %bitcast.13), calls=%async_computation | async-start | bytes 4194304 | tf_op jit(solution)/shard_map/all_to_all | solution.py:104
  15.5 5.6 %copy-start.6 = (bf16[1,32,2048]{2,1,0:T(8,128)(2,1)S(1)}, bf16[1,32,2048]{2,1,0:T(8,128)(2,1)}, u32[]{:S(2)}) copy-start(bf16[1,32,2048]{2,1,0:T(8,128)(2,1)} %param.17) | copy-start | bytes 393220
  21.4 5.6 %copy-start.15 = (s32[1,32]{1,0:T(1,128)S(1)}, s32[1,32]{1,0:T(1,128)}, u32[]{:S(2)}) copy-start(s32[1,32]{1,0:T(1,128)} %param.21) | copy-start | bytes 388
  21.4 5.6 %copy-start.12 = (s32[1,4]{1,0:T(1,128)S(1)}, s32[1,4]{1,0:T(1,128)}, u32[]{:S(2)}) copy-start(s32[1,4]{1,0:T(1,128)} %param.22) | copy-start | bytes 52
  27.1 4.9 %copy-start.1 = (bf16[128,8,16,128]{3,2,1,0:T(8,128)(2,1)S(1)}, bf16[128,8,16,128]{3,2,1,0:T(8,128)(2,1)}, u32[]{:S(2)}) copy-start(bf16[128,8,16,128]{3,2,1,0:T(8,128)(2,1)} %copy.63) | copy-start | bytes 12582916
  32.0 2.5 %copy-start.3 = (f32[16,4,256,32]{2,3,1,0:T(8,128)}, f32[16,4,256,32]{2,3,1,0:T(8,128)S(1)}, u32[]{:S(2)}) copy-start(f32[16,4,256,32]{2,3,1,0:T(8,128)S(1)} %get-tuple-element.30) | copy-start | bytes 6291460
  35.9 4.7 %copy-start.10 = (s32[65,8]{0,1:T(8,128)S(1)}, s32[65,8]{0,1:T(8,128)}, u32[]{:S(2)}) copy-start(s32[65,8]{0,1:T(8,128)} %param.27) | copy-start | bytes 6244
  65.3 15.1 %all-to-all-start.1 = ((f32[32,1,2112]{2,1,0:T(1,128)}), f32[32,1,2112]{2,1,0:T(1,128)S(1)}, u32[]{:S(2)}, u32[]{:S(2)}) async-start(f32[32,1,2112]{2,1,0:T(1,128)} %copy.51), calls=%async_computation.1 | async-start | bytes 557056 | tf_op jit(solution)/shard_map/all_to_all | solution.py:64
  70.0 17.4 %copy-start.9 = (bf16[1,1,2048]{2,1,0:T(2,128)(2,1)S(1)}, bf16[1,1,2048]{2,1,0:T(2,128)(2,1)}, u32[]{:S(2)}) copy-start(bf16[1,1,2048]{2,1,0:T(2,128)(2,1)} %param.23) | copy-start | bytes 12292
  80.4 18.9 %copy-start.8 = (f32[2048]{0:T(1024)S(1)}, f32[2048]{0:T(1024)}, u32[]{:S(2)}) copy-start(f32[2048]{0:T(1024)} %param.26) | copy-start | bytes 24580
  84.7 13.2 %all-to-all-start.2 = ((f32[32,1,2048]{2,1,0:T(1,128)}), f32[32,1,2048]{2,1,0:T(1,128)S(1)}, u32[]{:S(2)}, u32[]{:S(2)}) async-start(f32[32,1,2048]{2,1,0:T(1,128)} %copy.52), calls=%async_computation.2 | async-start | bytes 524288 | tf_op jit(solution)/shard_map/all_to_all | solution.py:82
  100.8 29.6 %all-to-all-start.3 = ((bf16[32,8,2048]{2,1,0:T(8,128)(2,1)}), bf16[32,8,2048]{2,1,0:T(8,128)(2,1)}, u32[]{:S(2)}, u32[]{:S(2)}) async-start(bf16[32,8,2048]{2,1,0:T(8,128)(2,1)} %fusion.22), calls=%async_computation.3 | async-start | bytes 2097152 | tf_op jit(solution)/shard_map/all_to_all | solution.py:104
  104.2 4.7 %copy-start.14 = (bf16[1,2048,1024]{2,1,0:T(8,128)(2,1)S(1)}, bf16[1,2048,1024]{2,1,0:T(8,128)(2,1)}, u32[]{:S(2)}) copy-start(bf16[1,2048,1024]{2,1,0:T(8,128)(2,1)} %param.30) | copy-start | bytes 12582916
  108.9 2.6 %copy-start.13 = (bf16[1,1024,2048]{2,1,0:T(8,128)(2,1)S(1)}, bf16[1,1024,2048]{2,1,0:T(8,128)(2,1)}, u32[]{:S(2)}) copy-start(bf16[1,1024,2048]{2,1,0:T(8,128)(2,1)} %param.31) | copy-start | bytes 12582916
  130.4 52.4 %all-to-all-start.4 = ((bf16[32,16,2048]{2,1,0:T(8,128)(2,1)}), bf16[32,16,2048]{2,1,0:T(8,128)(2,1)S(1)}, u32[]{:S(2)}, u32[]{:S(2)}) async-start(bf16[32,16,2048]{2,1,0:T(8,128)(2,1)} %fusion.16), calls=%async_computation.4 | async-start | bytes 4194304 | tf_op jit(solution)/shard_map/all_to_all | solution.py:121
  144.8 42.1 %copy-start.11 = (f32[65,8]{0,1:T(8,128)S(1)}, f32[65,8]{0,1:T(8,128)}, u32[]{:S(2)}) copy-start(f32[65,8]{0,1:T(8,128)} %param.28) | copy-start | bytes 6244
  182.9 30.3 %all-to-all-start.5 = ((bf16[32,8,2048]{2,1,0:T(8,128)(2,1)}), bf16[32,8,2048]{2,1,0:T(8,128)(2,1)S(1)}, u32[]{:S(2)}, u32[]{:S(2)}) async-start(bf16[32,8,2048]{2,1,0:T(8,128)(2,1)} %fusion.19), calls=%async_computation.5 | async-start | bytes 2097152 | tf_op jit(solution)/shard_map/all_to_all | solution.py:121
  213.1 0.9 copy-start.4
  213.1 0.9 copy-start.5
  214.1 0.9 copy-start.2

commit v7 on v6

--- a/solution.py
+++ b/solution.py
@@ -190,9 +190,8 @@
     second_done = experts_on(second_in, experts)
     first_back, second_done = lax.optimization_barrier((first_back, second_done))
     second_back = give_back(second_done)
-    returned = jnp.concatenate([first_back, second_back], axis=1).reshape(
-        tensor_count * stride, model_width
-    )
+    first_back = first_back.reshape(tensor_count * early, model_width)
+    second_back = second_back.reshape(tensor_count * late, model_width)
     place = jnp.concatenate(
         [
             prefill_routes * stride + prefill_rank,
@@ -208,20 +207,16 @@
     rest = mixing - high.astype(jnp.float32)
     middle = rest.astype(jnp.bfloat16)
     low = (rest - middle.astype(jnp.float32)).astype(jnp.bfloat16)
-
-    def combined(lo, hi, row_float):
-        parts = jnp.dot(
-            jnp.concatenate([high[lo:hi], middle[lo:hi], low[lo:hi]], axis=0),
-            returned,
-            preferred_element_type=jnp.float32,
-        ).reshape(3, hi - lo, model_width)
-        weighted = (parts[0] + parts[1]) + parts[2]
-        return (row_float + weighted).astype(jnp.bfloat16)
-
-    return (
-        combined(0, prefill_count, prefill_float),
-        combined(prefill_count, row_count, decode_float)[None],
-    )
+    split = jnp.concatenate([high, middle, low], axis=0).reshape(3 * row_count, tensor_count, stride)
+    first_mix = split[:, :, :early].reshape(3 * row_count, tensor_count * early)
+    second_mix = split[:, :, early:].reshape(3 * row_count, tensor_count * late)
+    first_sum = jnp.dot(first_mix, first_back, preferred_element_type=jnp.float32)
+    second_sum = jnp.dot(second_mix, second_back, preferred_element_type=jnp.float32)
+    parts = (first_sum + second_sum).reshape(3, row_count, model_width)
+    weighted = (parts[0] + parts[1]) + parts[2]
+    row_float = jnp.concatenate([prefill_float, decode_float], axis=0)
+    mixed_rows = (row_float + weighted).astype(jnp.bfloat16)
+    return (mixed_rows[:prefill_count], mixed_rows[prefill_count:][None])
 
 
 def solution(mesh):

time: 218 us -> 219 us (level)
  matrix products: 34.9 us -> 38.7 us
    dot_general x2, matrix products: 1.3 us -> 3.76 us  [the longest x1 2.2 us: per_device(): jnp.dot(second_mix, second_back, preferred_element_type=jnp.float32)]
  transfers between devices with their start and end apart: 6 -> 6, of which waited for: 6 -> 6; matrix products, arithmetic and copies ran while one was open for 23% -> 24% of each run, Pallas kernels for 0% -> 0%
where the time goes in v7:
time: 219 us
  waiting for transfers between devices  120 us (55%)
  matrix products  38.7 us (18%)
  starting transfers between devices  25.3 us (12%)
  local copies, waits for them, and re-layouts  22.4 us (10%)
  other arithmetic  10.7 us (5%)
    all_to_all x2, waiting for transfers between devices, give_back(): lax.all_to_all(lax.psum_scatter(done, 'dp', scatter_dimension=0, tiled=Tr...  60.8 us
    all_to_all x2, waiting for transfers between devices, dispatch(): lax.all_to_all(outgoing, 'tensor', split_axis=0, concat_axis=0, tiled=True)  38.6 us
    unnamed x39, local copies, waits for them, and re-layouts  12.3 us
    dot_general x2, matrix products, expert_mlp(): return jnp.dot(active, down_w, preferred_element_type=jnp.float32)  11.1 us
    all_to_all x2, starting transfers between devices, dispatch(): lax.all_to_all(outgoing, 'tensor', split_axis=0, concat_axis=0, tiled=True)  10.7 us
    all_to_all x1, waiting for transfers between devices, attention_finish(): received = lax.all_to_all(payload, 'tensor', 0, 0, tiled=True)  10.2 us
    all_to_all x1, waiting for transfers between devices, attention_finish(): lax.all_to_all(partial.reshape(tensor_count, per_device, model_width), 't...  10 us
    dot_general x2, matrix products, expert_mlp(): gate = jnp.dot(flat_rows, gate_w, preferred_element_type=jnp.float32)  9.41 us
  transfers between devices with their start and end apart: 6, of which 6 were waited for; matrix products, arithmetic and copies ran while one was open for 24% of the time, Pallas kernels for 0%

profile of v7, /device:TPU:0, one launch (start us, length us, event | category | flops | bytes accessed | tf_op | source)
XLA Modules:
  0.0 218.6 jit_solution(9836901456270479292)
XLA Ops:
  6.0 2.2 convolution_convert_fusion
  8.1 7.3 %all-to-all-start = ((bf16[32,16,2048]{2,1,0:T(8,128)(2,1)}), bf16[32,16,2048]{2,1,0:T(8,128)(2,1)S(1)}, u32[]{:S(2)}, u32[]{:S(2)}) async-start(bf16[32,16,2048]{2,1,0:T(8,128)(2,1)} %bitcast.13), calls=%async_computation | async-start | bytes 4194304 | tf_op jit(solution)/shard_map/all_to_all | solution.py:104
  15.5 5.6 %copy.75 = bf16[128,8,16,128]{3,2,1,0:T(8,128)(2,1)} copy(bf16[128,8,16,128]{3,1,2,0:T(8,128)(2,1)} %bitcast.163) | data formatting | bytes 8388608
  21.4 5.6 %copy.78 = bf16[128,8,16,128]{3,2,1,0:T(8,128)(2,1)} copy(bf16[128,8,16,128]{3,1,2,0:T(8,128)(2,1)} %bitcast.164) | data formatting | bytes 8388608
  27.2 4.8 %fusion.24 = (f32[32,16]{0,1:T(8,128)S(1)}, f32[16,4,256,32]{2,3,1,0:T(8,128)S(1)}) fusion(pred[4,32,256]{2,1,0:T(8,128)(4,1)S(1)} %broadcast_and_fusion, bf16[32,16,128,1]{2,1,0,3:T(8,128)(2,1)S(1)} %bitcast.180, bf16[4,256,16,128]{3,2,1,0:T(8,128)(2,1)} %bitcast.165), kind=kOutput, calls=%fused_computation.30 | convolution fusion | flops 135790080 | bytes 6457344 | tf_op jit(solution)/shard_map/rhd,gjhd->grhj/dot_general | solution.py:35
  32.0 2.4 %fusion.41 = f32[32,16,128]{2,0,1:T(8,128)S(1)} fusion(bf16[4,256,16,128]{3,2,1,0:T(8,128)(2,1)S(1)} %bitcast.166, f32[16,4,256,32]{2,3,1,0:T(8,128)S(1)} %get-tuple-element.29, f32[32,16]{0,1:T(8,128)S(1)} %get-tuple-element.23, pred[4,32,256]{2,1,0:T(8,128)(4,1)S(1)} %broadcast_and_fusion), kind=kOutput, calls=%fused_computation.42 | convolution fusion | flops 136314880 | bytes 6588416 | tf_op jit(solution)/shard_map/grhj,gjhd->rhd/dot_general | solution.py:48
  37.2 2.2 %fusion.30 = f32[32,16]{0,1:T(8,128)S(1)} fusion(f32[16,4,256,32]{2,3,1,0:T(8,128)} %copy-done.3, f32[32,16]{0,1:T(8,128)S(1)} %get-tuple-element.23, pred[4,32,256]{2,1,0:T(8,128)(4,1)S(1)} %broadcast_and_fusion), kind=kLoop, calls=%fused_computation.35 | loop fusion | flops 2096640 | bytes 2134016 | tf_op jit(solution)/shard_map/reduce_sum | solution.py:47
  40.9 23.4 %all-to-all-done = bf16[32,16,2048]{2,1,0:T(8,128)(2,1)S(1)} async-done(((bf16[32,16,2048]{2,1,0:T(8,128)(2,1)}), bf16[32,16,2048]{2,1,0:T(8,128)(2,1)S(1)}, u32[]{:S(2)}, u32[]{:S(2)}) %all-to-all-start) | async-done | bytes 2097184 | tf_op jit(solution)/shard_map/all_to_all | solution.py:104
  65.3 4.0 %all-to-all-start.1 = ((f32[32,1,2112]{2,1,0:T(1,128)}), f32[32,1,2112]{2,1,0:T(1,128)S(1)}, u32[]{:S(2)}, u32[]{:S(2)}) async-start(f32[32,1,2112]{2,1,0:T(1,128)} %copy.60), calls=%async_computation.1 | async-start | bytes 557056 | tf_op jit(solution)/shard_map/all_to_all | solution.py:64
  70.3 10.2 %all-to-all-done.1 = f32[32,1,2112]{2,1,0:T(1,128)S(1)} async-done(((f32[32,1,2112]{2,1,0:T(1,128)}), f32[32,1,2112]{2,1,0:T(1,128)S(1)}, u32[]{:S(2)}, u32[]{:S(2)}) %all-to-all-start.1) | async-done | bytes 270368 | tf_op jit(solution)/shard_map/all_to_all | solution.py:64
  84.7 2.8 %all-to-all-start.2 = ((f32[32,1,2048]{2,1,0:T(1,128)}), f32[32,1,2048]{2,1,0:T(1,128)S(1)}, u32[]{:S(2)}, u32[]{:S(2)}) async-start(f32[32,1,2048]{2,1,0:T(1,128)} %copy.61), calls=%async_computation.2 | async-start | bytes 524288 | tf_op jit(solution)/shard_map/all_to_all | solution.py:82
  87.9 10.0 %all-to-all-done.2 = f32[32,1,2048]{2,1,0:T(1,128)S(1)} async-done(((f32[32,1,2048]{2,1,0:T(1,128)}), f32[32,1,2048]{2,1,0:T(1,128)S(1)}, u32[]{:S(2)}, u32[]{:S(2)}) %all-to-all-start.2) | async-done | bytes 262176 | tf_op jit(solution)/shard_map/all_to_all | solution.py:82
  100.9 3.4 %all-to-all-start.3 = ((bf16[32,8,2048]{2,1,0:T(8,128)(2,1)}), bf16[32,8,2048]{2,1,0:T(8,128)(2,1)}, u32[]{:S(2)}, u32[]{:S(2)}) async-start(bf16[32,8,2048]{2,1,0:T(8,128)(2,1)} %fusion.23), calls=%async_computation.3 | async-start | bytes 2097152 | tf_op jit(solution)/shard_map/all_to_all | solution.py:104
  104.3 4.7 %fusion.10 = f32[512,1024]{1,0:T(8,128)S(1)} fusion(bf16[512,2048]{1,0:T(8,128)(2,1)S(1)} %bitcast.171, bf16[1,2048,1024]{2,1,0:T(8,128)(2,1)} %param.29), kind=kOutput, calls=%fused_computation.13 | convolution fusion | flops 2147483648 | bytes 8388608 | tf_op jit(solution)/shard_map/dot_general | solution.py:14
  108.9 2.5 %multiply_convert_fusion = bf16[512,1024]{1,0:T(8,128)(2,1)S(1)} fusion(f32[512,1024]{1,0:T(8,128)S(1)} %fusion.10, bf16[512,2048]{1,0:T(8,128)(2,1)S(1)} %bitcast.172, bf16[1,2048,1024]{2,1,0:T(8,128)(2,1)S(1)} %copy-done.14), kind=kOutput, calls=%fused_computation.34 | convolution fusion | flops 2150629376 | bytes 9437184 | tf_op jit(solution)/shard_map/dot_general | solution.py:15
  111.5 3.7 %fusion.16 = bf16[32,16,2048]{2,1,0:T(8,128)(2,1)} fusion(bf16[32,16,1024]{2,1,0:T(8,128)(2,1)S(1)} %bitcast.187, bf16[1,1024,2048]{2,1,0:T(8,128)(2,1)S(1)} %copy-done.13), kind=kOutput, calls=%fused_computation.19 | convolution fusion | flops 2148532224 | bytes 7340032 | tf_op jit(solution)/shard_map/dot_general | solution.py:17
  115.2 15.2 %all-to-all-done.3 = bf16[32,8,2048]{2,1,0:T(8,128)(2,1)} async-done(((bf16[32,8,2048]{2,1,0:T(8,128)(2,1)}), bf16[32,8,2048]{2,1,0:T(8,128)(2,1)}, u32[]{:S(2)}, u32[]{:S(2)}) %all-to-all-start.3) | async-done | bytes 1048608 | tf_op jit(solution)/shard_map/all_to_all | solution.py:104
  130.4 3.5 %all-to-all-start.4 = ((bf16[32,16,2048]{2,1,0:T(8,128)(2,1)}), bf16[32,16,2048]{2,1,0:T(8,128)(2,1)S(1)}, u32[]{:S(2)}, u32[]{:S(2)}) async-start(bf16[32,16,2048]{2,1,0:T(8,128)(2,1)} %fusion.16), calls=%async_computation.4 | async-start | bytes 4194304 | tf_op jit(solution)/shard_map/all_to_all | solution.py:121
  134.0 4.7 %fusion.8 = f32[256,1024]{1,0:T(8,128)} fusion(bf16[1,2048,1024]{2,1,0:T(8,128)(2,1)} %param.29, bf16[32,8,2048]{2,1,0:T(8,128)(2,1)} %all-to-all-done.3), kind=kOutput, calls=%fused_computation.11 | convolution fusion | flops 1073741824 | bytes 6291456 | tf_op jit(solution)/shard_map/dot_general | solution.py:14
  138.7 7.4 %fusion.19 = bf16[32,8,2048]{2,1,0:T(8,128)(2,1)} fusion(bf16[1,1024,2048]{2,1,0:T(8,128)(2,1)} %param.31, bf16[1,2048,1024]{2,1,0:T(8,128)(2,1)} %param.30, bf16[32,8,2048]{2,1,0:T(8,128)(2,1)} %all-to-all-done.3, f32[256,1024]{1,0:T(8,128)} %fusion.8), kind=kOutput, calls=%fused_computation.23 | convolution fusion | flops 2149580800 | bytes 11534336 | tf_op jit(solution)/shard_map/dot_general | solution.py:17
  146.2 36.7 %all-to-all-done.4 = bf16[32,16,2048]{2,1,0:T(8,128)(2,1)S(1)} async-done(((bf16[32,16,2048]{2,1,0:T(8,128)(2,1)}), bf16[32,16,2048]{2,1,0:T(8,128)(2,1)S(1)}, u32[]{:S(2)}, u32[]{:S(2)}) %all-to-all-start.4) | async-done | bytes 2097184 | tf_op jit(solution)/shard_map/all_to_all | solution.py:121
  182.9 4.4 %all-to-all-start.5 = ((bf16[32,8,2048]{2,1,0:T(8,128)(2,1)}), bf16[32,8,2048]{2,1,0:T(8,128)(2,1)}, u32[]{:S(2)}, u32[]{:S(2)}) async-start(bf16[32,8,2048]{2,1,0:T(8,128)(2,1)} %fusion.19), calls=%async_computation.5 | async-start | bytes 2097152 | tf_op jit(solution)/shard_map/all_to_all | solution.py:121
  189.2 24.1 %all-to-all-done.5 = bf16[32,8,2048]{2,1,0:T(8,128)(2,1)} async-done(((bf16[32,8,2048]{2,1,0:T(8,128)(2,1)}), bf16[32,8,2048]{2,1,0:T(8,128)(2,1)}, u32[]{:S(2)}, u32[]{:S(2)}) %all-to-all-start.5) | async-done | bytes 1048608 | tf_op jit(solution)/shard_map/all_to_all | solution.py:121
  213.2 2.2 %convolution_bitcast_fusion = f32[195,2048]{1,0:T(8,128)S(1)} fusion(bf16[32,8,2048]{2,1,0:T(8,128)(2,1)} %all-to-all-done.5, bf16[65,32,24]{0,1,2:T(8,128)(2,1)} %get-tuple-element.21, bf16[65,32,24]{0,1,2:T(8,128)(2,1)} %get-tuple-element.20, bf16[65,32,24]{0,1,2:T(8,128)(2,1)S(1)} %copy.105), kind=kOutput, calls=%fused_computation.21 | convolution fusion | flops 205370880 | bytes 2945536 | tf_op jit(solution)/shard_map/dot_general | solution.py:214
  (110 shorter events, 23.6 us)
Async XLA Ops:
  0.6 82.2 %copy-start = (bf16[64,2048]{1,0:T(8,128)(2,1)S(1)}, bf16[64,2048]{1,0:T(8,128)(2,1)}, u32[]{:S(2)}) copy-start(bf16[64,2048]{1,0:T(8,128)(2,1)} %param.24) | copy-start | bytes 786436
  8.1 7.3 %copy-start.7 = (bf16[1,32,2048]{2,1,0:T(8,128)(2,1)S(1)}, bf16[1,32,2048]{2,1,0:T(8,128)(2,1)}, u32[]{:S(2)}) copy-start(bf16[1,32,2048]{2,1,0:T(8,128)(2,1)} %param.16) | copy-start | bytes 393220
  8.1 56.2 %all-to-all-start = ((bf16[32,16,2048]{2,1,0:T(8,128)(2,1)}), bf16[32,16,2048]{2,1,0:T(8,128)(2,1)S(1)}, u32[]{:S(2)}, u32[]{:S(2)}) async-start(bf16[32,16,2048]{2,1,0:T(8,128)(2,1)} %bitcast.13), calls=%async_computation | async-start | bytes 4194304 | tf_op jit(solution)/shard_map/all_to_all | solution.py:104
  15.5 5.6 %copy-start.6 = (bf16[1,32,2048]{2,1,0:T(8,128)(2,1)S(1)}, bf16[1,32,2048]{2,1,0:T(8,128)(2,1)}, u32[]{:S(2)}) copy-start(bf16[1,32,2048]{2,1,0:T(8,128)(2,1)} %param.17) | copy-start | bytes 393220
  21.4 5.6 %copy-start.15 = (s32[1,32]{1,0:T(1,128)S(1)}, s32[1,32]{1,0:T(1,128)}, u32[]{:S(2)}) copy-start(s32[1,32]{1,0:T(1,128)} %param.21) | copy-start | bytes 388
  21.4 5.6 %copy-start.12 = (s32[1,4]{1,0:T(1,128)S(1)}, s32[1,4]{1,0:T(1,128)}, u32[]{:S(2)}) copy-start(s32[1,4]{1,0:T(1,128)} %param.22) | copy-start | bytes 52
  27.2 4.9 %copy-start.1 = (bf16[128,8,16,128]{3,2,1,0:T(8,128)(2,1)S(1)}, bf16[128,8,16,128]{3,2,1,0:T(8,128)(2,1)}, u32[]{:S(2)}) copy-start(bf16[128,8,16,128]{3,2,1,0:T(8,128)(2,1)} %copy.78) | copy-start | bytes 12582916
  32.0 2.5 %copy-start.3 = (f32[16,4,256,32]{2,3,1,0:T(8,128)}, f32[16,4,256,32]{2,3,1,0:T(8,128)S(1)}, u32[]{:S(2)}) copy-start(f32[16,4,256,32]{2,3,1,0:T(8,128)S(1)} %get-tuple-element.29) | copy-start | bytes 6291460
  35.9 4.7 %copy-start.10 = (s32[65,8]{0,1:T(8,128)S(1)}, s32[65,8]{0,1:T(8,128)}, u32[]{:S(2)}) copy-start(s32[65,8]{0,1:T(8,128)} %param.27) | copy-start | bytes 6244
  65.3 15.1 %all-to-all-start.1 = ((f32[32,1,2112]{2,1,0:T(1,128)}), f32[32,1,2112]{2,1,0:T(1,128)S(1)}, u32[]{:S(2)}, u32[]{:S(2)}) async-start(f32[32,1,2112]{2,1,0:T(1,128)} %copy.60), calls=%async_computation.1 | async-start | bytes 557056 | tf_op jit(solution)/shard_map/all_to_all | solution.py:64
  70.1 17.4 %copy-start.9 = (bf16[1,1,2048]{2,1,0:T(2,128)(2,1)S(1)}, bf16[1,1,2048]{2,1,0:T(2,128)(2,1)}, u32[]{:S(2)}) copy-start(bf16[1,1,2048]{2,1,0:T(2,128)(2,1)} %param.23) | copy-start | bytes 12292
  80.5 18.9 %copy-start.8 = (f32[2048]{0:T(1024)S(1)}, f32[2048]{0:T(1024)}, u32[]{:S(2)}) copy-start(f32[2048]{0:T(1024)} %param.26) | copy-start | bytes 24580
  84.7 13.2 %all-to-all-start.2 = ((f32[32,1,2048]{2,1,0:T(1,128)}), f32[32,1,2048]{2,1,0:T(1,128)S(1)}, u32[]{:S(2)}, u32[]{:S(2)}) async-start(f32[32,1,2048]{2,1,0:T(1,128)} %copy.61), calls=%async_computation.2 | async-start | bytes 524288 | tf_op jit(solution)/shard_map/all_to_all | solution.py:82
  100.9 29.6 %all-to-all-start.3 = ((bf16[32,8,2048]{2,1,0:T(8,128)(2,1)}), bf16[32,8,2048]{2,1,0:T(8,128)(2,1)}, u32[]{:S(2)}, u32[]{:S(2)}) async-start(bf16[32,8,2048]{2,1,0:T(8,128)(2,1)} %fusion.23), calls=%async_computation.3 | async-start | bytes 2097152 | tf_op jit(solution)/shard_map/all_to_all | solution.py:104
  104.2 4.7 %copy-start.14 = (bf16[1,2048,1024]{2,1,0:T(8,128)(2,1)S(1)}, bf16[1,2048,1024]{2,1,0:T(8,128)(2,1)}, u32[]{:S(2)}) copy-start(bf16[1,2048,1024]{2,1,0:T(8,128)(2,1)} %param.30) | copy-start | bytes 12582916
  108.9 2.6 %copy-start.13 = (bf16[1,1024,2048]{2,1,0:T(8,128)(2,1)S(1)}, bf16[1,1024,2048]{2,1,0:T(8,128)(2,1)}, u32[]{:S(2)}) copy-start(bf16[1,1024,2048]{2,1,0:T(8,128)(2,1)} %param.31) | copy-start | bytes 12582916
  130.4 52.4 %all-to-all-start.4 = ((bf16[32,16,2048]{2,1,0:T(8,128)(2,1)}), bf16[32,16,2048]{2,1,0:T(8,128)(2,1)S(1)}, u32[]{:S(2)}, u32[]{:S(2)}) async-start(bf16[32,16,2048]{2,1,0:T(8,128)(2,1)} %fusion.16), calls=%async_computation.4 | async-start | bytes 4194304 | tf_op jit(solution)/shard_map/all_to_all | solution.py:121
  146.1 41.1 %copy-start.2 = (bf16[64,2048]{1,0:T(8,128)(2,1)S(1)}, bf16[64,2048]{1,0:T(8,128)(2,1)}, u32[]{:S(2)}) copy-start(bf16[64,2048]{1,0:T(8,128)(2,1)} %param.25) | copy-start | bytes 786436
  146.1 41.2 %copy-start.11 = (f32[65,8]{0,1:T(8,128)S(1)}, f32[65,8]{0,1:T(8,128)}, u32[]{:S(2)}) copy-start(f32[65,8]{0,1:T(8,128)} %param.28) | copy-start | bytes 6244
  182.9 30.4 %all-to-all-start.5 = ((bf16[32,8,2048]{2,1,0:T(8,128)(2,1)}), bf16[32,8,2048]{2,1,0:T(8,128)(2,1)}, u32[]{:S(2)}, u32[]{:S(2)}) async-start(bf16[32,8,2048]{2,1,0:T(8,128)(2,1)} %fusion.19), calls=%async_computation.5 | async-start | bytes 2097152 | tf_op jit(solution)/shard_map/all_to_all | solution.py:121
  213.2 2.2 %copy-start.4 = (bf16[65,32,24]{0,1,2:T(8,128)(2,1)S(1)}, bf16[65,32,24]{0,1,2:T(8,128)(2,1)}, u32[]{:S(2)}) copy-start(bf16[65,32,24]{0,1,2:T(8,128)(2,1)} %get-tuple-element.20) | copy-start | bytes 299524
  213.2 2.2 %copy-start.5 = (bf16[65,32,24]{0,1,2:T(8,128)(2,1)S(1)}, bf16[65,32,24]{0,1,2:T(8,128)(2,1)}, u32[]{:S(2)}) copy-start(bf16[65,32,24]{0,1,2:T(8,128)(2,1)} %get-tuple-element.21) | copy-start | bytes 299524

commit v8 on v6

--- a/solution.py
+++ b/solution.py
@@ -80,9 +80,10 @@
     partial = jnp.dot(attended, out_weight, preferred_element_type=jnp.float32)
     per_device = requests // tensor_count
     gathered = lax.all_to_all(
-        partial.reshape(tensor_count, per_device, model_width), "tensor", 0, 0, tiled=True
-    )
-    projected = jnp.sum(gathered, axis=0)
+        partial.astype(jnp.bfloat16).reshape(tensor_count, per_device, model_width),
+        "tensor", 0, 0, tiled=True,
+    )
+    projected = jnp.sum(gathered.astype(jnp.float32), axis=0)
     return (decode_residual[0].astype(jnp.float32) + projected).astype(jnp.bfloat16)
 
 
@@ -113,7 +114,13 @@
     one_hot = (flat_expert[:, None] == jnp.arange(tensor_count, dtype=jnp.int32)[None, :]).astype(
         jnp.int32
     )
-    earlier = jnp.cumsum(one_hot, axis=0) - one_hot
+    count = flat_expert.shape[0]
+    lower = (
+        jnp.arange(count, dtype=jnp.int32)[:, None] > jnp.arange(count, dtype=jnp.int32)[None, :]
+    ).astype(jnp.bfloat16)
+    earlier = jnp.dot(
+        lower, one_hot.astype(jnp.bfloat16), preferred_element_type=jnp.float32
+    ).astype(jnp.int32)
     return jnp.sum(earlier * one_hot, axis=1), jnp.sum(one_hot, axis=0)
 
 

time: 218 us -> 215 us (0.986)
    all_to_all x2, waiting for transfers between devices: 38.6 us -> 42.8 us  [dispatch(): lax.all_to_all(outgoing, 'tensor', split_axis=0, concat_axis=0, tiled=True)]
    all_to_all x1, waiting for transfers between devices: 10 us -> 7.66 us  [attention_finish(): lax.all_to_all(partial.astype(jnp.bfloat16).reshape(tensor_count, per_dev...]
    dot_general x1, matrix products: 4.84 us -> 2.48 us  [attention_partials(): jnp.einsum('rhd,gjhd->grhj', query_heads, key_table, preferred_element_ty...]
    unnamed x39 -> x41, local copies, waits for them, and re-layouts: 13.1 us -> 12.1 us
  transfers between devices with their start and end apart: 6 -> 6, of which waited for: 6 -> 6; matrix products, arithmetic and copies ran while one was open for 23% -> 22% of each run, Pallas kernels for 0% -> 0%
where the time goes in v8:
time: 215 us; the launch traced here: 214 us
  waiting for transfers between devices  123 us (57%)
  matrix products  33.1 us (15%)
  starting transfers between devices  25 us (12%)
  local copies, waits for them, and re-layouts  21.2 us (10%)
  other arithmetic  10.5 us (5%)
    all_to_all x2, waiting for transfers between devices, give_back(): lax.all_to_all(lax.psum_scatter(done, 'dp', scatter_dimension=0, tiled=Tr...  62.1 us
    all_to_all x2, waiting for transfers between devices, dispatch(): lax.all_to_all(outgoing, 'tensor', split_axis=0, concat_axis=0, tiled=True)  42.8 us
    unnamed x41, local copies, waits for them, and re-layouts  12.1 us
    dot_general x2, matrix products, expert_mlp(): return jnp.dot(active, down_w, preferred_element_type=jnp.float32)  10.8 us
    all_to_all x2, starting transfers between devices, dispatch(): lax.all_to_all(outgoing, 'tensor', split_axis=0, concat_axis=0, tiled=True)  10.7 us
    all_to_all x1, waiting for transfers between devices, attention_finish(): received = lax.all_to_all(payload, 'tensor', 0, 0, tiled=True)  10.1 us
    dot_general x2, matrix products, expert_mlp(): gate = jnp.dot(flat_rows, gate_w, preferred_element_type=jnp.float32)  8.42 us
    all_to_all x1, waiting for transfers between devices, attention_finish(): lax.all_to_all(partial.astype(jnp.bfloat16).reshape(tensor_count, per_dev...  7.66 us
  transfers between devices with their start and end apart: 6, of which 6 were waited for; matrix products, arithmetic and copies ran while one was open for 22% of the time, Pallas kernels for 0%

profile of v8, /device:TPU:0, one launch (start us, length us, event | category | flops | bytes accessed | tf_op | source)
XLA Modules:
  0.0 214.2 jit_solution(9269932025871102870)
XLA Ops:
  4.5 2.1 convolution_convert_fusion
  6.6 7.3 %all-to-all-start = ((bf16[32,16,2048]{2,1,0:T(8,128)(2,1)}), bf16[32,16,2048]{2,1,0:T(8,128)(2,1)S(1)}, u32[]{:S(2)}, u32[]{:S(2)}) async-start(bf16[32,16,2048]{2,1,0:T(8,128)(2,1)} %bitcast.12), calls=%async_computation | async-start | bytes 4194304 | tf_op jit(solution)/shard_map/all_to_all | solution.py:105
  14.0 5.6 %copy.56 = bf16[128,8,16,128]{3,2,1,0:T(8,128)(2,1)} copy(bf16[128,8,16,128]{3,1,2,0:T(8,128)(2,1)} %bitcast.154) | data formatting | bytes 8388608
  19.9 3.7 %copy.59 = bf16[128,8,16,128]{3,2,1,0:T(8,128)(2,1)S(1)} copy(bf16[128,8,16,128]{3,1,2,0:T(8,128)(2,1)} %bitcast.155) | data formatting | bytes 8388608
  23.9 2.5 %fusion.24 = (f32[32,16]{0,1:T(8,128)S(1)}, f32[16,4,256,32]{2,3,1,0:T(8,128)S(1)}) fusion(pred[4,32,256]{2,1,0:T(8,128)(4,1)S(1)} %broadcast_and_fusion, bf16[32,16,128,1]{2,1,0,3:T(8,128)(2,1)S(1)} %bitcast.169, bf16[4,256,16,128]{3,2,1,0:T(8,128)(2,1)S(1)} %bitcast.156), kind=kOutput, calls=%fused_computation.29 | convolution fusion | flops 135790080 | bytes 6457344 | tf_op jit(solution)/shard_map/rhd,gjhd->grhj/dot_general | solution.py:35
  26.4 2.5 %fusion.40 = f32[32,16,128]{2,0,1:T(8,128)S(1)} fusion(bf16[4,256,16,128]{3,2,1,0:T(8,128)(2,1)S(1)} %bitcast.157, f32[16,4,256,32]{2,3,1,0:T(8,128)S(1)} %get-tuple-element.28, f32[32,16]{0,1:T(8,128)S(1)} %get-tuple-element.22, pred[4,32,256]{2,1,0:T(8,128)(4,1)S(1)} %broadcast_and_fusion), kind=kOutput, calls=%fused_computation.40 | convolution fusion | flops 136314880 | bytes 6588416 | tf_op jit(solution)/shard_map/grhj,gjhd->rhd/dot_general | solution.py:48
  31.5 2.2 %fusion.29 = f32[32,16]{0,1:T(8,128)S(1)} fusion(f32[16,4,256,32]{2,3,1,0:T(8,128)} %copy-done.3, f32[32,16]{0,1:T(8,128)S(1)} %get-tuple-element.22, pred[4,32,256]{2,1,0:T(8,128)(4,1)S(1)} %broadcast_and_fusion), kind=kLoop, calls=%fused_computation.33 | loop fusion | flops 2096640 | bytes 2134016 | tf_op jit(solution)/shard_map/reduce_sum | solution.py:47
  35.3 27.6 %all-to-all-done = bf16[32,16,2048]{2,1,0:T(8,128)(2,1)S(1)} async-done(((bf16[32,16,2048]{2,1,0:T(8,128)(2,1)}), bf16[32,16,2048]{2,1,0:T(8,128)(2,1)S(1)}, u32[]{:S(2)}, u32[]{:S(2)}) %all-to-all-start) | async-done | bytes 2097184 | tf_op jit(solution)/shard_map/all_to_all | solution.py:105
  63.8 4.0 %all-to-all-start.1 = ((f32[32,1,2112]{2,1,0:T(1,128)}), f32[32,1,2112]{2,1,0:T(1,128)S(1)}, u32[]{:S(2)}, u32[]{:S(2)}) async-start(f32[32,1,2112]{2,1,0:T(1,128)} %copy.48), calls=%async_computation.1 | async-start | bytes 557056 | tf_op jit(solution)/shard_map/all_to_all | solution.py:64
  68.8 10.1 %all-to-all-done.1 = f32[32,1,2112]{2,1,0:T(1,128)S(1)} async-done(((f32[32,1,2112]{2,1,0:T(1,128)}), f32[32,1,2112]{2,1,0:T(1,128)S(1)}, u32[]{:S(2)}, u32[]{:S(2)}) %all-to-all-start.1) | async-done | bytes 270368 | tf_op jit(solution)/shard_map/all_to_all | solution.py:64
  84.2 2.8 %all-to-all-start.2 = ((bf16[32,2,1024]{2,1,0:T(2,128)(2,1)}), bf16[32,2,1024]{2,1,0:T(2,128)(2,1)S(1)}, u32[]{:S(2)}, u32[]{:S(2)}) async-start(bf16[32,2,1024]{2,1,0:T(2,128)(2,1)} %reshape.344), calls=%async_computation.2 | async-start | bytes 262144 | tf_op jit(solution)/shard_map/all_to_all | solution.py:82
  87.3 7.7 %all-to-all-done.2 = bf16[32,2,1024]{2,1,0:T(2,128)(2,1)S(1)} async-done(((bf16[32,2,1024]{2,1,0:T(2,128)(2,1)}), bf16[32,2,1024]{2,1,0:T(2,128)(2,1)S(1)}, u32[]{:S(2)}, u32[]{:S(2)}) %all-to-all-start.2) | async-done | bytes 131104 | tf_op jit(solution)/shard_map/all_to_all | solution.py:82
  96.7 1.5 fusion.22
  98.1 3.4 %all-to-all-start.3 = ((bf16[32,8,2048]{2,1,0:T(8,128)(2,1)}), bf16[32,8,2048]{2,1,0:T(8,128)(2,1)}, u32[]{:S(2)}, u32[]{:S(2)}) async-start(bf16[32,8,2048]{2,1,0:T(8,128)(2,1)} %fusion.22), calls=%async_computation.3 | async-start | bytes 2097152 | tf_op jit(solution)/shard_map/all_to_all | solution.py:105
  101.5 4.7 %fusion.10 = f32[512,1024]{1,0:T(8,128)S(1)} fusion(bf16[512,2048]{1,0:T(8,128)(2,1)S(1)} %bitcast.160, bf16[1,2048,1024]{2,1,0:T(8,128)(2,1)} %param.29), kind=kOutput, calls=%fused_computation.13 | convolution fusion | flops 2147483648 | bytes 8388608 | tf_op jit(solution)/shard_map/dot_general | solution.py:14
  106.2 2.5 %multiply_convert_fusion = bf16[512,1024]{1,0:T(8,128)(2,1)S(1)} fusion(f32[512,1024]{1,0:T(8,128)S(1)} %fusion.10, bf16[512,2048]{1,0:T(8,128)(2,1)S(1)} %bitcast.161, bf16[1,2048,1024]{2,1,0:T(8,128)(2,1)S(1)} %copy-done.14), kind=kOutput, calls=%fused_computation.32 | convolution fusion | flops 2150629376 | bytes 9437184 | tf_op jit(solution)/shard_map/dot_general | solution.py:15
  108.8 3.7 %fusion.16 = bf16[32,16,2048]{2,1,0:T(8,128)(2,1)} fusion(bf16[32,16,1024]{2,1,0:T(8,128)(2,1)S(1)} %bitcast.176, bf16[1,1024,2048]{2,1,0:T(8,128)(2,1)S(1)} %copy-done.13), kind=kOutput, calls=%fused_computation.20 | convolution fusion | flops 2148532224 | bytes 7340032 | tf_op jit(solution)/shard_map/dot_general | solution.py:17
  112.5 15.2 %all-to-all-done.3 = bf16[32,8,2048]{2,1,0:T(8,128)(2,1)} async-done(((bf16[32,8,2048]{2,1,0:T(8,128)(2,1)}), bf16[32,8,2048]{2,1,0:T(8,128)(2,1)}, u32[]{:S(2)}, u32[]{:S(2)}) %all-to-all-start.3) | async-done | bytes 1048608 | tf_op jit(solution)/shard_map/all_to_all | solution.py:105
  127.7 3.5 %all-to-all-start.4 = ((bf16[32,16,2048]{2,1,0:T(8,128)(2,1)}), bf16[32,16,2048]{2,1,0:T(8,128)(2,1)S(1)}, u32[]{:S(2)}, u32[]{:S(2)}) async-start(bf16[32,16,2048]{2,1,0:T(8,128)(2,1)} %fusion.16), calls=%async_computation.4 | async-start | bytes 4194304 | tf_op jit(solution)/shard_map/all_to_all | solution.py:128
  131.3 3.8 %fusion.8 = f32[256,1024]{1,0:T(8,128)S(1)} fusion(bf16[1,2048,1024]{2,1,0:T(8,128)(2,1)} %param.29, bf16[32,8,2048]{2,1,0:T(8,128)(2,1)} %all-to-all-done.3), kind=kOutput, calls=%fused_computation.11 | convolution fusion | flops 1073741824 | bytes 6291456 | tf_op jit(solution)/shard_map/dot_general | solution.py:14
  135.0 7.1 %fusion.19 = bf16[32,8,2048]{2,1,0:T(8,128)(2,1)} fusion(bf16[1,1024,2048]{2,1,0:T(8,128)(2,1)} %param.31, bf16[1,2048,1024]{2,1,0:T(8,128)(2,1)} %param.30, bf16[32,8,2048]{2,1,0:T(8,128)(2,1)} %all-to-all-done.3, f32[256,1024]{1,0:T(8,128)S(1)} %fusion.8), kind=kOutput, calls=%fused_computation.22 | convolution fusion | flops 2149580800 | bytes 11534336 | tf_op jit(solution)/shard_map/dot_general | solution.py:17
  142.1 38.0 %all-to-all-done.4 = bf16[32,16,2048]{2,1,0:T(8,128)(2,1)S(1)} async-done(((bf16[32,16,2048]{2,1,0:T(8,128)(2,1)}), bf16[32,16,2048]{2,1,0:T(8,128)(2,1)S(1)}, u32[]{:S(2)}, u32[]{:S(2)}) %all-to-all-start.4) | async-done | bytes 2097184 | tf_op jit(solution)/shard_map/all_to_all | solution.py:128
  180.2 4.0 %all-to-all-start.5 = ((bf16[32,8,2048]{2,1,0:T(8,128)(2,1)}), bf16[32,8,2048]{2,1,0:T(8,128)(2,1)S(1)}, u32[]{:S(2)}, u32[]{:S(2)}) async-start(bf16[32,8,2048]{2,1,0:T(8,128)(2,1)} %fusion.19), calls=%async_computation.5 | async-start | bytes 2097152 | tf_op jit(solution)/shard_map/all_to_all | solution.py:128
  186.3 24.1 %all-to-all-done.5 = bf16[32,8,2048]{2,1,0:T(8,128)(2,1)S(1)} async-done(((bf16[32,8,2048]{2,1,0:T(8,128)(2,1)}), bf16[32,8,2048]{2,1,0:T(8,128)(2,1)S(1)}, u32[]{:S(2)}, u32[]{:S(2)}) %all-to-all-start.5) | async-done | bytes 1048608 | tf_op jit(solution)/shard_map/all_to_all | solution.py:128
  (108 shorter events, 22.9 us)
Async XLA Ops:
  0.6 80.7 %copy-start = (bf16[64,2048]{1,0:T(8,128)(2,1)S(1)}, bf16[64,2048]{1,0:T(8,128)(2,1)}, u32[]{:S(2)}) copy-start(bf16[64,2048]{1,0:T(8,128)(2,1)} %param.24) | copy-start | bytes 786436
  6.6 7.3 %copy-start.7 = (bf16[1,32,2048]{2,1,0:T(8,128)(2,1)S(1)}, bf16[1,32,2048]{2,1,0:T(8,128)(2,1)}, u32[]{:S(2)}) copy-start(bf16[1,32,2048]{2,1,0:T(8,128)(2,1)} %param.16) | copy-start | bytes 393220
  6.6 56.2 %all-to-all-start = ((bf16[32,16,2048]{2,1,0:T(8,128)(2,1)}), bf16[32,16,2048]{2,1,0:T(8,128)(2,1)S(1)}, u32[]{:S(2)}, u32[]{:S(2)}) async-start(bf16[32,16,2048]{2,1,0:T(8,128)(2,1)} %bitcast.12), calls=%async_computation | async-start | bytes 4194304 | tf_op jit(solution)/shard_map/all_to_all | solution.py:105
  14.0 5.6 %copy-start.6 = (bf16[1,32,2048]{2,1,0:T(8,128)(2,1)S(1)}, bf16[1,32,2048]{2,1,0:T(8,128)(2,1)}, u32[]{:S(2)}) copy-start(bf16[1,32,2048]{2,1,0:T(8,128)(2,1)} %param.17) | copy-start | bytes 393220
  19.9 3.8 %copy-start.15 = (s32[1,32]{1,0:T(1,128)S(1)}, s32[1,32]{1,0:T(1,128)}, u32[]{:S(2)}) copy-start(s32[1,32]{1,0:T(1,128)} %param.21) | copy-start | bytes 388
  19.9 3.8 %copy-start.12 = (s32[1,4]{1,0:T(1,128)S(1)}, s32[1,4]{1,0:T(1,128)}, u32[]{:S(2)}) copy-start(s32[1,4]{1,0:T(1,128)} %param.22) | copy-start | bytes 52
  19.9 4.0 %copy-start.1 = (bf16[128,8,16,128]{3,2,1,0:T(8,128)(2,1)S(1)}, bf16[128,8,16,128]{3,2,1,0:T(8,128)(2,1)}, u32[]{:S(2)}) copy-start(bf16[128,8,16,128]{3,2,1,0:T(8,128)(2,1)} %copy.56) | copy-start | bytes 12582916
  26.3 2.5 %copy-start.3 = (f32[16,4,256,32]{2,3,1,0:T(8,128)}, f32[16,4,256,32]{2,3,1,0:T(8,128)S(1)}, u32[]{:S(2)}) copy-start(f32[16,4,256,32]{2,3,1,0:T(8,128)S(1)} %get-tuple-element.28) | copy-start | bytes 6291460
  30.3 4.7 %copy-start.10 = (s32[65,8]{0,1:T(8,128)S(1)}, s32[65,8]{0,1:T(8,128)}, u32[]{:S(2)}) copy-start(s32[65,8]{0,1:T(8,128)} %param.27) | copy-start | bytes 6244
  63.8 15.1 %all-to-all-start.1 = ((f32[32,1,2112]{2,1,0:T(1,128)}), f32[32,1,2112]{2,1,0:T(1,128)S(1)}, u32[]{:S(2)}, u32[]{:S(2)}) async-start(f32[32,1,2112]{2,1,0:T(1,128)} %copy.48), calls=%async_computation.1 | async-start | bytes 557056 | tf_op jit(solution)/shard_map/all_to_all | solution.py:64
  67.9 19.1 %copy-start.9 = (bf16[1,1,2048]{2,1,0:T(2,128)(2,1)S(1)}, bf16[1,1,2048]{2,1,0:T(2,128)(2,1)}, u32[]{:S(2)}) copy-start(bf16[1,1,2048]{2,1,0:T(2,128)(2,1)} %param.23) | copy-start | bytes 12292
  79.0 17.7 %copy-start.8 = (f32[2048]{0:T(1024)S(1)}, f32[2048]{0:T(1024)}, u32[]{:S(2)}) copy-start(f32[2048]{0:T(1024)} %param.26) | copy-start | bytes 24580
  84.2 10.8 %all-to-all-start.2 = ((bf16[32,2,1024]{2,1,0:T(2,128)(2,1)}), bf16[32,2,1024]{2,1,0:T(2,128)(2,1)S(1)}, u32[]{:S(2)}, u32[]{:S(2)}) async-start(bf16[32,2,1024]{2,1,0:T(2,128)(2,1)} %reshape.344), calls=%async_computation.2 | async-start | bytes 262144 | tf_op jit(solution)/shard_map/all_to_all | solution.py:82
  98.1 29.6 %all-to-all-start.3 = ((bf16[32,8,2048]{2,1,0:T(8,128)(2,1)}), bf16[32,8,2048]{2,1,0:T(8,128)(2,1)}, u32[]{:S(2)}, u32[]{:S(2)}) async-start(bf16[32,8,2048]{2,1,0:T(8,128)(2,1)} %fusion.22), calls=%async_computation.3 | async-start | bytes 2097152 | tf_op jit(solution)/shard_map/all_to_all | solution.py:105
  101.5 4.7 %copy-start.14 = (bf16[1,2048,1024]{2,1,0:T(8,128)(2,1)S(1)}, bf16[1,2048,1024]{2,1,0:T(8,128)(2,1)}, u32[]{:S(2)}) copy-start(bf16[1,2048,1024]{2,1,0:T(8,128)(2,1)} %param.30) | copy-start | bytes 12582916
  106.2 2.6 %copy-start.13 = (bf16[1,1024,2048]{2,1,0:T(8,128)(2,1)S(1)}, bf16[1,1024,2048]{2,1,0:T(8,128)(2,1)}, u32[]{:S(2)}) copy-start(bf16[1,1024,2048]{2,1,0:T(8,128)(2,1)} %param.31) | copy-start | bytes 12582916
  127.7 52.4 %all-to-all-start.4 = ((bf16[32,16,2048]{2,1,0:T(8,128)(2,1)}), bf16[32,16,2048]{2,1,0:T(8,128)(2,1)S(1)}, u32[]{:S(2)}, u32[]{:S(2)}) async-start(bf16[32,16,2048]{2,1,0:T(8,128)(2,1)} %fusion.16), calls=%async_computation.4 | async-start | bytes 4194304 | tf_op jit(solution)/shard_map/all_to_all | solution.py:128
  142.1 42.1 %copy-start.11 = (f32[65,8]{0,1:T(8,128)S(1)}, f32[65,8]{0,1:T(8,128)}, u32[]{:S(2)}) copy-start(f32[65,8]{0,1:T(8,128)} %param.28) | copy-start | bytes 6244
  180.2 30.3 %all-to-all-start.5 = ((bf16[32,8,2048]{2,1,0:T(8,128)(2,1)}), bf16[32,8,2048]{2,1,0:T(8,128)(2,1)S(1)}, u32[]{:S(2)}, u32[]{:S(2)}) async-start(bf16[32,8,2048]{2,1,0:T(8,128)(2,1)} %fusion.19), calls=%async_computation.5 | async-start | bytes 2097152 | tf_op jit(solution)/shard_map/all_to_all | solution.py:128
  210.4 0.9 copy-start.4
  210.4 0.9 copy-start.5
  211.4 0.9 copy-start.2

commit v9 on v8

--- a/solution.py
+++ b/solution.py
@@ -105,9 +105,10 @@
     return lax.all_to_all(outgoing, "tensor", split_axis=0, concat_axis=0, tiled=True)
 
 
-def experts_on(received, experts):
+def experts_on(received, experts, norm_gain):
     block = lax.all_gather(received, "dp", axis=0, tiled=True)
-    return expert_mlp(block, *experts).reshape(block.shape).astype(jnp.bfloat16)
+    _, normed = rms_normed(block.reshape(-1, block.shape[-1]), norm_gain)
+    return expert_mlp(normed, *experts).reshape(block.shape).astype(jnp.bfloat16)
 
 
 def rank_in_expert(flat_expert, tensor_count):
@@ -167,9 +168,9 @@
     prefill_rank, prefill_counts = rank_in_expert(prefill_routes, tensor_count)
     decode_rank, _ = rank_in_expert(decode_routes, tensor_count)
     overflow = jnp.maximum(prefill_counts - early, 0)
-    prefill_float, prefill_normed = rms_normed(prefill_states, norm_gain)
+    prefill_float = prefill_states.astype(jnp.float32)
     first_in = dispatch(
-        prefill_normed,
+        prefill_states,
         jnp.where(prefill_rank < early, prefill_routes * early + prefill_rank, -1),
         tensor_count * early,
     )
@@ -178,9 +179,9 @@
         out_weight.shape[0],
     )
     payload, first_in = lax.optimization_barrier((payload, first_in))
-    first_done = experts_on(first_in, experts)
+    first_done = experts_on(first_in, experts, norm_gain)
     decode_hidden = attention_finish(payload, own_score, new_values, decode_residual, out_weight)
-    decode_float, decode_normed = rms_normed(decode_hidden, norm_gain)
+    decode_float = decode_hidden.astype(jnp.float32)
     late_slot = jnp.concatenate(
         [
             jnp.where(
@@ -190,11 +191,11 @@
         ]
     )
     second_in = dispatch(
-        jnp.concatenate([prefill_normed, decode_normed], axis=0), late_slot, tensor_count * late
+        jnp.concatenate([prefill_states, decode_hidden], axis=0), late_slot, tensor_count * late
     )
     first_done, second_in = lax.optimization_barrier((first_done, second_in))
     first_back = give_back(first_done)
-    second_done = experts_on(second_in, experts)
+    second_done = experts_on(second_in, experts, norm_gain)
     first_back, second_done = lax.optimization_barrier((first_back, second_done))
     second_back = give_back(second_done)
     returned = jnp.concatenate([first_back, second_back], axis=1).reshape(

time: 215 us -> 210 us (0.977)
  waiting for transfers between devices: 123 us -> 116 us
  matrix products: 33.1 us -> 37.2 us
    all_to_all x2, waiting for transfers between devices: 42.8 us -> 38.6 us  [dispatch(): lax.all_to_all(outgoing, 'tensor', split_axis=0, concat_axis=0, tiled=True)]
    dot_general x1, matrix products: 2.48 us -> 4.83 us  [attention_partials(): jnp.einsum('rhd,gjhd->grhj', query_heads, key_table, preferred_element_ty...]
    unnamed x41 -> x47, local copies, waits for them, and re-layouts: 12.1 us -> 13.2 us
  transfers between devices with their start and end apart: 6 -> 6, of which waited for: 6 -> 6; matrix products, arithmetic and copies ran while one was open for 22% -> 25% of each run, Pallas kernels for 0% -> 0%
where the time goes in v9:
time: 210 us; the launch traced here: 209 us
  waiting for transfers between devices  116 us (55%)
  matrix products  37.2 us (18%)
  starting transfers between devices  24.3 us (12%)
  local copies, waits for them, and re-layouts  20.4 us (10%)
  other arithmetic  9.42 us (4%)
    all_to_all x2, waiting for transfers between devices, give_back(): lax.all_to_all(lax.psum_scatter(done, 'dp', scatter_dimension=0, tiled=Tr...  61.1 us
    all_to_all x2, waiting for transfers between devices, dispatch(): lax.all_to_all(outgoing, 'tensor', split_axis=0, concat_axis=0, tiled=True)  38.6 us
    unnamed x47, local copies, waits for them, and re-layouts  13.2 us
    dot_general x2, matrix products, expert_mlp(): return jnp.dot(active, down_w, preferred_element_type=jnp.float32)  10.9 us
    all_to_all x1, waiting for transfers between devices, attention_finish(): received = lax.all_to_all(payload, 'tensor', 0, 0, tiled=True)  10.3 us
    all_to_all x2, starting transfers between devices, dispatch(): lax.all_to_all(outgoing, 'tensor', split_axis=0, concat_axis=0, tiled=True)  9.94 us
    dot_general x2, matrix products, expert_mlp(): gate = jnp.dot(flat_rows, gate_w, preferred_element_type=jnp.float32)  9.13 us
    all_to_all x2, starting transfers between devices, give_back(): lax.all_to_all(lax.psum_scatter(done, 'dp', scatter_dimension=0, tiled=Tr...  7.55 us
  transfers between devices with their start and end apart: 6, of which 6 were waited for; matrix products, arithmetic and copies ran while one was open for 25% of the time, Pallas kernels for 0%

profile of v9, /device:TPU:0, one launch (start us, length us, event | category | flops | bytes accessed | tf_op | source)
XLA Modules:
  0.0 208.9 jit_solution(11512083037878001274)
XLA Ops:
  2.3 3.1 %convolution_convert_fusion = bf16[512,2048]{1,0:T(8,128)(2,1)} fusion(pred[512,64]{0,1:T(8,128)(4,1)S(1)} %fusion.58, bf16[64,2048]{1,0:T(8,128)(2,1)} %param.25), kind=kOutput, calls=%fused_computation.26 | convolution fusion | flops 135266304 | bytes 2392064 | tf_op jit(solution)/shard_map/dot_general | solution.py:102
  5.4 7.3 %all-to-all-start = ((bf16[32,16,2048]{2,1,0:T(8,128)(2,1)}), bf16[32,16,2048]{2,1,0:T(8,128)(2,1)S(1)}, u32[]{:S(2)}, u32[]{:S(2)}) async-start(bf16[32,16,2048]{2,1,0:T(8,128)(2,1)} %bitcast.145), calls=%async_computation | async-start | bytes 4194304 | tf_op jit(solution)/shard_map/all_to_all | solution.py:105
  12.8 5.6 %copy.56 = bf16[128,8,16,128]{3,2,1,0:T(8,128)(2,1)} copy(bf16[128,8,16,128]{3,1,2,0:T(8,128)(2,1)} %bitcast.146) | data formatting | bytes 8388608
  18.7 5.6 %copy.59 = bf16[128,8,16,128]{3,2,1,0:T(8,128)(2,1)} copy(bf16[128,8,16,128]{3,1,2,0:T(8,128)(2,1)} %bitcast.147) | data formatting | bytes 8388608
  24.4 4.8 %fusion.30 = (f32[32,16]{0,1:T(8,128)S(1)}, f32[16,4,256,32]{2,3,1,0:T(8,128)S(1)}) fusion(pred[4,32,256]{2,1,0:T(8,128)(4,1)S(1)} %broadcast_and_fusion, bf16[32,16,128,1]{2,1,0,3:T(8,128)(2,1)S(1)} %bitcast.161, bf16[4,256,16,128]{3,2,1,0:T(8,128)(2,1)} %bitcast.149), kind=kOutput, calls=%fused_computation.39 | convolution fusion | flops 135790080 | bytes 6457344 | tf_op jit(solution)/shard_map/rhd,gjhd->grhj/dot_general | solution.py:35
  29.3 2.4 %fusion.46 = f32[32,16,128]{2,0,1:T(8,128)S(1)} fusion(bf16[4,256,16,128]{3,2,1,0:T(8,128)(2,1)S(1)} %bitcast.148, f32[16,4,256,32]{2,3,1,0:T(8,128)S(1)} %get-tuple-element.26, f32[32,16]{0,1:T(8,128)S(1)} %get-tuple-element.20, pred[4,32,256]{2,1,0:T(8,128)(4,1)S(1)} %broadcast_and_fusion), kind=kOutput, calls=%fused_computation.50 | convolution fusion | flops 136314880 | bytes 6588416 | tf_op jit(solution)/shard_map/grhj,gjhd->rhd/dot_general | solution.py:48
  33.3 2.2 %fusion.35 = f32[32,16]{0,1:T(8,128)S(1)} fusion(f32[16,4,256,32]{2,3,1,0:T(8,128)} %copy-done.4, f32[32,16]{0,1:T(8,128)S(1)} %get-tuple-element.20, pred[4,32,256]{2,1,0:T(8,128)(4,1)S(1)} %broadcast_and_fusion), kind=kLoop, calls=%fused_computation.43 | loop fusion | flops 2096640 | bytes 2134016 | tf_op jit(solution)/shard_map/reduce_sum | solution.py:47
  38.2 23.4 %all-to-all-done = bf16[32,16,2048]{2,1,0:T(8,128)(2,1)S(1)} async-done(((bf16[32,16,2048]{2,1,0:T(8,128)(2,1)}), bf16[32,16,2048]{2,1,0:T(8,128)(2,1)S(1)}, u32[]{:S(2)}, u32[]{:S(2)}) %all-to-all-start) | async-done | bytes 2097184 | tf_op jit(solution)/shard_map/all_to_all | solution.py:105
  62.6 4.0 %all-to-all-start.1 = ((f32[32,1,2112]{2,1,0:T(1,128)}), f32[32,1,2112]{2,1,0:T(1,128)S(1)}, u32[]{:S(2)}, u32[]{:S(2)}) async-start(f32[32,1,2112]{2,1,0:T(1,128)} %copy.48), calls=%async_computation.1 | async-start | bytes 557056 | tf_op jit(solution)/shard_map/all_to_all | solution.py:64
  67.4 10.3 %all-to-all-done.1 = f32[32,1,2112]{2,1,0:T(1,128)S(1)} async-done(((f32[32,1,2112]{2,1,0:T(1,128)}), f32[32,1,2112]{2,1,0:T(1,128)S(1)}, u32[]{:S(2)}, u32[]{:S(2)}) %all-to-all-start.1) | async-done | bytes 270368 | tf_op jit(solution)/shard_map/all_to_all | solution.py:64
  81.3 2.8 %all-to-all-start.2 = ((bf16[32,2,1024]{2,1,0:T(2,128)(2,1)}), bf16[32,2,1024]{2,1,0:T(2,128)(2,1)S(1)}, u32[]{:S(2)}, u32[]{:S(2)}) async-start(bf16[32,2,1024]{2,1,0:T(2,128)(2,1)} %reshape.377), calls=%async_computation.2 | async-start | bytes 262144 | tf_op jit(solution)/shard_map/all_to_all | solution.py:82
  84.1 1.9 fusion.2
  86.0 6.3 %all-to-all-done.2 = bf16[32,2,1024]{2,1,0:T(2,128)(2,1)S(1)} async-done(((bf16[32,2,1024]{2,1,0:T(2,128)(2,1)}), bf16[32,2,1024]{2,1,0:T(2,128)(2,1)S(1)}, u32[]{:S(2)}, u32[]{:S(2)}) %all-to-all-start.2) | async-done | bytes 131104 | tf_op jit(solution)/shard_map/all_to_all | solution.py:82
  94.2 2.6 %all-to-all-start.3 = ((bf16[32,8,2048]{2,1,0:T(8,128)(2,1)}), bf16[32,8,2048]{2,1,0:T(8,128)(2,1)S(1)}, u32[]{:S(2)}, u32[]{:S(2)}) async-start(bf16[32,8,2048]{2,1,0:T(8,128)(2,1)} %fusion.25), calls=%async_computation.3 | async-start | bytes 2097152 | tf_op jit(solution)/shard_map/all_to_all | solution.py:105
  96.8 4.7 %fusion.13 = f32[512,1024]{1,0:T(8,128)S(1)} fusion(bf16[512,2048]{1,0:T(8,128)(2,1)S(1)} %bitcast.152, bf16[1,2048,1024]{2,1,0:T(8,128)(2,1)} %param.29), kind=kOutput, calls=%fused_computation.18 | convolution fusion | flops 2147483648 | bytes 8388608 | tf_op jit(solution)/shard_map/dot_general | solution.py:14
  101.5 2.5 %multiply_convert_fusion = bf16[512,1024]{1,0:T(8,128)(2,1)S(1)} fusion(f32[512,1024]{1,0:T(8,128)S(1)} %fusion.13, bf16[512,2048]{1,0:T(8,128)(2,1)S(1)} %bitcast.153, bf16[1,2048,1024]{2,1,0:T(8,128)(2,1)S(1)} %copy-done.17), kind=kOutput, calls=%fused_computation.42 | convolution fusion | flops 2150629376 | bytes 9437184 | tf_op jit(solution)/shard_map/dot_general | solution.py:15
  104.1 3.7 %fusion.19 = bf16[32,16,2048]{2,1,0:T(8,128)(2,1)} fusion(bf16[32,16,1024]{2,1,0:T(8,128)(2,1)S(1)} %bitcast.167, bf16[1,1024,2048]{2,1,0:T(8,128)(2,1)S(1)} %copy-done.16), kind=kOutput, calls=%fused_computation.25 | convolution fusion | flops 2148532224 | bytes 7340032 | tf_op jit(solution)/shard_map/dot_general | solution.py:17
  107.8 15.2 %all-to-all-done.3 = bf16[32,8,2048]{2,1,0:T(8,128)(2,1)S(1)} async-done(((bf16[32,8,2048]{2,1,0:T(8,128)(2,1)}), bf16[32,8,2048]{2,1,0:T(8,128)(2,1)S(1)}, u32[]{:S(2)}, u32[]{:S(2)}) %all-to-all-start.3) | async-done | bytes 1048608 | tf_op jit(solution)/shard_map/all_to_all | solution.py:105
  123.0 3.5 %all-to-all-start.4 = ((bf16[32,16,2048]{2,1,0:T(8,128)(2,1)}), bf16[32,16,2048]{2,1,0:T(8,128)(2,1)S(1)}, u32[]{:S(2)}, u32[]{:S(2)}) async-start(bf16[32,16,2048]{2,1,0:T(8,128)(2,1)} %fusion.19), calls=%async_computation.4 | async-start | bytes 4194304 | tf_op jit(solution)/shard_map/all_to_all | solution.py:129
  126.9 4.5 %fusion.11 = f32[256,1024]{1,0:T(8,128)} fusion(bf16[1,2048,1024]{2,1,0:T(8,128)(2,1)} %param.29, bf16[32,8,2048]{2,1,0:T(8,128)(2,1)S(1)} %all-to-all-done.3, f32[2048]{0:T(1024)S(1)} %copy-done.12, f32[32,8]{1,0:T(8,128)S(1)} %add_rsqrt_fusion), kind=kOutput, calls=%fused_computation.16 | convolution fusion | flops 1075838976 | bytes 6300672 | tf_op jit(solution)/shard_map/dot_general | solution.py:14
  131.3 7.2 %fusion.22 = bf16[32,8,2048]{2,1,0:T(8,128)(2,1)} fusion(bf16[1,1024,2048]{2,1,0:T(8,128)(2,1)} %param.31, bf16[1,2048,1024]{2,1,0:T(8,128)(2,1)} %param.30, f32[256,1024]{1,0:T(8,128)} %fusion.11, bf16[32,8,2048]{2,1,0:T(8,128)(2,1)S(1)} %all-to-all-done.3, f32[2048]{0:T(1024)S(1)} %copy-done.12, f32[32,8]{1,0:T(8,128)S(1)} %add_rsqrt_fusion), kind=kOutput, calls=%fused_computation.29 | convolution fusion | flops 2151677952 | bytes 11543552 | tf_op jit(solution)/shard_map/dot_general | solution.py:17
  138.5 37.0 %all-to-all-done.4 = bf16[32,16,2048]{2,1,0:T(8,128)(2,1)S(1)} async-done(((bf16[32,16,2048]{2,1,0:T(8,128)(2,1)}), bf16[32,16,2048]{2,1,0:T(8,128)(2,1)S(1)}, u32[]{:S(2)}, u32[]{:S(2)}) %all-to-all-start.4) | async-done | bytes 2097184 | tf_op jit(solution)/shard_map/all_to_all | solution.py:129
  175.5 4.0 %all-to-all-start.5 = ((bf16[32,8,2048]{2,1,0:T(8,128)(2,1)}), bf16[32,8,2048]{2,1,0:T(8,128)(2,1)S(1)}, u32[]{:S(2)}, u32[]{:S(2)}) async-start(bf16[32,8,2048]{2,1,0:T(8,128)(2,1)} %fusion.22), calls=%async_computation.5 | async-start | bytes 2097152 | tf_op jit(solution)/shard_map/all_to_all | solution.py:129
  181.6 24.1 %all-to-all-done.5 = bf16[32,8,2048]{2,1,0:T(8,128)(2,1)S(1)} async-done(((bf16[32,8,2048]{2,1,0:T(8,128)(2,1)}), bf16[32,8,2048]{2,1,0:T(8,128)(2,1)S(1)}, u32[]{:S(2)}, u32[]{:S(2)}) %all-to-all-start.5) | async-done | bytes 1048608 | tf_op jit(solution)/shard_map/all_to_all | solution.py:129
  (113 shorter events, 18.8 us)
Async XLA Ops:
  0.6 77.8 %copy-start = (bf16[64,2048]{1,0:T(8,128)(2,1)S(1)}, bf16[64,2048]{1,0:T(8,128)(2,1)}, u32[]{:S(2)}) copy-start(bf16[64,2048]{1,0:T(8,128)(2,1)} %param.24) | copy-start | bytes 786436
  5.4 7.3 %copy-start.9 = (bf16[1,32,2048]{2,1,0:T(8,128)(2,1)S(1)}, bf16[1,32,2048]{2,1,0:T(8,128)(2,1)}, u32[]{:S(2)}) copy-start(bf16[1,32,2048]{2,1,0:T(8,128)(2,1)} %param.17) | copy-start | bytes 393220
  5.4 7.4 %copy-start.10 = (bf16[1,32,2048]{2,1,0:T(8,128)(2,1)S(1)}, bf16[1,32,2048]{2,1,0:T(8,128)(2,1)}, u32[]{:S(2)}) copy-start(bf16[1,32,2048]{2,1,0:T(8,128)(2,1)} %param.16) | copy-start | bytes 393220
  5.4 56.2 %all-to-all-start = ((bf16[32,16,2048]{2,1,0:T(8,128)(2,1)}), bf16[32,16,2048]{2,1,0:T(8,128)(2,1)S(1)}, u32[]{:S(2)}, u32[]{:S(2)}) async-start(bf16[32,16,2048]{2,1,0:T(8,128)(2,1)} %bitcast.145), calls=%async_computation | async-start | bytes 4194304 | tf_op jit(solution)/shard_map/all_to_all | solution.py:105
  18.7 5.6 %copy-start.18 = (s32[1,32]{1,0:T(1,128)S(1)}, s32[1,32]{1,0:T(1,128)}, u32[]{:S(2)}) copy-start(s32[1,32]{1,0:T(1,128)} %param.21) | copy-start | bytes 388
  18.7 5.6 %copy-start.15 = (s32[1,4]{1,0:T(1,128)S(1)}, s32[1,4]{1,0:T(1,128)}, u32[]{:S(2)}) copy-start(s32[1,4]{1,0:T(1,128)} %param.22) | copy-start | bytes 52
  24.4 4.9 %copy-start.1 = (bf16[128,8,16,128]{3,2,1,0:T(8,128)(2,1)S(1)}, bf16[128,8,16,128]{3,2,1,0:T(8,128)(2,1)}, u32[]{:S(2)}) copy-start(bf16[128,8,16,128]{3,2,1,0:T(8,128)(2,1)} %copy.59) | copy-start | bytes 12582916
  29.3 2.5 %copy-start.4 = (f32[16,4,256,32]{2,3,1,0:T(8,128)}, f32[16,4,256,32]{2,3,1,0:T(8,128)S(1)}, u32[]{:S(2)}) copy-start(f32[16,4,256,32]{2,3,1,0:T(8,128)S(1)} %get-tuple-element.26) | copy-start | bytes 6291460
  32.1 4.6 %copy-start.11 = (s32[65,8]{0,1:T(8,128)S(1)}, s32[65,8]{0,1:T(8,128)}, u32[]{:S(2)}) copy-start(s32[65,8]{0,1:T(8,128)} %param.27) | copy-start | bytes 6244
  33.3 4.8 %copy-start.6 = (f32[32,2048]{1,0:T(8,128)S(1)}, f32[32,2048]{1,0:T(8,128)}, u32[]{:S(2)}) copy-start(f32[32,2048]{1,0:T(8,128)} %reshape.340) | copy-start | bytes 786436
  62.6 15.1 %all-to-all-start.1 = ((f32[32,1,2112]{2,1,0:T(1,128)}), f32[32,1,2112]{2,1,0:T(1,128)S(1)}, u32[]{:S(2)}, u32[]{:S(2)}) async-start(f32[32,1,2112]{2,1,0:T(1,128)} %copy.48), calls=%async_computation.1 | async-start | bytes 557056 | tf_op jit(solution)/shard_map/all_to_all | solution.py:64
  67.4 16.7 %copy-start.12 = (f32[2048]{0:T(1024)S(1)}, f32[2048]{0:T(1024)}, u32[]{:S(2)}) copy-start(f32[2048]{0:T(1024)} %param.26) | copy-start | bytes 24580
  81.3 11.0 %all-to-all-start.2 = ((bf16[32,2,1024]{2,1,0:T(2,128)(2,1)}), bf16[32,2,1024]{2,1,0:T(2,128)(2,1)S(1)}, u32[]{:S(2)}, u32[]{:S(2)}) async-start(bf16[32,2,1024]{2,1,0:T(2,128)(2,1)} %reshape.377), calls=%async_computation.2 | async-start | bytes 262144 | tf_op jit(solution)/shard_map/all_to_all | solution.py:82
  84.1 8.6 %copy-start.13 = (bf16[1,1,2048]{2,1,0:T(2,128)(2,1)S(1)}, bf16[1,1,2048]{2,1,0:T(2,128)(2,1)}, u32[]{:S(2)}) copy-start(bf16[1,1,2048]{2,1,0:T(2,128)(2,1)} %param.23) | copy-start | bytes 12292
  84.1 8.6 %copy-start.2 = (bf16[64,2048]{1,0:T(8,128)(2,1)S(1)}, bf16[64,2048]{1,0:T(8,128)(2,1)}, u32[]{:S(2)}) copy-start(bf16[64,2048]{1,0:T(8,128)(2,1)} %param.25) | copy-start | bytes 786436
  86.0 10.8 %copy-start.5 = (bf16[32,16,2048]{2,1,0:T(8,128)(2,1)S(1)}, bf16[32,16,2048]{2,1,0:T(8,128)(2,1)}, u32[]{:S(2)}) copy-start(bf16[32,16,2048]{2,1,0:T(8,128)(2,1)} %fusion.2) | copy-start | bytes 6291460
  94.2 28.9 %all-to-all-start.3 = ((bf16[32,8,2048]{2,1,0:T(8,128)(2,1)}), bf16[32,8,2048]{2,1,0:T(8,128)(2,1)S(1)}, u32[]{:S(2)}, u32[]{:S(2)}) async-start(bf16[32,8,2048]{2,1,0:T(8,128)(2,1)} %fusion.25), calls=%async_computation.3 | async-start | bytes 2097152 | tf_op jit(solution)/shard_map/all_to_all | solution.py:105
  96.8 4.7 %copy-start.17 = (bf16[1,2048,1024]{2,1,0:T(8,128)(2,1)S(1)}, bf16[1,2048,1024]{2,1,0:T(8,128)(2,1)}, u32[]{:S(2)}) copy-start(bf16[1,2048,1024]{2,1,0:T(8,128)(2,1)} %param.30) | copy-start | bytes 12582916
  101.5 2.6 %copy-start.16 = (bf16[1,1024,2048]{2,1,0:T(8,128)(2,1)S(1)}, bf16[1,1024,2048]{2,1,0:T(8,128)(2,1)}, u32[]{:S(2)}) copy-start(bf16[1,1024,2048]{2,1,0:T(8,128)(2,1)} %param.31) | copy-start | bytes 12582916
  123.0 52.4 %all-to-all-start.4 = ((bf16[32,16,2048]{2,1,0:T(8,128)(2,1)}), bf16[32,16,2048]{2,1,0:T(8,128)(2,1)S(1)}, u32[]{:S(2)}, u32[]{:S(2)}) async-start(bf16[32,16,2048]{2,1,0:T(8,128)(2,1)} %fusion.19), calls=%async_computation.4 | async-start | bytes 4194304 | tf_op jit(solution)/shard_map/all_to_all | solution.py:129
  138.5 41.1 %copy-start.14 = (f32[65,8]{0,1:T(8,128)S(1)}, f32[65,8]{0,1:T(8,128)}, u32[]{:S(2)}) copy-start(f32[65,8]{0,1:T(8,128)} %param.28) | copy-start | bytes 6244
  175.5 30.3 %all-to-all-start.5 = ((bf16[32,8,2048]{2,1,0:T(8,128)(2,1)}), bf16[32,8,2048]{2,1,0:T(8,128)(2,1)S(1)}, u32[]{:S(2)}, u32[]{:S(2)}) async-start(bf16[32,8,2048]{2,1,0:T(8,128)(2,1)} %fusion.22), calls=%async_computation.5 | async-start | bytes 2097152 | tf_op jit(solution)/shard_map/all_to_all | solution.py:129
  205.9 1.2 copy-start.7
  206.0 1.2 copy-start.8
  (1 other events, 1.0 us)

commit v10 on v9

--- a/solution.py
+++ b/solution.py
@@ -105,6 +105,20 @@
     return lax.all_to_all(outgoing, "tensor", split_axis=0, concat_axis=0, tiled=True)
 
 
+def dispatch_two(early_rows, early_slots, late_rows, late_slots, slot_count):
+    def picked(rows, slot_index):
+        slots = jnp.arange(slot_count, dtype=jnp.int32)
+        select = jnp.any(
+            slot_index.reshape(rows.shape[0], -1)[None, :, :] == slots[:, None, None], axis=2
+        ).astype(jnp.bfloat16)
+        return jnp.dot(select, rows, preferred_element_type=jnp.float32)
+
+    outgoing = (picked(early_rows, early_slots) + picked(late_rows, late_slots)).astype(jnp.bfloat16)
+    tensor_count = lax.axis_size("tensor")
+    outgoing = outgoing.reshape(tensor_count, slot_count // tensor_count, early_rows.shape[1])
+    return lax.all_to_all(outgoing, "tensor", split_axis=0, concat_axis=0, tiled=True)
+
+
 def experts_on(received, experts, norm_gain):
     block = lax.all_gather(received, "dp", axis=0, tiled=True)
     _, normed = rms_normed(block.reshape(-1, block.shape[-1]), norm_gain)
@@ -190,8 +204,9 @@
             decode_routes * late + overflow[decode_routes] + decode_rank,
         ]
     )
-    second_in = dispatch(
-        jnp.concatenate([prefill_states, decode_hidden], axis=0), late_slot, tensor_count * late
+    second_in = dispatch_two(
+        prefill_states, late_slot[:prefill_count * top_count],
+        decode_hidden, late_slot[prefill_count * top_count:], tensor_count * late,
     )
     first_done, second_in = lax.optimization_barrier((first_done, second_in))
     first_back = give_back(first_done)

time: 210 us -> 210 us (level)
  waiting for transfers between devices: 116 us -> 120 us
  matrix products: 37.2 us -> 34.8 us
    all_to_all x0 -> x1, waiting for transfers between devices: none -> 15.2 us  [dispatch_two(): lax.all_to_all(outgoing, 'tensor', split_axis=0, concat_axis=0, tiled=True)]
    all_to_all x2 -> x1, waiting for transfers between devices: 38.6 us -> 27.4 us  [dispatch(): lax.all_to_all(outgoing, 'tensor', split_axis=0, concat_axis=0, tiled=True)]
    all_to_all x2 -> x1, starting transfers between devices: 9.94 us -> 7.3 us  [dispatch(): lax.all_to_all(outgoing, 'tensor', split_axis=0, concat_axis=0, tiled=True)]
    all_to_all x0 -> x1, starting transfers between devices: none -> 2.64 us  [dispatch_two(): lax.all_to_all(outgoing, 'tensor', split_axis=0, concat_axis=0, tiled=True)]
    dot_general x1, matrix products: 4.83 us -> 2.48 us  [attention_partials(): jnp.einsum('rhd,gjhd->grhj', query_heads, key_table, preferred_element_ty...]
    dot_general x2 -> x1, matrix products: 4.58 us -> 3.04 us  [dispatch(): jnp.dot(select, normed, preferred_element_type=jnp.float32)]
  transfers between devices with their start and end apart: 6 -> 6, of which waited for: 6 -> 6; matrix products, arithmetic and copies ran while one was open for 25% -> 23% of each run, Pallas kernels for 0% -> 0%
where the time goes in v10:
time: 210 us; the launch traced here: 209 us
  waiting for transfers between devices  120 us (57%)
  matrix products  34.8 us (17%)
  starting transfers between devices  24.3 us (12%)
  local copies, waits for them, and re-layouts  19.1 us (9%)
  other arithmetic  9.69 us (5%)
    all_to_all x2, waiting for transfers between devices, give_back(): lax.all_to_all(lax.psum_scatter(done, 'dp', scatter_dimension=0, tiled=Tr...  61.1 us
    all_to_all x1, waiting for transfers between devices, dispatch(): lax.all_to_all(outgoing, 'tensor', split_axis=0, concat_axis=0, tiled=True)  27.4 us
    all_to_all x1, waiting for transfers between devices, dispatch_two(): lax.all_to_all(outgoing, 'tensor', split_axis=0, concat_axis=0, tiled=True)  15.2 us
    unnamed x47, local copies, waits for them, and re-layouts  11.9 us
    dot_general x2, matrix products, expert_mlp(): return jnp.dot(active, down_w, preferred_element_type=jnp.float32)  10.9 us
    all_to_all x1, waiting for transfers between devices, attention_finish(): received = lax.all_to_all(payload, 'tensor', 0, 0, tiled=True)  10.5 us
    dot_general x2, matrix products, expert_mlp(): gate = jnp.dot(flat_rows, gate_w, preferred_element_type=jnp.float32)  9.13 us
    all_to_all x2, starting transfers between devices, give_back(): lax.all_to_all(lax.psum_scatter(done, 'dp', scatter_dimension=0, tiled=Tr...  7.55 us
  transfers between devices with their start and end apart: 6, of which 6 were waited for; matrix products, arithmetic and copies ran while one was open for 23% of the time, Pallas kernels for 0%

profile of v10, /device:TPU:0, one launch (start us, length us, event | category | flops | bytes accessed | tf_op | source)
XLA Modules:
  0.0 209.5 jit_solution(16524615493869493725)
XLA Ops:
  2.3 3.0 %convolution_convert_fusion = bf16[512,2048]{1,0:T(8,128)(2,1)} fusion(pred[512,64]{0,1:T(8,128)(4,1)S(1)} %fusion.59, bf16[64,2048]{1,0:T(8,128)(2,1)} %param.25), kind=kOutput, calls=%fused_computation.26 | convolution fusion | flops 135266304 | bytes 2392064 | tf_op jit(solution)/shard_map/dot_general | solution.py:102
  5.4 7.3 %all-to-all-start = ((bf16[32,16,2048]{2,1,0:T(8,128)(2,1)}), bf16[32,16,2048]{2,1,0:T(8,128)(2,1)S(1)}, u32[]{:S(2)}, u32[]{:S(2)}) async-start(bf16[32,16,2048]{2,1,0:T(8,128)(2,1)} %bitcast.154), calls=%async_computation | async-start | bytes 4194304 | tf_op jit(solution)/shard_map/all_to_all | solution.py:105
  12.8 5.6 %copy.57 = bf16[128,8,16,128]{3,2,1,0:T(8,128)(2,1)} copy(bf16[128,8,16,128]{3,1,2,0:T(8,128)(2,1)} %bitcast.155) | data formatting | bytes 8388608
  18.6 3.7 %copy.60 = bf16[128,8,16,128]{3,2,1,0:T(8,128)(2,1)S(1)} copy(bf16[128,8,16,128]{3,1,2,0:T(8,128)(2,1)} %bitcast.156) | data formatting | bytes 8388608
  22.6 2.5 %fusion.31 = (f32[32,16]{0,1:T(8,128)S(1)}, f32[16,4,256,32]{2,3,1,0:T(8,128)S(1)}) fusion(pred[4,32,256]{2,1,0:T(8,128)(4,1)S(1)} %broadcast_and_fusion, bf16[32,16,128,1]{2,1,0,3:T(8,128)(2,1)S(1)} %bitcast.170, bf16[4,256,16,128]{3,2,1,0:T(8,128)(2,1)S(1)} %bitcast.157), kind=kOutput, calls=%fused_computation.40 | convolution fusion | flops 135790080 | bytes 6457344 | tf_op jit(solution)/shard_map/rhd,gjhd->grhj/dot_general | solution.py:35
  25.1 2.5 %fusion.47 = f32[32,16,128]{2,0,1:T(8,128)S(1)} fusion(bf16[4,256,16,128]{3,2,1,0:T(8,128)(2,1)S(1)} %bitcast.158, f32[16,4,256,32]{2,3,1,0:T(8,128)S(1)} %get-tuple-element.26, f32[32,16]{0,1:T(8,128)S(1)} %get-tuple-element.22, pred[4,32,256]{2,1,0:T(8,128)(4,1)S(1)} %broadcast_and_fusion), kind=kOutput, calls=%fused_computation.51 | convolution fusion | flops 136314880 | bytes 6588416 | tf_op jit(solution)/shard_map/grhj,gjhd->rhd/dot_general | solution.py:48
  29.1 2.2 %fusion.36 = f32[32,16]{0,1:T(8,128)S(1)} fusion(f32[16,4,256,32]{2,3,1,0:T(8,128)} %copy-done.5, f32[32,16]{0,1:T(8,128)S(1)} %get-tuple-element.22, pred[4,32,256]{2,1,0:T(8,128)(4,1)S(1)} %broadcast_and_fusion), kind=kLoop, calls=%fused_computation.44 | loop fusion | flops 2096640 | bytes 2134016 | tf_op jit(solution)/shard_map/reduce_sum | solution.py:47
  34.2 27.4 %all-to-all-done = bf16[32,16,2048]{2,1,0:T(8,128)(2,1)S(1)} async-done(((bf16[32,16,2048]{2,1,0:T(8,128)(2,1)}), bf16[32,16,2048]{2,1,0:T(8,128)(2,1)S(1)}, u32[]{:S(2)}, u32[]{:S(2)}) %all-to-all-start) | async-done | bytes 2097184 | tf_op jit(solution)/shard_map/all_to_all | solution.py:105
  62.6 4.0 %all-to-all-start.1 = ((f32[32,1,2112]{2,1,0:T(1,128)}), f32[32,1,2112]{2,1,0:T(1,128)S(1)}, u32[]{:S(2)}, u32[]{:S(2)}) async-start(f32[32,1,2112]{2,1,0:T(1,128)} %copy.49), calls=%async_computation.1 | async-start | bytes 557056 | tf_op jit(solution)/shard_map/all_to_all | solution.py:64
  67.2 10.5 %all-to-all-done.1 = f32[32,1,2112]{2,1,0:T(1,128)S(1)} async-done(((f32[32,1,2112]{2,1,0:T(1,128)}), f32[32,1,2112]{2,1,0:T(1,128)S(1)}, u32[]{:S(2)}, u32[]{:S(2)}) %all-to-all-start.1) | async-done | bytes 270368 | tf_op jit(solution)/shard_map/all_to_all | solution.py:64
  81.2 2.8 %all-to-all-start.2 = ((bf16[32,2,1024]{2,1,0:T(2,128)(2,1)}), bf16[32,2,1024]{2,1,0:T(2,128)(2,1)S(1)}, u32[]{:S(2)}, u32[]{:S(2)}) async-start(bf16[32,2,1024]{2,1,0:T(2,128)(2,1)} %reshape.434), calls=%async_computation.2 | async-start | bytes 262144 | tf_op jit(solution)/shard_map/all_to_all | solution.py:82
  84.0 1.9 fusion.2
  85.9 6.3 %all-to-all-done.2 = bf16[32,2,1024]{2,1,0:T(2,128)(2,1)S(1)} async-done(((bf16[32,2,1024]{2,1,0:T(2,128)(2,1)}), bf16[32,2,1024]{2,1,0:T(2,128)(2,1)S(1)}, u32[]{:S(2)}, u32[]{:S(2)}) %all-to-all-start.2) | async-done | bytes 131104 | tf_op jit(solution)/shard_map/all_to_all | solution.py:82
  94.1 2.6 %all-to-all-start.3 = ((bf16[32,8,2048]{2,1,0:T(8,128)(2,1)}), bf16[32,8,2048]{2,1,0:T(8,128)(2,1)S(1)}, u32[]{:S(2)}, u32[]{:S(2)}) async-start(bf16[32,8,2048]{2,1,0:T(8,128)(2,1)} %fusion.26), calls=%async_computation.3 | async-start | bytes 2097152 | tf_op jit(solution)/shard_map/all_to_all | solution.py:119
  96.7 4.7 %fusion.13 = f32[512,1024]{1,0:T(8,128)S(1)} fusion(bf16[512,2048]{1,0:T(8,128)(2,1)S(1)} %bitcast.161, bf16[1,2048,1024]{2,1,0:T(8,128)(2,1)} %param.29), kind=kOutput, calls=%fused_computation.18 | convolution fusion | flops 2147483648 | bytes 8388608 | tf_op jit(solution)/shard_map/dot_general | solution.py:14
  101.4 2.5 %multiply_convert_fusion = bf16[512,1024]{1,0:T(8,128)(2,1)S(1)} fusion(f32[512,1024]{1,0:T(8,128)S(1)} %fusion.13, bf16[512,2048]{1,0:T(8,128)(2,1)S(1)} %bitcast.162, bf16[1,2048,1024]{2,1,0:T(8,128)(2,1)S(1)} %copy-done.17), kind=kOutput, calls=%fused_computation.43 | convolution fusion | flops 2150629376 | bytes 9437184 | tf_op jit(solution)/shard_map/dot_general | solution.py:15
  104.0 3.7 %fusion.19 = bf16[32,16,2048]{2,1,0:T(8,128)(2,1)} fusion(bf16[32,16,1024]{2,1,0:T(8,128)(2,1)S(1)} %bitcast.177, bf16[1,1024,2048]{2,1,0:T(8,128)(2,1)S(1)} %copy-done.16), kind=kOutput, calls=%fused_computation.25 | convolution fusion | flops 2148532224 | bytes 7340032 | tf_op jit(solution)/shard_map/dot_general | solution.py:17
  107.7 15.2 %all-to-all-done.3 = bf16[32,8,2048]{2,1,0:T(8,128)(2,1)S(1)} async-done(((bf16[32,8,2048]{2,1,0:T(8,128)(2,1)}), bf16[32,8,2048]{2,1,0:T(8,128)(2,1)S(1)}, u32[]{:S(2)}, u32[]{:S(2)}) %all-to-all-start.3) | async-done | bytes 1048608 | tf_op jit(solution)/shard_map/all_to_all | solution.py:119
  122.9 3.5 %all-to-all-start.4 = ((bf16[32,16,2048]{2,1,0:T(8,128)(2,1)}), bf16[32,16,2048]{2,1,0:T(8,128)(2,1)S(1)}, u32[]{:S(2)}, u32[]{:S(2)}) async-start(bf16[32,16,2048]{2,1,0:T(8,128)(2,1)} %fusion.19), calls=%async_computation.4 | async-start | bytes 4194304 | tf_op jit(solution)/shard_map/all_to_all | solution.py:143
  126.8 4.5 %fusion.11 = f32[256,1024]{1,0:T(8,128)} fusion(bf16[1,2048,1024]{2,1,0:T(8,128)(2,1)} %param.29, bf16[32,8,2048]{2,1,0:T(8,128)(2,1)S(1)} %all-to-all-done.3, f32[2048]{0:T(1024)S(1)} %copy-done.13, f32[32,8]{1,0:T(8,128)S(1)} %add_rsqrt_fusion), kind=kOutput, calls=%fused_computation.16 | convolution fusion | flops 1075838976 | bytes 6300672 | tf_op jit(solution)/shard_map/dot_general | solution.py:14
  131.2 7.2 %fusion.23 = bf16[32,8,2048]{2,1,0:T(8,128)(2,1)} fusion(bf16[1,1024,2048]{2,1,0:T(8,128)(2,1)} %param.31, bf16[1,2048,1024]{2,1,0:T(8,128)(2,1)} %param.30, f32[256,1024]{1,0:T(8,128)} %fusion.11, bf16[32,8,2048]{2,1,0:T(8,128)(2,1)S(1)} %all-to-all-done.3, f32[2048]{0:T(1024)S(1)} %copy-done.13, f32[32,8]{1,0:T(8,128)S(1)} %add_rsqrt_fusion), kind=kOutput, calls=%fused_computation.31 | convolution fusion | flops 2151677952 | bytes 11543552 | tf_op jit(solution)/shard_map/dot_general | solution.py:17
  138.4 37.0 %all-to-all-done.4 = bf16[32,16,2048]{2,1,0:T(8,128)(2,1)S(1)} async-done(((bf16[32,16,2048]{2,1,0:T(8,128)(2,1)}), bf16[32,16,2048]{2,1,0:T(8,128)(2,1)S(1)}, u32[]{:S(2)}, u32[]{:S(2)}) %all-to-all-start.4) | async-done | bytes 2097184 | tf_op jit(solution)/shard_map/all_to_all | solution.py:143
  175.4 4.0 %all-to-all-start.5 = ((bf16[32,8,2048]{2,1,0:T(8,128)(2,1)}), bf16[32,8,2048]{2,1,0:T(8,128)(2,1)S(1)}, u32[]{:S(2)}, u32[]{:S(2)}) async-start(bf16[32,8,2048]{2,1,0:T(8,128)(2,1)} %fusion.23), calls=%async_computation.5 | async-start | bytes 2097152 | tf_op jit(solution)/shard_map/all_to_all | solution.py:143
  181.5 24.1 %all-to-all-done.5 = bf16[32,8,2048]{2,1,0:T(8,128)(2,1)S(1)} async-done(((bf16[32,8,2048]{2,1,0:T(8,128)(2,1)}), bf16[32,8,2048]{2,1,0:T(8,128)(2,1)S(1)}, u32[]{:S(2)}, u32[]{:S(2)}) %all-to-all-start.5) | async-done | bytes 1048608 | tf_op jit(solution)/shard_map/all_to_all | solution.py:143
  (115 shorter events, 19.6 us)
Async XLA Ops:
  0.6 77.7 %copy-start = (bf16[64,2048]{1,0:T(8,128)(2,1)S(1)}, bf16[64,2048]{1,0:T(8,128)(2,1)}, u32[]{:S(2)}) copy-start(bf16[64,2048]{1,0:T(8,128)(2,1)} %param.24) | copy-start | bytes 786436
  5.4 7.3 %copy-start.10 = (bf16[1,32,2048]{2,1,0:T(8,128)(2,1)S(1)}, bf16[1,32,2048]{2,1,0:T(8,128)(2,1)}, u32[]{:S(2)}) copy-start(bf16[1,32,2048]{2,1,0:T(8,128)(2,1)} %param.16) | copy-start | bytes 393220
  5.4 56.2 %all-to-all-start = ((bf16[32,16,2048]{2,1,0:T(8,128)(2,1)}), bf16[32,16,2048]{2,1,0:T(8,128)(2,1)S(1)}, u32[]{:S(2)}, u32[]{:S(2)}) async-start(bf16[32,16,2048]{2,1,0:T(8,128)(2,1)} %bitcast.154), calls=%async_computation | async-start | bytes 4194304 | tf_op jit(solution)/shard_map/all_to_all | solution.py:105
  12.7 5.6 %copy-start.9 = (bf16[1,32,2048]{2,1,0:T(8,128)(2,1)S(1)}, bf16[1,32,2048]{2,1,0:T(8,128)(2,1)}, u32[]{:S(2)}) copy-start(bf16[1,32,2048]{2,1,0:T(8,128)(2,1)} %param.17) | copy-start | bytes 393220
  18.6 3.8 %copy-start.18 = (s32[1,32]{1,0:T(1,128)S(1)}, s32[1,32]{1,0:T(1,128)}, u32[]{:S(2)}) copy-start(s32[1,32]{1,0:T(1,128)} %param.21) | copy-start | bytes 388
  18.6 3.8 %copy-start.15 = (s32[1,4]{1,0:T(1,128)S(1)}, s32[1,4]{1,0:T(1,128)}, u32[]{:S(2)}) copy-start(s32[1,4]{1,0:T(1,128)} %param.22) | copy-start | bytes 52
  18.6 4.0 %copy-start.1 = (bf16[128,8,16,128]{3,2,1,0:T(8,128)(2,1)S(1)}, bf16[128,8,16,128]{3,2,1,0:T(8,128)(2,1)}, u32[]{:S(2)}) copy-start(bf16[128,8,16,128]{3,2,1,0:T(8,128)(2,1)} %copy.57) | copy-start | bytes 12582916
  25.1 2.5 %copy-start.5 = (f32[16,4,256,32]{2,3,1,0:T(8,128)}, f32[16,4,256,32]{2,3,1,0:T(8,128)S(1)}, u32[]{:S(2)}) copy-start(f32[16,4,256,32]{2,3,1,0:T(8,128)S(1)} %get-tuple-element.26) | copy-start | bytes 6291460
  27.9 4.6 %copy-start.11 = (bf16[1,1,2048]{2,1,0:T(2,128)(2,1)S(1)}, bf16[1,1,2048]{2,1,0:T(2,128)(2,1)}, u32[]{:S(2)}) copy-start(bf16[1,1,2048]{2,1,0:T(2,128)(2,1)} %param.23) | copy-start | bytes 12292
  27.9 4.7 %copy-start.12 = (s32[65,8]{0,1:T(8,128)S(1)}, s32[65,8]{0,1:T(8,128)}, u32[]{:S(2)}) copy-start(s32[65,8]{0,1:T(8,128)} %param.27) | copy-start | bytes 6244
  29.1 4.4 %copy-start.6 = (f32[32,2048]{1,0:T(8,128)S(1)}, f32[32,2048]{1,0:T(8,128)}, u32[]{:S(2)}) copy-start(f32[32,2048]{1,0:T(8,128)} %reshape.396) | copy-start | bytes 786436
  62.6 15.1 %all-to-all-start.1 = ((f32[32,1,2112]{2,1,0:T(1,128)}), f32[32,1,2112]{2,1,0:T(1,128)S(1)}, u32[]{:S(2)}, u32[]{:S(2)}) async-start(f32[32,1,2112]{2,1,0:T(1,128)} %copy.49), calls=%async_computation.1 | async-start | bytes 557056 | tf_op jit(solution)/shard_map/all_to_all | solution.py:64
  67.1 16.9 %copy-start.13 = (f32[2048]{0:T(1024)S(1)}, f32[2048]{0:T(1024)}, u32[]{:S(2)}) copy-start(f32[2048]{0:T(1024)} %param.26) | copy-start | bytes 24580
  81.2 11.0 %all-to-all-start.2 = ((bf16[32,2,1024]{2,1,0:T(2,128)(2,1)}), bf16[32,2,1024]{2,1,0:T(2,128)(2,1)S(1)}, u32[]{:S(2)}, u32[]{:S(2)}) async-start(bf16[32,2,1024]{2,1,0:T(2,128)(2,1)} %reshape.434), calls=%async_computation.2 | async-start | bytes 262144 | tf_op jit(solution)/shard_map/all_to_all | solution.py:82
  84.0 8.6 %copy-start.2 = (bf16[64,2048]{1,0:T(8,128)(2,1)S(1)}, bf16[64,2048]{1,0:T(8,128)(2,1)}, u32[]{:S(2)}) copy-start(bf16[64,2048]{1,0:T(8,128)(2,1)} %param.25) | copy-start | bytes 786436
  85.9 10.8 %copy-start.4 = (bf16[32,16,2048]{2,1,0:T(8,128)(2,1)S(1)}, bf16[32,16,2048]{2,1,0:T(8,128)(2,1)}, u32[]{:S(2)}) copy-start(bf16[32,16,2048]{2,1,0:T(8,128)(2,1)} %fusion.2) | copy-start | bytes 6291460
  94.1 28.9 %all-to-all-start.3 = ((bf16[32,8,2048]{2,1,0:T(8,128)(2,1)}), bf16[32,8,2048]{2,1,0:T(8,128)(2,1)S(1)}, u32[]{:S(2)}, u32[]{:S(2)}) async-start(bf16[32,8,2048]{2,1,0:T(8,128)(2,1)} %fusion.26), calls=%async_computation.3 | async-start | bytes 2097152 | tf_op jit(solution)/shard_map/all_to_all | solution.py:119
  96.7 4.7 %copy-start.17 = (bf16[1,2048,1024]{2,1,0:T(8,128)(2,1)S(1)}, bf16[1,2048,1024]{2,1,0:T(8,128)(2,1)}, u32[]{:S(2)}) copy-start(bf16[1,2048,1024]{2,1,0:T(8,128)(2,1)} %param.30) | copy-start | bytes 12582916
  101.4 2.6 %copy-start.16 = (bf16[1,1024,2048]{2,1,0:T(8,128)(2,1)S(1)}, bf16[1,1024,2048]{2,1,0:T(8,128)(2,1)}, u32[]{:S(2)}) copy-start(bf16[1,1024,2048]{2,1,0:T(8,128)(2,1)} %param.31) | copy-start | bytes 12582916
  122.9 52.4 %all-to-all-start.4 = ((bf16[32,16,2048]{2,1,0:T(8,128)(2,1)}), bf16[32,16,2048]{2,1,0:T(8,128)(2,1)S(1)}, u32[]{:S(2)}, u32[]{:S(2)}) async-start(bf16[32,16,2048]{2,1,0:T(8,128)(2,1)} %fusion.19), calls=%async_computation.4 | async-start | bytes 4194304 | tf_op jit(solution)/shard_map/all_to_all | solution.py:143
  138.4 41.1 %copy-start.14 = (f32[65,8]{0,1:T(8,128)S(1)}, f32[65,8]{0,1:T(8,128)}, u32[]{:S(2)}) copy-start(f32[65,8]{0,1:T(8,128)} %param.28) | copy-start | bytes 6244
  175.4 30.3 %all-to-all-start.5 = ((bf16[32,8,2048]{2,1,0:T(8,128)(2,1)}), bf16[32,8,2048]{2,1,0:T(8,128)(2,1)S(1)}, u32[]{:S(2)}, u32[]{:S(2)}) async-start(bf16[32,8,2048]{2,1,0:T(8,128)(2,1)} %fusion.23), calls=%async_computation.5 | async-start | bytes 2097152 | tf_op jit(solution)/shard_map/all_to_all | solution.py:143
  205.6 0.9 copy-start.8
  206.6 0.9 copy-start.3
  (1 other events, 0.9 us)

commit v11 on v9

--- a/solution.py
+++ b/solution.py
@@ -159,7 +159,7 @@
     row_count, top_count = routes.shape
     decode_count = row_count - prefill_count
     capacity = max(8, (row_count * top_count * 3 // (2 * tensor_count) + 7) // 8 * 8)
-    early = max(8, capacity * 2 // 3 // 8 * 8)
+    early = max(8, capacity // 3 // 8 * 8)
     late = max(capacity - early, decode_count)
     stride = early + late
     experts = (w_gate[0], w_up[0], w_down[0])

time: 210 us -> 213 us (1.014)
  local copies, waits for them, and re-layouts: 20.4 us -> 25.8 us
  matrix products: 37.2 us -> 34.8 us
    dot_general x1, matrix products: 4.83 us -> 2.48 us  [attention_partials(): jnp.einsum('rhd,gjhd->grhj', query_heads, key_table, preferred_element_ty...]
    unnamed x47 -> x55, local copies, waits for them, and re-layouts: 13.2 us -> 12.3 us
  transfers between devices with their start and end apart: 6 -> 6, of which waited for: 6 -> 6; matrix products, arithmetic and copies ran while one was open for 25% -> 24% of each run, Pallas kernels for 0% -> 0%
where the time goes in v11:
time: 213 us
  waiting for transfers between devices  118 us (55%)
  matrix products  34.8 us (16%)
  local copies, waits for them, and re-layouts  25.8 us (12%)
  starting transfers between devices  24.9 us (12%)
  other arithmetic  7.85 us (4%)
    all_to_all x2, waiting for transfers between devices, give_back(): lax.all_to_all(lax.psum_scatter(done, 'dp', scatter_dimension=0, tiled=Tr...  62 us
    all_to_all x2, waiting for transfers between devices, dispatch(): lax.all_to_all(outgoing, 'tensor', split_axis=0, concat_axis=0, tiled=True)  38.3 us
    unnamed x55, local copies, waits for them, and re-layouts  12.3 us
    dot_general x2, matrix products, expert_mlp(): return jnp.dot(active, down_w, preferred_element_type=jnp.float32)  10.9 us
    all_to_all x2, starting transfers between devices, dispatch(): lax.all_to_all(outgoing, 'tensor', split_axis=0, concat_axis=0, tiled=True)  10.2 us
    all_to_all x1, waiting for transfers between devices, attention_finish(): received = lax.all_to_all(payload, 'tensor', 0, 0, tiled=True)  10.1 us
    dot_general x2, matrix products, expert_mlp(): gate = jnp.dot(flat_rows, gate_w, preferred_element_type=jnp.float32)  9.14 us
    all_to_all x1, waiting for transfers between devices, attention_finish(): lax.all_to_all(partial.astype(jnp.bfloat16).reshape(tensor_count, per_dev...  7.54 us
  transfers between devices with their start and end apart: 6, of which 6 were waited for; matrix products, arithmetic and copies ran while one was open for 24% of the time, Pallas kernels for 0%

profile of v11, /device:TPU:0, one launch (start us, length us, event | category | flops | bytes accessed | tf_op | source)
XLA Modules:
  0.0 212.6 jit_solution(12856216938906485802)
XLA Ops:
  3.1 2.4 %fusion.25 = bf16[32,8,2048]{2,1,0:T(8,128)(2,1)} fusion(pred[256,64]{0,1:T(8,128)(4,1)S(1)} %fusion.69, bf16[64,2048]{1,0:T(8,128)(2,1)} %param.25), kind=kOutput, calls=%fused_computation.31 | convolution fusion | flops 67633152 | bytes 1327104 | tf_op jit(solution)/shard_map/dot_general | solution.py:102
  5.5 7.3 %all-to-all-start = ((bf16[32,8,2048]{2,1,0:T(8,128)(2,1)}), bf16[32,8,2048]{2,1,0:T(8,128)(2,1)S(1)}, u32[]{:S(2)}, u32[]{:S(2)}) async-start(bf16[32,8,2048]{2,1,0:T(8,128)(2,1)} %fusion.25), calls=%async_computation | async-start | bytes 2097152 | tf_op jit(solution)/shard_map/all_to_all | solution.py:105
  12.9 5.6 %copy.56 = bf16[128,8,16,128]{3,2,1,0:T(8,128)(2,1)} copy(bf16[128,8,16,128]{3,1,2,0:T(8,128)(2,1)} %bitcast.146) | data formatting | bytes 8388608
  18.8 3.7 %copy.59 = bf16[128,8,16,128]{3,2,1,0:T(8,128)(2,1)S(1)} copy(bf16[128,8,16,128]{3,1,2,0:T(8,128)(2,1)} %bitcast.147) | data formatting | bytes 8388608
  22.7 2.5 %fusion.30 = (f32[32,16]{0,1:T(8,128)S(1)}, f32[16,4,256,32]{2,3,1,0:T(8,128)S(1)}) fusion(pred[4,32,256]{2,1,0:T(8,128)(4,1)S(1)} %broadcast_and_fusion, bf16[32,16,128,1]{2,1,0,3:T(8,128)(2,1)S(1)} %bitcast.161, bf16[4,256,16,128]{3,2,1,0:T(8,128)(2,1)S(1)} %bitcast.148), kind=kOutput, calls=%fused_computation.39 | convolution fusion | flops 135790080 | bytes 6457344 | tf_op jit(solution)/shard_map/rhd,gjhd->grhj/dot_general | solution.py:35
  25.2 2.4 %fusion.46 = f32[32,16,128]{2,0,1:T(8,128)S(1)} fusion(bf16[4,256,16,128]{3,2,1,0:T(8,128)(2,1)S(1)} %bitcast.149, f32[16,4,256,32]{2,3,1,0:T(8,128)S(1)} %get-tuple-element.26, f32[32,16]{0,1:T(8,128)S(1)} %get-tuple-element.20, pred[4,32,256]{2,1,0:T(8,128)(4,1)S(1)} %broadcast_and_fusion), kind=kOutput, calls=%fused_computation.50 | convolution fusion | flops 136314880 | bytes 6588416 | tf_op jit(solution)/shard_map/grhj,gjhd->rhd/dot_general | solution.py:48
  30.4 2.2 %copy.47 = f32[32,32,64]{2,1,0:T(8,128)} copy(f32[32,32,64]{2,0,1:T(8,128)} %bitcast.154) | data formatting | bytes 524288 | tf_op jit(solution)/shard_map/transpose | solution.py:54
  32.6 2.0 reshape.340
  40.0 4.5 %all-to-all-start.1 = ((f32[32,1,2112]{2,1,0:T(1,128)}), f32[32,1,2112]{2,1,0:T(1,128)S(1)}, u32[]{:S(2)}, u32[]{:S(2)}) async-start(f32[32,1,2112]{2,1,0:T(1,128)} %copy.48), calls=%async_computation.1 | async-start | bytes 557056 | tf_op jit(solution)/shard_map/all_to_all | solution.py:64
  45.5 10.1 %all-to-all-done.1 = f32[32,1,2112]{2,1,0:T(1,128)S(1)} async-done(((f32[32,1,2112]{2,1,0:T(1,128)}), f32[32,1,2112]{2,1,0:T(1,128)S(1)}, u32[]{:S(2)}, u32[]{:S(2)}) %all-to-all-start.1) | async-done | bytes 270368 | tf_op jit(solution)/shard_map/all_to_all | solution.py:64
  59.2 2.8 %all-to-all-start.2 = ((bf16[32,2,1024]{2,1,0:T(2,128)(2,1)}), bf16[32,2,1024]{2,1,0:T(2,128)(2,1)S(1)}, u32[]{:S(2)}, u32[]{:S(2)}) async-start(bf16[32,2,1024]{2,1,0:T(2,128)(2,1)} %reshape.377), calls=%async_computation.2 | async-start | bytes 262144 | tf_op jit(solution)/shard_map/all_to_all | solution.py:82
  62.5 7.5 %all-to-all-done.2 = bf16[32,2,1024]{2,1,0:T(2,128)(2,1)S(1)} async-done(((bf16[32,2,1024]{2,1,0:T(2,128)(2,1)}), bf16[32,2,1024]{2,1,0:T(2,128)(2,1)S(1)}, u32[]{:S(2)}, u32[]{:S(2)}) %all-to-all-start.2) | async-done | bytes 131104 | tf_op jit(solution)/shard_map/all_to_all | solution.py:82
  70.4 2.1 convolution_convert_fusion
  72.5 2.9 %all-to-all-start.3 = ((bf16[32,16,2048]{2,1,0:T(8,128)(2,1)}), bf16[32,16,2048]{2,1,0:T(8,128)(2,1)S(1)}, u32[]{:S(2)}, u32[]{:S(2)}) async-start(bf16[32,16,2048]{2,1,0:T(8,128)(2,1)} %bitcast.145), calls=%async_computation.3 | async-start | bytes 4194304 | tf_op jit(solution)/shard_map/all_to_all | solution.py:105
  75.7 4.5 %fusion.13 = f32[256,1024]{1,0:T(8,128)} fusion(bf16[1,2048,1024]{2,1,0:T(8,128)(2,1)} %param.29, bf16[32,8,2048]{2,1,0:T(8,128)(2,1)S(1)} %all-to-all-done, f32[2048]{0:T(1024)S(1)} %copy-done.14, f32[32,8]{1,0:T(8,128)S(1)} %add_rsqrt_fusion.1), kind=kOutput, calls=%fused_computation.18 | convolution fusion | flops 1075838976 | bytes 6300672 | tf_op jit(solution)/shard_map/dot_general | solution.py:14
  80.2 7.2 %fusion.22 = bf16[32,8,2048]{2,1,0:T(8,128)(2,1)} fusion(bf16[1,1024,2048]{2,1,0:T(8,128)(2,1)} %param.31, bf16[1,2048,1024]{2,1,0:T(8,128)(2,1)} %param.30, f32[256,1024]{1,0:T(8,128)} %fusion.13, bf16[32,8,2048]{2,1,0:T(8,128)(2,1)S(1)} %all-to-all-done, f32[2048]{0:T(1024)S(1)} %copy-done.14, f32[32,8]{1,0:T(8,128)S(1)} %add_rsqrt_fusion.1), kind=kOutput, calls=%fused_computation.29 | convolution fusion | flops 2151677952 | bytes 11543552 | tf_op jit(solution)/shard_map/dot_general | solution.py:17
  87.4 37.0 %all-to-all-done.3 = bf16[32,16,2048]{2,1,0:T(8,128)(2,1)S(1)} async-done(((bf16[32,16,2048]{2,1,0:T(8,128)(2,1)}), bf16[32,16,2048]{2,1,0:T(8,128)(2,1)S(1)}, u32[]{:S(2)}, u32[]{:S(2)}) %all-to-all-start.3) | async-done | bytes 2097184 | tf_op jit(solution)/shard_map/all_to_all | solution.py:105
  126.7 3.9 %all-to-all-start.4 = ((bf16[32,8,2048]{2,1,0:T(8,128)(2,1)}), bf16[32,8,2048]{2,1,0:T(8,128)(2,1)S(1)}, u32[]{:S(2)}, u32[]{:S(2)}) async-start(bf16[32,8,2048]{2,1,0:T(8,128)(2,1)} %fusion.22), calls=%async_computation.4 | async-start | bytes 2097152 | tf_op jit(solution)/shard_map/all_to_all | solution.py:129
  130.7 4.7 %fusion.11 = f32[512,1024]{1,0:T(8,128)S(1)} fusion(bf16[512,2048]{1,0:T(8,128)(2,1)S(1)} %bitcast.152, bf16[1,2048,1024]{2,1,0:T(8,128)(2,1)} %param.29), kind=kOutput, calls=%fused_computation.16 | convolution fusion | flops 2147483648 | bytes 8388608 | tf_op jit(solution)/shard_map/dot_general | solution.py:14
  135.3 2.5 %multiply_convert_fusion = bf16[512,1024]{1,0:T(8,128)(2,1)S(1)} fusion(f32[512,1024]{1,0:T(8,128)S(1)} %fusion.11, bf16[512,2048]{1,0:T(8,128)(2,1)S(1)} %bitcast.153, bf16[1,2048,1024]{2,1,0:T(8,128)(2,1)S(1)} %copy-done.20), kind=kOutput, calls=%fused_computation.42 | convolution fusion | flops 2150629376 | bytes 9437184 | tf_op jit(solution)/shard_map/dot_general | solution.py:15
  137.9 3.7 %fusion.19 = bf16[32,16,2048]{2,1,0:T(8,128)(2,1)} fusion(bf16[32,16,1024]{2,1,0:T(8,128)(2,1)S(1)} %bitcast.167, bf16[1,1024,2048]{2,1,0:T(8,128)(2,1)S(1)} %copy-done.21), kind=kOutput, calls=%fused_computation.25 | convolution fusion | flops 2148532224 | bytes 7340032 | tf_op jit(solution)/shard_map/dot_general | solution.py:17
  141.6 15.2 %all-to-all-done.4 = bf16[32,8,2048]{2,1,0:T(8,128)(2,1)S(1)} async-done(((bf16[32,8,2048]{2,1,0:T(8,128)(2,1)}), bf16[32,8,2048]{2,1,0:T(8,128)(2,1)S(1)}, u32[]{:S(2)}, u32[]{:S(2)}) %all-to-all-start.4) | async-done | bytes 1048608 | tf_op jit(solution)/shard_map/all_to_all | solution.py:129
  156.9 3.6 %all-to-all-start.5 = ((bf16[32,16,2048]{2,1,0:T(8,128)(2,1)}), bf16[32,16,2048]{2,1,0:T(8,128)(2,1)S(1)}, u32[]{:S(2)}, u32[]{:S(2)}) async-start(bf16[32,16,2048]{2,1,0:T(8,128)(2,1)} %fusion.19), calls=%async_computation.5 | async-start | bytes 4194304 | tf_op jit(solution)/shard_map/all_to_all | solution.py:129
  162.6 46.8 %all-to-all-done.5 = bf16[32,16,2048]{2,1,0:T(8,128)(2,1)S(1)} async-done(((bf16[32,16,2048]{2,1,0:T(8,128)(2,1)}), bf16[32,16,2048]{2,1,0:T(8,128)(2,1)S(1)}, u32[]{:S(2)}, u32[]{:S(2)}) %all-to-all-start.5) | async-done | bytes 2097184 | tf_op jit(solution)/shard_map/all_to_all | solution.py:129
  (121 shorter events, 24.4 us)
Async XLA Ops:
  0.6 55.7 %copy-start = (bf16[64,2048]{1,0:T(8,128)(2,1)S(1)}, bf16[64,2048]{1,0:T(8,128)(2,1)}, u32[]{:S(2)}) copy-start(bf16[64,2048]{1,0:T(8,128)(2,1)} %param.24) | copy-start | bytes 786436
  0.6 12.2 %copy-start.22 = (s32[1,32]{1,0:T(1,128)S(1)}, s32[1,32]{1,0:T(1,128)}, u32[]{:S(2)}) copy-start(s32[1,32]{1,0:T(1,128)} %param.21) | copy-start | bytes 388
  0.7 12.2 %copy-start.10 = (bf16[1,32,2048]{2,1,0:T(8,128)(2,1)S(1)}, bf16[1,32,2048]{2,1,0:T(8,128)(2,1)}, u32[]{:S(2)}) copy-start(bf16[1,32,2048]{2,1,0:T(8,128)(2,1)} %param.16) | copy-start | bytes 393220
  5.5 33.5 %all-to-all-start = ((bf16[32,8,2048]{2,1,0:T(8,128)(2,1)}), bf16[32,8,2048]{2,1,0:T(8,128)(2,1)S(1)}, u32[]{:S(2)}, u32[]{:S(2)}) async-start(bf16[32,8,2048]{2,1,0:T(8,128)(2,1)} %fusion.25), calls=%async_computation | async-start | bytes 2097152 | tf_op jit(solution)/shard_map/all_to_all | solution.py:105
  12.9 5.6 %copy-start.9 = (bf16[1,32,2048]{2,1,0:T(8,128)(2,1)S(1)}, bf16[1,32,2048]{2,1,0:T(8,128)(2,1)}, u32[]{:S(2)}) copy-start(bf16[1,32,2048]{2,1,0:T(8,128)(2,1)} %param.17) | copy-start | bytes 393220
  18.8 3.8 %copy-start.19 = (s32[1,4]{1,0:T(1,128)S(1)}, s32[1,4]{1,0:T(1,128)}, u32[]{:S(2)}) copy-start(s32[1,4]{1,0:T(1,128)} %param.22) | copy-start | bytes 52
  18.8 3.9 %copy-start.1 = (bf16[128,8,16,128]{3,2,1,0:T(8,128)(2,1)S(1)}, bf16[128,8,16,128]{3,2,1,0:T(8,128)(2,1)}, u32[]{:S(2)}) copy-start(bf16[128,8,16,128]{3,2,1,0:T(8,128)(2,1)} %copy.56) | copy-start | bytes 12582916
  22.7 2.5 %copy-start.7 = (pred[4,32,256]{2,1,0:T(8,128)(4,1)}, pred[4,32,256]{2,1,0:T(8,128)(4,1)S(1)}, u32[]{:S(2)}) copy-start(pred[4,32,256]{2,1,0:T(8,128)(4,1)S(1)} %broadcast_and_fusion) | copy-start | bytes 98308
  27.7 6.9 %copy-start.8 = (pred[4,32,256]{2,1,0:T(8,128)(4,1)S(1)}, pred[4,32,256]{2,1,0:T(8,128)(4,1)}, u32[]{:S(2)}) copy-start(pred[4,32,256]{2,1,0:T(8,128)(4,1)} %copy-done.7) | copy-start | bytes 98308
  32.6 4.8 %copy-start.13 = (s32[65,8]{0,1:T(8,128)S(1)}, s32[65,8]{0,1:T(8,128)}, u32[]{:S(2)}) copy-start(s32[65,8]{0,1:T(8,128)} %param.27) | copy-start | bytes 6244
  32.6 5.0 %copy-start.12 = (s32[512]{0:T(512)S(1)}, s32[512]{0:T(512)}, u32[]{:S(2)}) copy-start(s32[512]{0:T(512)} %copy-done.11) | copy-start | bytes 6148
  34.6 10.9 %copy-start.17 = (s32[512]{0:T(512)S(1)}, s32[512]{0:T(512)}, u32[]{:S(2)}) copy-start(s32[512]{0:T(512)} %copy-done.16) | copy-start | bytes 6148
  40.0 15.6 %all-to-all-start.1 = ((f32[32,1,2112]{2,1,0:T(1,128)}), f32[32,1,2112]{2,1,0:T(1,128)S(1)}, u32[]{:S(2)}, u32[]{:S(2)}) async-start(f32[32,1,2112]{2,1,0:T(1,128)} %copy.48), calls=%async_computation.1 | async-start | bytes 557056 | tf_op jit(solution)/shard_map/all_to_all | solution.py:64
  55.7 14.7 %copy-start.15 = (bf16[1,1,2048]{2,1,0:T(2,128)(2,1)S(1)}, bf16[1,1,2048]{2,1,0:T(2,128)(2,1)}, u32[]{:S(2)}) copy-start(bf16[1,1,2048]{2,1,0:T(2,128)(2,1)} %param.23) | copy-start | bytes 12292
  55.7 14.7 %copy-start.2 = (bf16[64,2048]{1,0:T(8,128)(2,1)S(1)}, bf16[64,2048]{1,0:T(8,128)(2,1)}, u32[]{:S(2)}) copy-start(bf16[64,2048]{1,0:T(8,128)(2,1)} %param.25) | copy-start | bytes 786436
  59.2 10.8 %all-to-all-start.2 = ((bf16[32,2,1024]{2,1,0:T(2,128)(2,1)}), bf16[32,2,1024]{2,1,0:T(2,128)(2,1)S(1)}, u32[]{:S(2)}, u32[]{:S(2)}) async-start(bf16[32,2,1024]{2,1,0:T(2,128)(2,1)} %reshape.377), calls=%async_computation.2 | async-start | bytes 262144 | tf_op jit(solution)/shard_map/all_to_all | solution.py:82
  72.5 3.2 %copy-start.14 = (f32[2048]{0:T(1024)S(1)}, f32[2048]{0:T(1024)}, u32[]{:S(2)}) copy-start(f32[2048]{0:T(1024)} %param.26) | copy-start | bytes 24580
  72.5 51.8 %all-to-all-start.3 = ((bf16[32,16,2048]{2,1,0:T(8,128)(2,1)}), bf16[32,16,2048]{2,1,0:T(8,128)(2,1)S(1)}, u32[]{:S(2)}, u32[]{:S(2)}) async-start(bf16[32,16,2048]{2,1,0:T(8,128)(2,1)} %bitcast.145), calls=%async_computation.3 | async-start | bytes 4194304 | tf_op jit(solution)/shard_map/all_to_all | solution.py:105
  126.7 3.9 %copy-start.4 = (bf16[32,16,2048]{2,1,0:T(8,128)(2,1)S(1)}, bf16[32,16,2048]{2,1,0:T(8,128)(2,1)}, u32[]{:S(2)}) copy-start(bf16[32,16,2048]{2,1,0:T(8,128)(2,1)} %fusion.2) | copy-start | bytes 6291460
  126.7 30.1 %all-to-all-start.4 = ((bf16[32,8,2048]{2,1,0:T(8,128)(2,1)}), bf16[32,8,2048]{2,1,0:T(8,128)(2,1)S(1)}, u32[]{:S(2)}, u32[]{:S(2)}) async-start(bf16[32,8,2048]{2,1,0:T(8,128)(2,1)} %fusion.22), calls=%async_computation.4 | async-start | bytes 2097152 | tf_op jit(solution)/shard_map/all_to_all | solution.py:129
  130.6 4.7 %copy-start.20 = (bf16[1,2048,1024]{2,1,0:T(8,128)(2,1)S(1)}, bf16[1,2048,1024]{2,1,0:T(8,128)(2,1)}, u32[]{:S(2)}) copy-start(bf16[1,2048,1024]{2,1,0:T(8,128)(2,1)} %param.30) | copy-start | bytes 12582916
  135.3 2.6 %copy-start.21 = (bf16[1,1024,2048]{2,1,0:T(8,128)(2,1)S(1)}, bf16[1,1024,2048]{2,1,0:T(8,128)(2,1)}, u32[]{:S(2)}) copy-start(bf16[1,1024,2048]{2,1,0:T(8,128)(2,1)} %param.31) | copy-start | bytes 12582916
  141.6 19.0 %copy-start.18 = (f32[65,8]{0,1:T(8,128)S(1)}, f32[65,8]{0,1:T(8,128)}, u32[]{:S(2)}) copy-start(f32[65,8]{0,1:T(8,128)} %param.28) | copy-start | bytes 6244
  156.9 52.5 %all-to-all-start.5 = ((bf16[32,16,2048]{2,1,0:T(8,128)(2,1)}), bf16[32,16,2048]{2,1,0:T(8,128)(2,1)S(1)}, u32[]{:S(2)}, u32[]{:S(2)}) async-start(bf16[32,16,2048]{2,1,0:T(8,128)(2,1)} %fusion.19), calls=%async_computation.5 | async-start | bytes 4194304 | tf_op jit(solution)/shard_map/all_to_all | solution.py:129
  (5 other events, 4.4 us)

commit v12 on v9

--- a/solution.py
+++ b/solution.py
@@ -80,10 +80,9 @@
     partial = jnp.dot(attended, out_weight, preferred_element_type=jnp.float32)
     per_device = requests // tensor_count
     gathered = lax.all_to_all(
-        partial.astype(jnp.bfloat16).reshape(tensor_count, per_device, model_width),
-        "tensor", 0, 0, tiled=True,
-    )
-    projected = jnp.sum(gathered.astype(jnp.float32), axis=0)
+        partial.reshape(tensor_count, per_device, model_width), "tensor", 0, 0, tiled=True
+    )
+    projected = jnp.sum(gathered, axis=0)
     return (decode_residual[0].astype(jnp.float32) + projected).astype(jnp.bfloat16)
 
 

time: 210 us -> 211 us (level)
  waiting for transfers between devices: 116 us -> 119 us
    all_to_all x1, waiting for transfers between devices: 6.3 us -> 8.67 us  [attention_finish(): lax.all_to_all(partial.reshape(tensor_count, per_device, model_width), 't...]
    unnamed x47 -> x45, local copies, waits for them, and re-layouts: 13.2 us -> 12.4 us
where the time goes in v12:
time: 211 us; the launch traced here: 210 us
  waiting for transfers between devices  119 us (56%)
  matrix products  37.2 us (18%)
  starting transfers between devices  24.3 us (12%)
  local copies, waits for them, and re-layouts  20.1 us (10%)
  other arithmetic  8.83 us (4%)
    all_to_all x2, waiting for transfers between devices, give_back(): lax.all_to_all(lax.psum_scatter(done, 'dp', scatter_dimension=0, tiled=Tr...  61.1 us
    all_to_all x2, waiting for transfers between devices, dispatch(): lax.all_to_all(outgoing, 'tensor', split_axis=0, concat_axis=0, tiled=True)  38.6 us
    unnamed x45, local copies, waits for them, and re-layouts  12.4 us
    dot_general x2, matrix products, expert_mlp(): return jnp.dot(active, down_w, preferred_element_type=jnp.float32)  10.9 us
    all_to_all x1, waiting for transfers between devices, attention_finish(): received = lax.all_to_all(payload, 'tensor', 0, 0, tiled=True)  10.1 us
    all_to_all x2, starting transfers between devices, dispatch(): lax.all_to_all(outgoing, 'tensor', split_axis=0, concat_axis=0, tiled=True)  9.94 us
    dot_general x2, matrix products, expert_mlp(): gate = jnp.dot(flat_rows, gate_w, preferred_element_type=jnp.float32)  9.13 us
    all_to_all x1, waiting for transfers between devices, attention_finish(): lax.all_to_all(partial.reshape(tensor_count, per_device, model_width), 't...  8.67 us
  transfers between devices with their start and end apart: 6, of which 6 were waited for; matrix products, arithmetic and copies ran while one was open for 25% of the time, Pallas kernels for 0%

profile of v12, /device:TPU:0, one launch (start us, length us, event | category | flops | bytes accessed | tf_op | source)
XLA Modules:
  0.0 210.1 jit_solution(13049354480865872800)
XLA Ops:
  2.3 3.1 %convolution_convert_fusion = bf16[512,2048]{1,0:T(8,128)(2,1)} fusion(pred[512,64]{0,1:T(8,128)(4,1)S(1)} %fusion.57, bf16[64,2048]{1,0:T(8,128)(2,1)} %param.25), kind=kOutput, calls=%fused_computation.26 | convolution fusion | flops 135266304 | bytes 2392064 | tf_op jit(solution)/shard_map/dot_general | solution.py:101
  5.4 7.3 %all-to-all-start = ((bf16[32,16,2048]{2,1,0:T(8,128)(2,1)}), bf16[32,16,2048]{2,1,0:T(8,128)(2,1)S(1)}, u32[]{:S(2)}, u32[]{:S(2)}) async-start(bf16[32,16,2048]{2,1,0:T(8,128)(2,1)} %bitcast.145), calls=%async_computation | async-start | bytes 4194304 | tf_op jit(solution)/shard_map/all_to_all | solution.py:104
  12.8 5.6 %copy.56 = bf16[128,8,16,128]{3,2,1,0:T(8,128)(2,1)} copy(bf16[128,8,16,128]{3,1,2,0:T(8,128)(2,1)} %bitcast.146) | data formatting | bytes 8388608
  18.7 5.6 %copy.59 = bf16[128,8,16,128]{3,2,1,0:T(8,128)(2,1)} copy(bf16[128,8,16,128]{3,1,2,0:T(8,128)(2,1)} %bitcast.147) | data formatting | bytes 8388608
  24.4 4.8 %fusion.29 = (f32[32,16]{0,1:T(8,128)S(1)}, f32[16,4,256,32]{2,3,1,0:T(8,128)S(1)}) fusion(pred[4,32,256]{2,1,0:T(8,128)(4,1)S(1)} %broadcast_and_fusion, bf16[32,16,128,1]{2,1,0,3:T(8,128)(2,1)S(1)} %bitcast.161, bf16[4,256,16,128]{3,2,1,0:T(8,128)(2,1)} %bitcast.149), kind=kOutput, calls=%fused_computation.38 | convolution fusion | flops 135790080 | bytes 6457344 | tf_op jit(solution)/shard_map/rhd,gjhd->grhj/dot_general | solution.py:35
  29.3 2.4 %fusion.45 = f32[32,16,128]{2,0,1:T(8,128)S(1)} fusion(bf16[4,256,16,128]{3,2,1,0:T(8,128)(2,1)S(1)} %bitcast.148, f32[16,4,256,32]{2,3,1,0:T(8,128)S(1)} %get-tuple-element.26, f32[32,16]{0,1:T(8,128)S(1)} %get-tuple-element.20, pred[4,32,256]{2,1,0:T(8,128)(4,1)S(1)} %broadcast_and_fusion), kind=kOutput, calls=%fused_computation.49 | convolution fusion | flops 136314880 | bytes 6588416 | tf_op jit(solution)/shard_map/grhj,gjhd->rhd/dot_general | solution.py:48
  33.3 2.2 %fusion.34 = f32[32,16]{0,1:T(8,128)S(1)} fusion(f32[16,4,256,32]{2,3,1,0:T(8,128)} %copy-done.4, f32[32,16]{0,1:T(8,128)S(1)} %get-tuple-element.20, pred[4,32,256]{2,1,0:T(8,128)(4,1)S(1)} %broadcast_and_fusion), kind=kLoop, calls=%fused_computation.42 | loop fusion | flops 2096640 | bytes 2134016 | tf_op jit(solution)/shard_map/reduce_sum | solution.py:47
  38.2 23.4 %all-to-all-done = bf16[32,16,2048]{2,1,0:T(8,128)(2,1)S(1)} async-done(((bf16[32,16,2048]{2,1,0:T(8,128)(2,1)}), bf16[32,16,2048]{2,1,0:T(8,128)(2,1)S(1)}, u32[]{:S(2)}, u32[]{:S(2)}) %all-to-all-start) | async-done | bytes 2097184 | tf_op jit(solution)/shard_map/all_to_all | solution.py:104
  62.6 4.2 %all-to-all-start.1 = ((f32[32,1,2112]{2,1,0:T(1,128)}), f32[32,1,2112]{2,1,0:T(1,128)S(1)}, u32[]{:S(2)}, u32[]{:S(2)}) async-start(f32[32,1,2112]{2,1,0:T(1,128)} %copy.48), calls=%async_computation.1 | async-start | bytes 557056 | tf_op jit(solution)/shard_map/all_to_all | solution.py:64
  67.6 10.1 %all-to-all-done.1 = f32[32,1,2112]{2,1,0:T(1,128)S(1)} async-done(((f32[32,1,2112]{2,1,0:T(1,128)}), f32[32,1,2112]{2,1,0:T(1,128)S(1)}, u32[]{:S(2)}, u32[]{:S(2)}) %all-to-all-start.1) | async-done | bytes 270368 | tf_op jit(solution)/shard_map/all_to_all | solution.py:64
  80.3 2.6 %all-to-all-start.2 = ((f32[32,1,2048]{2,1,0:T(1,128)}), f32[32,1,2048]{2,1,0:T(1,128)S(1)}, u32[]{:S(2)}, u32[]{:S(2)}) async-start(f32[32,1,2048]{2,1,0:T(1,128)} %copy.49), calls=%async_computation.2 | async-start | bytes 524288 | tf_op jit(solution)/shard_map/all_to_all | solution.py:82
  83.0 1.9 fusion.2
  84.9 8.7 %all-to-all-done.2 = f32[32,1,2048]{2,1,0:T(1,128)S(1)} async-done(((f32[32,1,2048]{2,1,0:T(1,128)}), f32[32,1,2048]{2,1,0:T(1,128)S(1)}, u32[]{:S(2)}, u32[]{:S(2)}) %all-to-all-start.2) | async-done | bytes 262176 | tf_op jit(solution)/shard_map/all_to_all | solution.py:82
  95.2 2.6 %all-to-all-start.3 = ((bf16[32,8,2048]{2,1,0:T(8,128)(2,1)}), bf16[32,8,2048]{2,1,0:T(8,128)(2,1)S(1)}, u32[]{:S(2)}, u32[]{:S(2)}) async-start(bf16[32,8,2048]{2,1,0:T(8,128)(2,1)} %fusion.25), calls=%async_computation.3 | async-start | bytes 2097152 | tf_op jit(solution)/shard_map/all_to_all | solution.py:104
  97.9 4.7 %fusion.13 = f32[512,1024]{1,0:T(8,128)S(1)} fusion(bf16[512,2048]{1,0:T(8,128)(2,1)S(1)} %bitcast.152, bf16[1,2048,1024]{2,1,0:T(8,128)(2,1)} %param.29), kind=kOutput, calls=%fused_computation.18 | convolution fusion | flops 2147483648 | bytes 8388608 | tf_op jit(solution)/shard_map/dot_general | solution.py:14
  102.6 2.5 %multiply_convert_fusion = bf16[512,1024]{1,0:T(8,128)(2,1)S(1)} fusion(f32[512,1024]{1,0:T(8,128)S(1)} %fusion.13, bf16[512,2048]{1,0:T(8,128)(2,1)S(1)} %bitcast.153, bf16[1,2048,1024]{2,1,0:T(8,128)(2,1)S(1)} %copy-done.17), kind=kOutput, calls=%fused_computation.41 | convolution fusion | flops 2150629376 | bytes 9437184 | tf_op jit(solution)/shard_map/dot_general | solution.py:15
  105.1 3.7 %fusion.19 = bf16[32,16,2048]{2,1,0:T(8,128)(2,1)} fusion(bf16[32,16,1024]{2,1,0:T(8,128)(2,1)S(1)} %bitcast.167, bf16[1,1024,2048]{2,1,0:T(8,128)(2,1)S(1)} %copy-done.16), kind=kOutput, calls=%fused_computation.25 | convolution fusion | flops 2148532224 | bytes 7340032 | tf_op jit(solution)/shard_map/dot_general | solution.py:17
  108.9 15.2 %all-to-all-done.3 = bf16[32,8,2048]{2,1,0:T(8,128)(2,1)S(1)} async-done(((bf16[32,8,2048]{2,1,0:T(8,128)(2,1)}), bf16[32,8,2048]{2,1,0:T(8,128)(2,1)S(1)}, u32[]{:S(2)}, u32[]{:S(2)}) %all-to-all-start.3) | async-done | bytes 1048608 | tf_op jit(solution)/shard_map/all_to_all | solution.py:104
  124.1 3.5 %all-to-all-start.4 = ((bf16[32,16,2048]{2,1,0:T(8,128)(2,1)}), bf16[32,16,2048]{2,1,0:T(8,128)(2,1)S(1)}, u32[]{:S(2)}, u32[]{:S(2)}) async-start(bf16[32,16,2048]{2,1,0:T(8,128)(2,1)} %fusion.19), calls=%async_computation.4 | async-start | bytes 4194304 | tf_op jit(solution)/shard_map/all_to_all | solution.py:128
  127.9 4.5 %fusion.11 = f32[256,1024]{1,0:T(8,128)} fusion(bf16[1,2048,1024]{2,1,0:T(8,128)(2,1)} %param.29, bf16[32,8,2048]{2,1,0:T(8,128)(2,1)S(1)} %all-to-all-done.3, f32[2048]{0:T(1024)S(1)} %copy-done.12, f32[32,8]{1,0:T(8,128)S(1)} %add_rsqrt_fusion), kind=kOutput, calls=%fused_computation.16 | convolution fusion | flops 1075838976 | bytes 6300672 | tf_op jit(solution)/shard_map/dot_general | solution.py:14
  132.4 7.2 %fusion.22 = bf16[32,8,2048]{2,1,0:T(8,128)(2,1)} fusion(bf16[1,1024,2048]{2,1,0:T(8,128)(2,1)} %param.31, bf16[1,2048,1024]{2,1,0:T(8,128)(2,1)} %param.30, f32[256,1024]{1,0:T(8,128)} %fusion.11, bf16[32,8,2048]{2,1,0:T(8,128)(2,1)S(1)} %all-to-all-done.3, f32[2048]{0:T(1024)S(1)} %copy-done.12, f32[32,8]{1,0:T(8,128)S(1)} %add_rsqrt_fusion), kind=kOutput, calls=%fused_computation.29 | convolution fusion | flops 2151677952 | bytes 11543552 | tf_op jit(solution)/shard_map/dot_general | solution.py:17
  139.6 37.0 %all-to-all-done.4 = bf16[32,16,2048]{2,1,0:T(8,128)(2,1)S(1)} async-done(((bf16[32,16,2048]{2,1,0:T(8,128)(2,1)}), bf16[32,16,2048]{2,1,0:T(8,128)(2,1)S(1)}, u32[]{:S(2)}, u32[]{:S(2)}) %all-to-all-start.4) | async-done | bytes 2097184 | tf_op jit(solution)/shard_map/all_to_all | solution.py:128
  176.5 4.0 %all-to-all-start.5 = ((bf16[32,8,2048]{2,1,0:T(8,128)(2,1)}), bf16[32,8,2048]{2,1,0:T(8,128)(2,1)S(1)}, u32[]{:S(2)}, u32[]{:S(2)}) async-start(bf16[32,8,2048]{2,1,0:T(8,128)(2,1)} %fusion.22), calls=%async_computation.5 | async-start | bytes 2097152 | tf_op jit(solution)/shard_map/all_to_all | solution.py:128
  182.7 24.1 %all-to-all-done.5 = bf16[32,8,2048]{2,1,0:T(8,128)(2,1)S(1)} async-done(((bf16[32,8,2048]{2,1,0:T(8,128)(2,1)}), bf16[32,8,2048]{2,1,0:T(8,128)(2,1)S(1)}, u32[]{:S(2)}, u32[]{:S(2)}) %all-to-all-start.5) | async-done | bytes 1048608 | tf_op jit(solution)/shard_map/all_to_all | solution.py:128
  (110 shorter events, 17.9 us)
Async XLA Ops:
  0.6 77.8 %copy-start = (bf16[64,2048]{1,0:T(8,128)(2,1)S(1)}, bf16[64,2048]{1,0:T(8,128)(2,1)}, u32[]{:S(2)}) copy-start(bf16[64,2048]{1,0:T(8,128)(2,1)} %param.24) | copy-start | bytes 786436
  5.4 7.3 %copy-start.9 = (bf16[1,32,2048]{2,1,0:T(8,128)(2,1)S(1)}, bf16[1,32,2048]{2,1,0:T(8,128)(2,1)}, u32[]{:S(2)}) copy-start(bf16[1,32,2048]{2,1,0:T(8,128)(2,1)} %param.17) | copy-start | bytes 393220
  5.4 7.4 %copy-start.10 = (bf16[1,32,2048]{2,1,0:T(8,128)(2,1)S(1)}, bf16[1,32,2048]{2,1,0:T(8,128)(2,1)}, u32[]{:S(2)}) copy-start(bf16[1,32,2048]{2,1,0:T(8,128)(2,1)} %param.16) | copy-start | bytes 393220
  5.4 56.2 %all-to-all-start = ((bf16[32,16,2048]{2,1,0:T(8,128)(2,1)}), bf16[32,16,2048]{2,1,0:T(8,128)(2,1)S(1)}, u32[]{:S(2)}, u32[]{:S(2)}) async-start(bf16[32,16,2048]{2,1,0:T(8,128)(2,1)} %bitcast.145), calls=%async_computation | async-start | bytes 4194304 | tf_op jit(solution)/shard_map/all_to_all | solution.py:104
  18.7 5.6 %copy-start.18 = (s32[1,32]{1,0:T(1,128)S(1)}, s32[1,32]{1,0:T(1,128)}, u32[]{:S(2)}) copy-start(s32[1,32]{1,0:T(1,128)} %param.21) | copy-start | bytes 388
  18.7 5.6 %copy-start.15 = (s32[1,4]{1,0:T(1,128)S(1)}, s32[1,4]{1,0:T(1,128)}, u32[]{:S(2)}) copy-start(s32[1,4]{1,0:T(1,128)} %param.22) | copy-start | bytes 52
  24.4 4.9 %copy-start.1 = (bf16[128,8,16,128]{3,2,1,0:T(8,128)(2,1)S(1)}, bf16[128,8,16,128]{3,2,1,0:T(8,128)(2,1)}, u32[]{:S(2)}) copy-start(bf16[128,8,16,128]{3,2,1,0:T(8,128)(2,1)} %copy.59) | copy-start | bytes 12582916
  29.3 2.5 %copy-start.4 = (f32[16,4,256,32]{2,3,1,0:T(8,128)}, f32[16,4,256,32]{2,3,1,0:T(8,128)S(1)}, u32[]{:S(2)}) copy-start(f32[16,4,256,32]{2,3,1,0:T(8,128)S(1)} %get-tuple-element.26) | copy-start | bytes 6291460
  32.1 4.6 %copy-start.11 = (s32[65,8]{0,1:T(8,128)S(1)}, s32[65,8]{0,1:T(8,128)}, u32[]{:S(2)}) copy-start(s32[65,8]{0,1:T(8,128)} %param.27) | copy-start | bytes 6244
  33.3 4.8 %copy-start.6 = (f32[32,2048]{1,0:T(8,128)S(1)}, f32[32,2048]{1,0:T(8,128)}, u32[]{:S(2)}) copy-start(f32[32,2048]{1,0:T(8,128)} %reshape.340) | copy-start | bytes 786436
  62.6 15.1 %all-to-all-start.1 = ((f32[32,1,2112]{2,1,0:T(1,128)}), f32[32,1,2112]{2,1,0:T(1,128)S(1)}, u32[]{:S(2)}, u32[]{:S(2)}) async-start(f32[32,1,2112]{2,1,0:T(1,128)} %copy.48), calls=%async_computation.1 | async-start | bytes 557056 | tf_op jit(solution)/shard_map/all_to_all | solution.py:64
  67.6 15.4 %copy-start.12 = (f32[2048]{0:T(1024)S(1)}, f32[2048]{0:T(1024)}, u32[]{:S(2)}) copy-start(f32[2048]{0:T(1024)} %param.26) | copy-start | bytes 24580
  80.3 13.2 %all-to-all-start.2 = ((f32[32,1,2048]{2,1,0:T(1,128)}), f32[32,1,2048]{2,1,0:T(1,128)S(1)}, u32[]{:S(2)}, u32[]{:S(2)}) async-start(f32[32,1,2048]{2,1,0:T(1,128)} %copy.49), calls=%async_computation.2 | async-start | bytes 524288 | tf_op jit(solution)/shard_map/all_to_all | solution.py:82
  82.9 10.8 %copy-start.13 = (bf16[1,1,2048]{2,1,0:T(2,128)(2,1)S(1)}, bf16[1,1,2048]{2,1,0:T(2,128)(2,1)}, u32[]{:S(2)}) copy-start(bf16[1,1,2048]{2,1,0:T(2,128)(2,1)} %param.23) | copy-start | bytes 12292
  83.0 10.8 %copy-start.2 = (bf16[64,2048]{1,0:T(8,128)(2,1)S(1)}, bf16[64,2048]{1,0:T(8,128)(2,1)}, u32[]{:S(2)}) copy-start(bf16[64,2048]{1,0:T(8,128)(2,1)} %param.25) | copy-start | bytes 786436
  84.9 13.0 %copy-start.5 = (bf16[32,16,2048]{2,1,0:T(8,128)(2,1)S(1)}, bf16[32,16,2048]{2,1,0:T(8,128)(2,1)}, u32[]{:S(2)}) copy-start(bf16[32,16,2048]{2,1,0:T(8,128)(2,1)} %fusion.2) | copy-start | bytes 6291460
  95.2 28.9 %all-to-all-start.3 = ((bf16[32,8,2048]{2,1,0:T(8,128)(2,1)}), bf16[32,8,2048]{2,1,0:T(8,128)(2,1)S(1)}, u32[]{:S(2)}, u32[]{:S(2)}) async-start(bf16[32,8,2048]{2,1,0:T(8,128)(2,1)} %fusion.25), calls=%async_computation.3 | async-start | bytes 2097152 | tf_op jit(solution)/shard_map/all_to_all | solution.py:104
  97.9 4.7 %copy-start.17 = (bf16[1,2048,1024]{2,1,0:T(8,128)(2,1)S(1)}, bf16[1,2048,1024]{2,1,0:T(8,128)(2,1)}, u32[]{:S(2)}) copy-start(bf16[1,2048,1024]{2,1,0:T(8,128)(2,1)} %param.30) | copy-start | bytes 12582916
  102.6 2.6 %copy-start.16 = (bf16[1,1024,2048]{2,1,0:T(8,128)(2,1)S(1)}, bf16[1,1024,2048]{2,1,0:T(8,128)(2,1)}, u32[]{:S(2)}) copy-start(bf16[1,1024,2048]{2,1,0:T(8,128)(2,1)} %param.31) | copy-start | bytes 12582916
  124.1 52.4 %all-to-all-start.4 = ((bf16[32,16,2048]{2,1,0:T(8,128)(2,1)}), bf16[32,16,2048]{2,1,0:T(8,128)(2,1)S(1)}, u32[]{:S(2)}, u32[]{:S(2)}) async-start(bf16[32,16,2048]{2,1,0:T(8,128)(2,1)} %fusion.19), calls=%async_computation.4 | async-start | bytes 4194304 | tf_op jit(solution)/shard_map/all_to_all | solution.py:128
  139.6 41.1 %copy-start.14 = (f32[65,8]{0,1:T(8,128)S(1)}, f32[65,8]{0,1:T(8,128)}, u32[]{:S(2)}) copy-start(f32[65,8]{0,1:T(8,128)} %param.28) | copy-start | bytes 6244
  176.5 30.3 %all-to-all-start.5 = ((bf16[32,8,2048]{2,1,0:T(8,128)(2,1)}), bf16[32,8,2048]{2,1,0:T(8,128)(2,1)S(1)}, u32[]{:S(2)}, u32[]{:S(2)}) async-start(bf16[32,8,2048]{2,1,0:T(8,128)(2,1)} %fusion.22), calls=%async_computation.5 | async-start | bytes 2097152 | tf_op jit(solution)/shard_map/all_to_all | solution.py:128
  207.2 1.2 copy-start.7
  207.2 1.2 copy-start.8
  (1 other events, 1.0 us)

commit v13 on v9

--- a/solution.py
+++ b/solution.py
@@ -77,13 +77,21 @@
     own_values = lax.dynamic_slice_in_dim(new_values[0], first_column, width, 1).astype(jnp.float32)
     summed_mix = jnp.sum(scale[:, :, None] * part_mix, axis=0) + own_prob[:, None] * own_values
     attended = (summed_mix / totals[:, None]).astype(jnp.bfloat16)
-    partial = jnp.dot(attended, out_weight, preferred_element_type=jnp.float32)
+    lanes = 128
+    partial = jnp.einsum(
+        "rc,ctl->rtl", attended, out_weight.reshape(width, model_width // lanes, lanes),
+        preferred_element_type=jnp.float32,
+    )
     per_device = requests // tensor_count
     gathered = lax.all_to_all(
-        partial.astype(jnp.bfloat16).reshape(tensor_count, per_device, model_width),
+        partial.astype(jnp.bfloat16).reshape(
+            tensor_count, per_device * (model_width // lanes), lanes
+        ),
         "tensor", 0, 0, tiled=True,
     )
-    projected = jnp.sum(gathered.astype(jnp.float32), axis=0)
+    projected = jnp.sum(
+        gathered.astype(jnp.float32).reshape(tensor_count, per_device, model_width), axis=0
+    )
     return (decode_residual[0].astype(jnp.float32) + projected).astype(jnp.bfloat16)
 
 

time: 210 us -> 208 us (level)
  waiting for transfers between devices: 116 us -> 120 us
  matrix products: 37.2 us -> 34 us
    all_to_all x2, waiting for transfers between devices: 38.6 us -> 42.5 us  [dispatch(): lax.all_to_all(outgoing, 'tensor', split_axis=0, concat_axis=0, tiled=True)]
    unnamed x47 -> x45, local copies, waits for them, and re-layouts: 13.2 us -> 10.6 us
    dot_general x1, matrix products: 4.83 us -> 2.48 us  [attention_partials(): jnp.einsum('rhd,gjhd->grhj', query_heads, key_table, preferred_element_ty...]
  transfers between devices with their start and end apart: 6 -> 6, of which waited for: 6 -> 6; matrix products, arithmetic and copies ran while one was open for 25% -> 24% of each run, Pallas kernels for 0% -> 0%
where the time goes in v13:
time: 208 us; the launch traced here: 207 us
  waiting for transfers between devices  120 us (58%)
  matrix products  34 us (16%)
  starting transfers between devices  24.3 us (12%)
  local copies, waits for them, and re-layouts  18.3 us (9%)
  other arithmetic  9.51 us (5%)
    all_to_all x2, waiting for transfers between devices, give_back(): lax.all_to_all(lax.psum_scatter(done, 'dp', scatter_dimension=0, tiled=Tr...  61.1 us
    all_to_all x2, waiting for transfers between devices, dispatch(): lax.all_to_all(outgoing, 'tensor', split_axis=0, concat_axis=0, tiled=True)  42.5 us
    dot_general x2, matrix products, expert_mlp(): return jnp.dot(active, down_w, preferred_element_type=jnp.float32)  10.9 us
    unnamed x45, local copies, waits for them, and re-layouts  10.6 us
    all_to_all x2, starting transfers between devices, dispatch(): lax.all_to_all(outgoing, 'tensor', split_axis=0, concat_axis=0, tiled=True)  9.94 us
    all_to_all x1, waiting for transfers between devices, attention_finish(): received = lax.all_to_all(payload, 'tensor', 0, 0, tiled=True)  9.74 us
    dot_general x2, matrix products, expert_mlp(): gate = jnp.dot(flat_rows, gate_w, preferred_element_type=jnp.float32)  9.14 us
    all_to_all x2, starting transfers between devices, give_back(): lax.all_to_all(lax.psum_scatter(done, 'dp', scatter_dimension=0, tiled=Tr...  7.55 us
  transfers between devices with their start and end apart: 6, of which 6 were waited for; matrix products, arithmetic and copies ran while one was open for 24% of the time, Pallas kernels for 0%

profile of v13, /device:TPU:0, one launch (start us, length us, event | category | flops | bytes accessed | tf_op | source)
XLA Modules:
  0.0 207.0 jit_solution(10619599892447681918)
XLA Ops:
  2.3 3.0 %convolution_convert_fusion = bf16[512,2048]{1,0:T(8,128)(2,1)} fusion(pred[512,64]{0,1:T(8,128)(4,1)S(1)} %fusion.57, bf16[64,2048]{1,0:T(8,128)(2,1)} %param.25), kind=kOutput, calls=%fused_computation.26 | convolution fusion | flops 135266304 | bytes 2392064 | tf_op jit(solution)/shard_map/dot_general | solution.py:110
  5.4 7.3 %all-to-all-start = ((bf16[32,16,2048]{2,1,0:T(8,128)(2,1)}), bf16[32,16,2048]{2,1,0:T(8,128)(2,1)S(1)}, u32[]{:S(2)}, u32[]{:S(2)}) async-start(bf16[32,16,2048]{2,1,0:T(8,128)(2,1)} %bitcast.144), calls=%async_computation | async-start | bytes 4194304 | tf_op jit(solution)/shard_map/all_to_all | solution.py:113
  12.7 5.6 %copy.61 = bf16[128,8,16,128]{3,2,1,0:T(8,128)(2,1)} copy(bf16[128,8,16,128]{3,1,2,0:T(8,128)(2,1)} %bitcast.145) | data formatting | bytes 8388608
  18.6 3.7 %copy.64 = bf16[128,8,16,128]{3,2,1,0:T(8,128)(2,1)S(1)} copy(bf16[128,8,16,128]{3,1,2,0:T(8,128)(2,1)} %bitcast.146) | data formatting | bytes 8388608
  22.6 2.5 %fusion.29 = (f32[32,16]{0,1:T(8,128)S(1)}, f32[16,4,256,32]{2,3,1,0:T(8,128)S(1)}) fusion(pred[4,32,256]{2,1,0:T(8,128)(4,1)S(1)} %broadcast_and_fusion, bf16[32,16,128,1]{2,1,0,3:T(8,128)(2,1)S(1)} %bitcast.160, bf16[4,256,16,128]{3,2,1,0:T(8,128)(2,1)S(1)} %bitcast.147), kind=kOutput, calls=%fused_computation.37 | convolution fusion | flops 135790080 | bytes 6457344 | tf_op jit(solution)/shard_map/rhd,gjhd->grhj/dot_general | solution.py:35
  25.1 2.5 %fusion.45 = f32[32,16,128]{2,0,1:T(8,128)S(1)} fusion(bf16[4,256,16,128]{3,2,1,0:T(8,128)(2,1)S(1)} %bitcast.148, f32[16,4,256,32]{2,3,1,0:T(8,128)S(1)} %get-tuple-element.26, f32[32,16]{0,1:T(8,128)S(1)} %get-tuple-element.20, pred[4,32,256]{2,1,0:T(8,128)(4,1)S(1)} %broadcast_and_fusion), kind=kOutput, calls=%fused_computation.48 | convolution fusion | flops 136314880 | bytes 6588416 | tf_op jit(solution)/shard_map/grhj,gjhd->rhd/dot_general | solution.py:48
  29.1 2.2 %fusion.34 = f32[32,16]{0,1:T(8,128)S(1)} fusion(f32[16,4,256,32]{2,3,1,0:T(8,128)} %copy-done.4, f32[32,16]{0,1:T(8,128)S(1)} %get-tuple-element.20, pred[4,32,256]{2,1,0:T(8,128)(4,1)S(1)} %broadcast_and_fusion), kind=kLoop, calls=%fused_computation.41 | loop fusion | flops 2096640 | bytes 2134016 | tf_op jit(solution)/shard_map/reduce_sum | solution.py:47
  34.3 27.3 %all-to-all-done = bf16[32,16,2048]{2,1,0:T(8,128)(2,1)S(1)} async-done(((bf16[32,16,2048]{2,1,0:T(8,128)(2,1)}), bf16[32,16,2048]{2,1,0:T(8,128)(2,1)S(1)}, u32[]{:S(2)}, u32[]{:S(2)}) %all-to-all-start) | async-done | bytes 2097184 | tf_op jit(solution)/shard_map/all_to_all | solution.py:113
  62.6 4.0 %all-to-all-start.1 = ((f32[32,1,2112]{2,1,0:T(1,128)}), f32[32,1,2112]{2,1,0:T(1,128)S(1)}, u32[]{:S(2)}, u32[]{:S(2)}) async-start(f32[32,1,2112]{2,1,0:T(1,128)} %copy.51), calls=%async_computation.1 | async-start | bytes 557056 | tf_op jit(solution)/shard_map/all_to_all | solution.py:64
  67.9 9.7 %all-to-all-done.1 = f32[32,1,2112]{2,1,0:T(1,128)S(1)} async-done(((f32[32,1,2112]{2,1,0:T(1,128)}), f32[32,1,2112]{2,1,0:T(1,128)S(1)}, u32[]{:S(2)}, u32[]{:S(2)}) %all-to-all-start.1) | async-done | bytes 270368 | tf_op jit(solution)/shard_map/all_to_all | solution.py:64
  79.6 2.8 %all-to-all-start.2 = ((bf16[32,16,128]{2,1,0:T(8,128)(2,1)}), bf16[32,16,128]{2,1,0:T(8,128)(2,1)S(1)}, u32[]{:S(2)}, u32[]{:S(2)}) async-start(bf16[32,16,128]{2,1,0:T(8,128)(2,1)} %copy.53), calls=%async_computation.2 | async-start | bytes 262144 | tf_op jit(solution)/shard_map/all_to_all | solution.py:86
  82.4 1.9 fusion.2
  84.3 6.3 %all-to-all-done.2 = bf16[32,16,128]{2,1,0:T(8,128)(2,1)S(1)} async-done(((bf16[32,16,128]{2,1,0:T(8,128)(2,1)}), bf16[32,16,128]{2,1,0:T(8,128)(2,1)S(1)}, u32[]{:S(2)}, u32[]{:S(2)}) %all-to-all-start.2) | async-done | bytes 131104 | tf_op jit(solution)/shard_map/all_to_all | solution.py:86
  92.1 2.6 %all-to-all-start.3 = ((bf16[32,8,2048]{2,1,0:T(8,128)(2,1)}), bf16[32,8,2048]{2,1,0:T(8,128)(2,1)S(1)}, u32[]{:S(2)}, u32[]{:S(2)}) async-start(bf16[32,8,2048]{2,1,0:T(8,128)(2,1)} %fusion.25), calls=%async_computation.3 | async-start | bytes 2097152 | tf_op jit(solution)/shard_map/all_to_all | solution.py:113
  94.8 4.7 %fusion.13 = f32[512,1024]{1,0:T(8,128)S(1)} fusion(bf16[512,2048]{1,0:T(8,128)(2,1)S(1)} %bitcast.151, bf16[1,2048,1024]{2,1,0:T(8,128)(2,1)} %param.29), kind=kOutput, calls=%fused_computation.18 | convolution fusion | flops 2147483648 | bytes 8388608 | tf_op jit(solution)/shard_map/dot_general | solution.py:14
  99.5 2.5 %multiply_convert_fusion = bf16[512,1024]{1,0:T(8,128)(2,1)S(1)} fusion(f32[512,1024]{1,0:T(8,128)S(1)} %fusion.13, bf16[512,2048]{1,0:T(8,128)(2,1)S(1)} %bitcast.152, bf16[1,2048,1024]{2,1,0:T(8,128)(2,1)S(1)} %copy-done.17), kind=kOutput, calls=%fused_computation.40 | convolution fusion | flops 2150629376 | bytes 9437184 | tf_op jit(solution)/shard_map/dot_general | solution.py:15
  102.0 3.7 %fusion.19 = bf16[32,16,2048]{2,1,0:T(8,128)(2,1)} fusion(bf16[32,16,1024]{2,1,0:T(8,128)(2,1)S(1)} %bitcast.166, bf16[1,1024,2048]{2,1,0:T(8,128)(2,1)S(1)} %copy-done.16), kind=kOutput, calls=%fused_computation.25 | convolution fusion | flops 2148532224 | bytes 7340032 | tf_op jit(solution)/shard_map/dot_general | solution.py:17
  105.8 15.2 %all-to-all-done.3 = bf16[32,8,2048]{2,1,0:T(8,128)(2,1)S(1)} async-done(((bf16[32,8,2048]{2,1,0:T(8,128)(2,1)}), bf16[32,8,2048]{2,1,0:T(8,128)(2,1)S(1)}, u32[]{:S(2)}, u32[]{:S(2)}) %all-to-all-start.3) | async-done | bytes 1048608 | tf_op jit(solution)/shard_map/all_to_all | solution.py:113
  121.0 3.5 %all-to-all-start.4 = ((bf16[32,16,2048]{2,1,0:T(8,128)(2,1)}), bf16[32,16,2048]{2,1,0:T(8,128)(2,1)S(1)}, u32[]{:S(2)}, u32[]{:S(2)}) async-start(bf16[32,16,2048]{2,1,0:T(8,128)(2,1)} %fusion.19), calls=%async_computation.4 | async-start | bytes 4194304 | tf_op jit(solution)/shard_map/all_to_all | solution.py:137
  124.8 4.5 %fusion.11 = f32[256,1024]{1,0:T(8,128)} fusion(bf16[1,2048,1024]{2,1,0:T(8,128)(2,1)} %param.29, bf16[32,8,2048]{2,1,0:T(8,128)(2,1)S(1)} %all-to-all-done.3, f32[2048]{0:T(1024)S(1)} %copy-done.12, f32[32,8]{1,0:T(8,128)S(1)} %add_rsqrt_fusion), kind=kOutput, calls=%fused_computation.16 | convolution fusion | flops 1075838976 | bytes 6300672 | tf_op jit(solution)/shard_map/dot_general | solution.py:14
  129.3 7.2 %fusion.22 = bf16[32,8,2048]{2,1,0:T(8,128)(2,1)} fusion(bf16[1,1024,2048]{2,1,0:T(8,128)(2,1)} %param.31, bf16[1,2048,1024]{2,1,0:T(8,128)(2,1)} %param.30, f32[256,1024]{1,0:T(8,128)} %fusion.11, bf16[32,8,2048]{2,1,0:T(8,128)(2,1)S(1)} %all-to-all-done.3, f32[2048]{0:T(1024)S(1)} %copy-done.12, f32[32,8]{1,0:T(8,128)S(1)} %add_rsqrt_fusion), kind=kOutput, calls=%fused_computation.29 | convolution fusion | flops 2151677952 | bytes 11543552 | tf_op jit(solution)/shard_map/dot_general | solution.py:17
  136.5 37.0 %all-to-all-done.4 = bf16[32,16,2048]{2,1,0:T(8,128)(2,1)S(1)} async-done(((bf16[32,16,2048]{2,1,0:T(8,128)(2,1)}), bf16[32,16,2048]{2,1,0:T(8,128)(2,1)S(1)}, u32[]{:S(2)}, u32[]{:S(2)}) %all-to-all-start.4) | async-done | bytes 2097184 | tf_op jit(solution)/shard_map/all_to_all | solution.py:137
  173.4 4.0 %all-to-all-start.5 = ((bf16[32,8,2048]{2,1,0:T(8,128)(2,1)}), bf16[32,8,2048]{2,1,0:T(8,128)(2,1)S(1)}, u32[]{:S(2)}, u32[]{:S(2)}) async-start(bf16[32,8,2048]{2,1,0:T(8,128)(2,1)} %fusion.22), calls=%async_computation.5 | async-start | bytes 2097152 | tf_op jit(solution)/shard_map/all_to_all | solution.py:137
  179.6 24.1 %all-to-all-done.5 = bf16[32,8,2048]{2,1,0:T(8,128)(2,1)S(1)} async-done(((bf16[32,8,2048]{2,1,0:T(8,128)(2,1)}), bf16[32,8,2048]{2,1,0:T(8,128)(2,1)S(1)}, u32[]{:S(2)}, u32[]{:S(2)}) %all-to-all-start.5) | async-done | bytes 1048608 | tf_op jit(solution)/shard_map/all_to_all | solution.py:137
  (116 shorter events, 17.9 us)
Async XLA Ops:
  0.6 78.1 %copy-start = (bf16[64,2048]{1,0:T(8,128)(2,1)S(1)}, bf16[64,2048]{1,0:T(8,128)(2,1)}, u32[]{:S(2)}) copy-start(bf16[64,2048]{1,0:T(8,128)(2,1)} %param.24) | copy-start | bytes 786436
  5.4 7.3 %copy-start.10 = (bf16[1,32,2048]{2,1,0:T(8,128)(2,1)S(1)}, bf16[1,32,2048]{2,1,0:T(8,128)(2,1)}, u32[]{:S(2)}) copy-start(bf16[1,32,2048]{2,1,0:T(8,128)(2,1)} %param.16) | copy-start | bytes 393220
  5.4 56.2 %all-to-all-start = ((bf16[32,16,2048]{2,1,0:T(8,128)(2,1)}), bf16[32,16,2048]{2,1,0:T(8,128)(2,1)S(1)}, u32[]{:S(2)}, u32[]{:S(2)}) async-start(bf16[32,16,2048]{2,1,0:T(8,128)(2,1)} %bitcast.144), calls=%async_computation | async-start | bytes 4194304 | tf_op jit(solution)/shard_map/all_to_all | solution.py:113
  12.7 5.6 %copy-start.9 = (bf16[1,32,2048]{2,1,0:T(8,128)(2,1)S(1)}, bf16[1,32,2048]{2,1,0:T(8,128)(2,1)}, u32[]{:S(2)}) copy-start(bf16[1,32,2048]{2,1,0:T(8,128)(2,1)} %param.17) | copy-start | bytes 393220
  18.6 3.8 %copy-start.18 = (s32[1,32]{1,0:T(1,128)S(1)}, s32[1,32]{1,0:T(1,128)}, u32[]{:S(2)}) copy-start(s32[1,32]{1,0:T(1,128)} %param.21) | copy-start | bytes 388
  18.6 3.8 %copy-start.15 = (s32[1,4]{1,0:T(1,128)S(1)}, s32[1,4]{1,0:T(1,128)}, u32[]{:S(2)}) copy-start(s32[1,4]{1,0:T(1,128)} %param.22) | copy-start | bytes 52
  18.6 4.0 %copy-start.1 = (bf16[128,8,16,128]{3,2,1,0:T(8,128)(2,1)S(1)}, bf16[128,8,16,128]{3,2,1,0:T(8,128)(2,1)}, u32[]{:S(2)}) copy-start(bf16[128,8,16,128]{3,2,1,0:T(8,128)(2,1)} %copy.61) | copy-start | bytes 12582916
  25.1 2.5 %copy-start.4 = (f32[16,4,256,32]{2,3,1,0:T(8,128)}, f32[16,4,256,32]{2,3,1,0:T(8,128)S(1)}, u32[]{:S(2)}) copy-start(f32[16,4,256,32]{2,3,1,0:T(8,128)S(1)} %get-tuple-element.26) | copy-start | bytes 6291460
  27.9 4.6 %copy-start.11 = (s32[65,8]{0,1:T(8,128)S(1)}, s32[65,8]{0,1:T(8,128)}, u32[]{:S(2)}) copy-start(s32[65,8]{0,1:T(8,128)} %param.27) | copy-start | bytes 6244
  29.1 4.8 %copy-start.6 = (f32[32,2048]{1,0:T(8,128)S(1)}, f32[32,2048]{1,0:T(8,128)}, u32[]{:S(2)}) copy-start(f32[32,2048]{1,0:T(8,128)} %reshape.368) | copy-start | bytes 786436
  62.6 15.1 %all-to-all-start.1 = ((f32[32,1,2112]{2,1,0:T(1,128)}), f32[32,1,2112]{2,1,0:T(1,128)S(1)}, u32[]{:S(2)}, u32[]{:S(2)}) async-start(f32[32,1,2112]{2,1,0:T(1,128)} %copy.51), calls=%async_computation.1 | async-start | bytes 557056 | tf_op jit(solution)/shard_map/all_to_all | solution.py:64
  67.9 14.4 %copy-start.12 = (f32[2048]{0:T(1024)S(1)}, f32[2048]{0:T(1024)}, u32[]{:S(2)}) copy-start(f32[2048]{0:T(1024)} %param.26) | copy-start | bytes 24580
  79.6 11.0 %all-to-all-start.2 = ((bf16[32,16,128]{2,1,0:T(8,128)(2,1)}), bf16[32,16,128]{2,1,0:T(8,128)(2,1)S(1)}, u32[]{:S(2)}, u32[]{:S(2)}) async-start(bf16[32,16,128]{2,1,0:T(8,128)(2,1)} %copy.53), calls=%async_computation.2 | async-start | bytes 262144 | tf_op jit(solution)/shard_map/all_to_all | solution.py:86
  82.3 8.3 %copy-start.13 = (bf16[1,1,2048]{2,1,0:T(2,128)(2,1)S(1)}, bf16[1,1,2048]{2,1,0:T(2,128)(2,1)}, u32[]{:S(2)}) copy-start(bf16[1,1,2048]{2,1,0:T(2,128)(2,1)} %param.23) | copy-start | bytes 12292
  82.4 8.3 %copy-start.2 = (bf16[64,2048]{1,0:T(8,128)(2,1)S(1)}, bf16[64,2048]{1,0:T(8,128)(2,1)}, u32[]{:S(2)}) copy-start(bf16[64,2048]{1,0:T(8,128)(2,1)} %param.25) | copy-start | bytes 786436
  84.3 10.5 %copy-start.5 = (bf16[32,16,2048]{2,1,0:T(8,128)(2,1)S(1)}, bf16[32,16,2048]{2,1,0:T(8,128)(2,1)}, u32[]{:S(2)}) copy-start(bf16[32,16,2048]{2,1,0:T(8,128)(2,1)} %fusion.2) | copy-start | bytes 6291460
  92.1 28.9 %all-to-all-start.3 = ((bf16[32,8,2048]{2,1,0:T(8,128)(2,1)}), bf16[32,8,2048]{2,1,0:T(8,128)(2,1)S(1)}, u32[]{:S(2)}, u32[]{:S(2)}) async-start(bf16[32,8,2048]{2,1,0:T(8,128)(2,1)} %fusion.25), calls=%async_computation.3 | async-start | bytes 2097152 | tf_op jit(solution)/shard_map/all_to_all | solution.py:113
  94.8 4.7 %copy-start.17 = (bf16[1,2048,1024]{2,1,0:T(8,128)(2,1)S(1)}, bf16[1,2048,1024]{2,1,0:T(8,128)(2,1)}, u32[]{:S(2)}) copy-start(bf16[1,2048,1024]{2,1,0:T(8,128)(2,1)} %param.30) | copy-start | bytes 12582916
  99.5 2.6 %copy-start.16 = (bf16[1,1024,2048]{2,1,0:T(8,128)(2,1)S(1)}, bf16[1,1024,2048]{2,1,0:T(8,128)(2,1)}, u32[]{:S(2)}) copy-start(bf16[1,1024,2048]{2,1,0:T(8,128)(2,1)} %param.31) | copy-start | bytes 12582916
  121.0 52.4 %all-to-all-start.4 = ((bf16[32,16,2048]{2,1,0:T(8,128)(2,1)}), bf16[32,16,2048]{2,1,0:T(8,128)(2,1)S(1)}, u32[]{:S(2)}, u32[]{:S(2)}) async-start(bf16[32,16,2048]{2,1,0:T(8,128)(2,1)} %fusion.19), calls=%async_computation.4 | async-start | bytes 4194304 | tf_op jit(solution)/shard_map/all_to_all | solution.py:137
  136.5 41.1 %copy-start.14 = (f32[65,8]{0,1:T(8,128)S(1)}, f32[65,8]{0,1:T(8,128)}, u32[]{:S(2)}) copy-start(f32[65,8]{0,1:T(8,128)} %param.28) | copy-start | bytes 6244
  173.4 30.3 %all-to-all-start.5 = ((bf16[32,8,2048]{2,1,0:T(8,128)(2,1)}), bf16[32,8,2048]{2,1,0:T(8,128)(2,1)S(1)}, u32[]{:S(2)}, u32[]{:S(2)}) async-start(bf16[32,8,2048]{2,1,0:T(8,128)(2,1)} %fusion.22), calls=%async_computation.5 | async-start | bytes 2097152 | tf_op jit(solution)/shard_map/all_to_all | solution.py:137
  204.1 1.2 copy-start.7
  204.1 1.2 copy-start.8
  (1 other events, 1.0 us)

commit v14 on v13

--- a/solution.py
+++ b/solution.py
@@ -107,6 +107,7 @@
     select = jnp.any(
         slot_index.reshape(row_count, -1)[None, :, :] == slots[:, None, None], axis=2
     ).astype(jnp.bfloat16)
+    select = lax.optimization_barrier(select)
     outgoing = jnp.dot(select, normed, preferred_element_type=jnp.float32).astype(jnp.bfloat16)
     tensor_count = lax.axis_size("tensor")
     outgoing = outgoing.reshape(tensor_count, slot_count // tensor_count, normed.shape[1])

time: 208 us -> 208 us (level)
  no operation moved by 1% of the time
where the time goes in v14:
time: 208 us; the launch traced here: 207 us
  waiting for transfers between devices  120 us (58%)
  matrix products  34 us (16%)
  starting transfers between devices  24.3 us (12%)
  local copies, waits for them, and re-layouts  18.3 us (9%)
  other arithmetic  9.52 us (5%)
    all_to_all x2, waiting for transfers between devices, give_back(): lax.all_to_all(lax.psum_scatter(done, 'dp', scatter_dimension=0, tiled=Tr...  61.1 us
    all_to_all x2, waiting for transfers between devices, dispatch(): lax.all_to_all(outgoing, 'tensor', split_axis=0, concat_axis=0, tiled=True)  42.5 us
    dot_general x2, matrix products, expert_mlp(): return jnp.dot(active, down_w, preferred_element_type=jnp.float32)  10.9 us
    unnamed x45, local copies, waits for them, and re-layouts  10.6 us
    all_to_all x2, starting transfers between devices, dispatch(): lax.all_to_all(outgoing, 'tensor', split_axis=0, concat_axis=0, tiled=True)  9.94 us
    all_to_all x1, waiting for transfers between devices, attention_finish(): received = lax.all_to_all(payload, 'tensor', 0, 0, tiled=True)  9.73 us
    dot_general x2, matrix products, expert_mlp(): gate = jnp.dot(flat_rows, gate_w, preferred_element_type=jnp.float32)  9.15 us
    all_to_all x2, starting transfers between devices, give_back(): lax.all_to_all(lax.psum_scatter(done, 'dp', scatter_dimension=0, tiled=Tr...  7.55 us
  transfers between devices with their start and end apart: 6, of which 6 were waited for; matrix products, arithmetic and copies ran while one was open for 24% of the time, Pallas kernels for 0%

profile of v14, /device:TPU:0, one launch (start us, length us, event | category | flops | bytes accessed | tf_op | source)
XLA Modules:
  0.0 206.9 jit_solution(9787192780129823886)
XLA Ops:
  2.3 3.0 %convolution_convert_fusion = bf16[512,2048]{1,0:T(8,128)(2,1)} fusion(bf16[512,64]{0,1:T(8,128)(2,1)S(1)} %convert_element_type.214, bf16[64,2048]{1,0:T(8,128)(2,1)} %param.25), kind=kOutput, calls=%fused_computation.26 | convolution fusion | flops 135266304 | bytes 2424832 | tf_op jit(solution)/shard_map/dot_general | solution.py:111
  5.4 7.3 %all-to-all-start = ((bf16[32,16,2048]{2,1,0:T(8,128)(2,1)}), bf16[32,16,2048]{2,1,0:T(8,128)(2,1)S(1)}, u32[]{:S(2)}, u32[]{:S(2)}) async-start(bf16[32,16,2048]{2,1,0:T(8,128)(2,1)} %bitcast.144), calls=%async_computation | async-start | bytes 4194304 | tf_op jit(solution)/shard_map/all_to_all | solution.py:114
  12.7 5.6 %copy.61 = bf16[128,8,16,128]{3,2,1,0:T(8,128)(2,1)} copy(bf16[128,8,16,128]{3,1,2,0:T(8,128)(2,1)} %bitcast.145) | data formatting | bytes 8388608
  18.6 3.7 %copy.64 = bf16[128,8,16,128]{3,2,1,0:T(8,128)(2,1)S(1)} copy(bf16[128,8,16,128]{3,1,2,0:T(8,128)(2,1)} %bitcast.146) | data formatting | bytes 8388608
  22.6 2.5 %fusion.29 = (f32[32,16]{0,1:T(8,128)S(1)}, f32[16,4,256,32]{2,3,1,0:T(8,128)S(1)}) fusion(pred[4,32,256]{2,1,0:T(8,128)(4,1)S(1)} %broadcast_and_fusion, bf16[32,16,128,1]{2,1,0,3:T(8,128)(2,1)S(1)} %bitcast.160, bf16[4,256,16,128]{3,2,1,0:T(8,128)(2,1)S(1)} %bitcast.147), kind=kOutput, calls=%fused_computation.37 | convolution fusion | flops 135790080 | bytes 6457344 | tf_op jit(solution)/shard_map/rhd,gjhd->grhj/dot_general | solution.py:35
  25.1 2.5 %fusion.45 = f32[32,16,128]{2,0,1:T(8,128)S(1)} fusion(bf16[4,256,16,128]{3,2,1,0:T(8,128)(2,1)S(1)} %bitcast.148, f32[16,4,256,32]{2,3,1,0:T(8,128)S(1)} %get-tuple-element.26, f32[32,16]{0,1:T(8,128)S(1)} %get-tuple-element.20, pred[4,32,256]{2,1,0:T(8,128)(4,1)S(1)} %broadcast_and_fusion), kind=kOutput, calls=%fused_computation.48 | convolution fusion | flops 136314880 | bytes 6588416 | tf_op jit(solution)/shard_map/grhj,gjhd->rhd/dot_general | solution.py:48
  29.1 2.2 %fusion.34 = f32[32,16]{0,1:T(8,128)S(1)} fusion(f32[16,4,256,32]{2,3,1,0:T(8,128)} %copy-done.4, f32[32,16]{0,1:T(8,128)S(1)} %get-tuple-element.20, pred[4,32,256]{2,1,0:T(8,128)(4,1)S(1)} %broadcast_and_fusion), kind=kLoop, calls=%fused_computation.41 | loop fusion | flops 2096640 | bytes 2134016 | tf_op jit(solution)/shard_map/reduce_sum | solution.py:47
  34.2 27.3 %all-to-all-done = bf16[32,16,2048]{2,1,0:T(8,128)(2,1)S(1)} async-done(((bf16[32,16,2048]{2,1,0:T(8,128)(2,1)}), bf16[32,16,2048]{2,1,0:T(8,128)(2,1)S(1)}, u32[]{:S(2)}, u32[]{:S(2)}) %all-to-all-start) | async-done | bytes 2097184 | tf_op jit(solution)/shard_map/all_to_all | solution.py:114
  62.5 4.0 %all-to-all-start.1 = ((f32[32,1,2112]{2,1,0:T(1,128)}), f32[32,1,2112]{2,1,0:T(1,128)S(1)}, u32[]{:S(2)}, u32[]{:S(2)}) async-start(f32[32,1,2112]{2,1,0:T(1,128)} %copy.51), calls=%async_computation.1 | async-start | bytes 557056 | tf_op jit(solution)/shard_map/all_to_all | solution.py:64
  67.9 9.7 %all-to-all-done.1 = f32[32,1,2112]{2,1,0:T(1,128)S(1)} async-done(((f32[32,1,2112]{2,1,0:T(1,128)}), f32[32,1,2112]{2,1,0:T(1,128)S(1)}, u32[]{:S(2)}, u32[]{:S(2)}) %all-to-all-start.1) | async-done | bytes 270368 | tf_op jit(solution)/shard_map/all_to_all | solution.py:64
  79.6 2.8 %all-to-all-start.2 = ((bf16[32,16,128]{2,1,0:T(8,128)(2,1)}), bf16[32,16,128]{2,1,0:T(8,128)(2,1)S(1)}, u32[]{:S(2)}, u32[]{:S(2)}) async-start(bf16[32,16,128]{2,1,0:T(8,128)(2,1)} %copy.53), calls=%async_computation.2 | async-start | bytes 262144 | tf_op jit(solution)/shard_map/all_to_all | solution.py:86
  82.3 1.9 fusion.2
  84.3 6.3 %all-to-all-done.2 = bf16[32,16,128]{2,1,0:T(8,128)(2,1)S(1)} async-done(((bf16[32,16,128]{2,1,0:T(8,128)(2,1)}), bf16[32,16,128]{2,1,0:T(8,128)(2,1)S(1)}, u32[]{:S(2)}, u32[]{:S(2)}) %all-to-all-start.2) | async-done | bytes 131104 | tf_op jit(solution)/shard_map/all_to_all | solution.py:86
  92.1 2.6 %all-to-all-start.3 = ((bf16[32,8,2048]{2,1,0:T(8,128)(2,1)}), bf16[32,8,2048]{2,1,0:T(8,128)(2,1)S(1)}, u32[]{:S(2)}, u32[]{:S(2)}) async-start(bf16[32,8,2048]{2,1,0:T(8,128)(2,1)} %fusion.25), calls=%async_computation.3 | async-start | bytes 2097152 | tf_op jit(solution)/shard_map/all_to_all | solution.py:114
  94.7 4.7 %fusion.13 = f32[512,1024]{1,0:T(8,128)S(1)} fusion(bf16[512,2048]{1,0:T(8,128)(2,1)S(1)} %bitcast.151, bf16[1,2048,1024]{2,1,0:T(8,128)(2,1)} %param.29), kind=kOutput, calls=%fused_computation.18 | convolution fusion | flops 2147483648 | bytes 8388608 | tf_op jit(solution)/shard_map/dot_general | solution.py:14
  99.4 2.5 %multiply_convert_fusion = bf16[512,1024]{1,0:T(8,128)(2,1)S(1)} fusion(f32[512,1024]{1,0:T(8,128)S(1)} %fusion.13, bf16[512,2048]{1,0:T(8,128)(2,1)S(1)} %bitcast.152, bf16[1,2048,1024]{2,1,0:T(8,128)(2,1)S(1)} %copy-done.17), kind=kOutput, calls=%fused_computation.40 | convolution fusion | flops 2150629376 | bytes 9437184 | tf_op jit(solution)/shard_map/dot_general | solution.py:15
  102.0 3.7 %fusion.19 = bf16[32,16,2048]{2,1,0:T(8,128)(2,1)} fusion(bf16[32,16,1024]{2,1,0:T(8,128)(2,1)S(1)} %bitcast.166, bf16[1,1024,2048]{2,1,0:T(8,128)(2,1)S(1)} %copy-done.16), kind=kOutput, calls=%fused_computation.25 | convolution fusion | flops 2148532224 | bytes 7340032 | tf_op jit(solution)/shard_map/dot_general | solution.py:17
  105.7 15.2 %all-to-all-done.3 = bf16[32,8,2048]{2,1,0:T(8,128)(2,1)S(1)} async-done(((bf16[32,8,2048]{2,1,0:T(8,128)(2,1)}), bf16[32,8,2048]{2,1,0:T(8,128)(2,1)S(1)}, u32[]{:S(2)}, u32[]{:S(2)}) %all-to-all-start.3) | async-done | bytes 1048608 | tf_op jit(solution)/shard_map/all_to_all | solution.py:114
  120.9 3.5 %all-to-all-start.4 = ((bf16[32,16,2048]{2,1,0:T(8,128)(2,1)}), bf16[32,16,2048]{2,1,0:T(8,128)(2,1)S(1)}, u32[]{:S(2)}, u32[]{:S(2)}) async-start(bf16[32,16,2048]{2,1,0:T(8,128)(2,1)} %fusion.19), calls=%async_computation.4 | async-start | bytes 4194304 | tf_op jit(solution)/shard_map/all_to_all | solution.py:138
  124.8 4.5 %fusion.11 = f32[256,1024]{1,0:T(8,128)} fusion(bf16[1,2048,1024]{2,1,0:T(8,128)(2,1)} %param.29, bf16[32,8,2048]{2,1,0:T(8,128)(2,1)S(1)} %all-to-all-done.3, f32[2048]{0:T(1024)S(1)} %copy-done.12, f32[32,8]{1,0:T(8,128)S(1)} %add_rsqrt_fusion), kind=kOutput, calls=%fused_computation.16 | convolution fusion | flops 1075838976 | bytes 6300672 | tf_op jit(solution)/shard_map/dot_general | solution.py:14
  129.3 7.2 %fusion.22 = bf16[32,8,2048]{2,1,0:T(8,128)(2,1)} fusion(bf16[1,1024,2048]{2,1,0:T(8,128)(2,1)} %param.31, bf16[1,2048,1024]{2,1,0:T(8,128)(2,1)} %param.30, f32[256,1024]{1,0:T(8,128)} %fusion.11, bf16[32,8,2048]{2,1,0:T(8,128)(2,1)S(1)} %all-to-all-done.3, f32[2048]{0:T(1024)S(1)} %copy-done.12, f32[32,8]{1,0:T(8,128)S(1)} %add_rsqrt_fusion), kind=kOutput, calls=%fused_computation.30 | convolution fusion | flops 2151677952 | bytes 11543552 | tf_op jit(solution)/shard_map/dot_general | solution.py:17
  136.4 37.0 %all-to-all-done.4 = bf16[32,16,2048]{2,1,0:T(8,128)(2,1)S(1)} async-done(((bf16[32,16,2048]{2,1,0:T(8,128)(2,1)}), bf16[32,16,2048]{2,1,0:T(8,128)(2,1)S(1)}, u32[]{:S(2)}, u32[]{:S(2)}) %all-to-all-start.4) | async-done | bytes 2097184 | tf_op jit(solution)/shard_map/all_to_all | solution.py:138
  173.4 4.0 %all-to-all-start.5 = ((bf16[32,8,2048]{2,1,0:T(8,128)(2,1)}), bf16[32,8,2048]{2,1,0:T(8,128)(2,1)S(1)}, u32[]{:S(2)}, u32[]{:S(2)}) async-start(bf16[32,8,2048]{2,1,0:T(8,128)(2,1)} %fusion.22), calls=%async_computation.5 | async-start | bytes 2097152 | tf_op jit(solution)/shard_map/all_to_all | solution.py:138
  179.5 24.1 %all-to-all-done.5 = bf16[32,8,2048]{2,1,0:T(8,128)(2,1)S(1)} async-done(((bf16[32,8,2048]{2,1,0:T(8,128)(2,1)}), bf16[32,8,2048]{2,1,0:T(8,128)(2,1)S(1)}, u32[]{:S(2)}, u32[]{:S(2)}) %all-to-all-start.5) | async-done | bytes 1048608 | tf_op jit(solution)/shard_map/all_to_all | solution.py:138
  (118 shorter events, 17.9 us)
Async XLA Ops:
  0.6 78.0 %copy-start = (bf16[64,2048]{1,0:T(8,128)(2,1)S(1)}, bf16[64,2048]{1,0:T(8,128)(2,1)}, u32[]{:S(2)}) copy-start(bf16[64,2048]{1,0:T(8,128)(2,1)} %param.24) | copy-start | bytes 786436
  5.4 7.3 %copy-start.10 = (bf16[1,32,2048]{2,1,0:T(8,128)(2,1)S(1)}, bf16[1,32,2048]{2,1,0:T(8,128)(2,1)}, u32[]{:S(2)}) copy-start(bf16[1,32,2048]{2,1,0:T(8,128)(2,1)} %param.16) | copy-start | bytes 393220
  5.4 56.2 %all-to-all-start = ((bf16[32,16,2048]{2,1,0:T(8,128)(2,1)}), bf16[32,16,2048]{2,1,0:T(8,128)(2,1)S(1)}, u32[]{:S(2)}, u32[]{:S(2)}) async-start(bf16[32,16,2048]{2,1,0:T(8,128)(2,1)} %bitcast.144), calls=%async_computation | async-start | bytes 4194304 | tf_op jit(solution)/shard_map/all_to_all | solution.py:114
  12.7 5.6 %copy-start.9 = (bf16[1,32,2048]{2,1,0:T(8,128)(2,1)S(1)}, bf16[1,32,2048]{2,1,0:T(8,128)(2,1)}, u32[]{:S(2)}) copy-start(bf16[1,32,2048]{2,1,0:T(8,128)(2,1)} %param.17) | copy-start | bytes 393220
  18.6 3.8 %copy-start.18 = (s32[1,32]{1,0:T(1,128)S(1)}, s32[1,32]{1,0:T(1,128)}, u32[]{:S(2)}) copy-start(s32[1,32]{1,0:T(1,128)} %param.21) | copy-start | bytes 388
  18.6 3.8 %copy-start.15 = (s32[1,4]{1,0:T(1,128)S(1)}, s32[1,4]{1,0:T(1,128)}, u32[]{:S(2)}) copy-start(s32[1,4]{1,0:T(1,128)} %param.22) | copy-start | bytes 52
  18.6 4.0 %copy-start.1 = (bf16[128,8,16,128]{3,2,1,0:T(8,128)(2,1)S(1)}, bf16[128,8,16,128]{3,2,1,0:T(8,128)(2,1)}, u32[]{:S(2)}) copy-start(bf16[128,8,16,128]{3,2,1,0:T(8,128)(2,1)} %copy.61) | copy-start | bytes 12582916
  25.1 2.5 %copy-start.4 = (f32[16,4,256,32]{2,3,1,0:T(8,128)}, f32[16,4,256,32]{2,3,1,0:T(8,128)S(1)}, u32[]{:S(2)}) copy-start(f32[16,4,256,32]{2,3,1,0:T(8,128)S(1)} %get-tuple-element.26) | copy-start | bytes 6291460
  27.9 4.6 %copy-start.11 = (s32[65,8]{0,1:T(8,128)S(1)}, s32[65,8]{0,1:T(8,128)}, u32[]{:S(2)}) copy-start(s32[65,8]{0,1:T(8,128)} %param.27) | copy-start | bytes 6244
  29.1 4.8 %copy-start.6 = (f32[32,2048]{1,0:T(8,128)S(1)}, f32[32,2048]{1,0:T(8,128)}, u32[]{:S(2)}) copy-start(f32[32,2048]{1,0:T(8,128)} %reshape.368) | copy-start | bytes 786436
  62.5 15.1 %all-to-all-start.1 = ((f32[32,1,2112]{2,1,0:T(1,128)}), f32[32,1,2112]{2,1,0:T(1,128)S(1)}, u32[]{:S(2)}, u32[]{:S(2)}) async-start(f32[32,1,2112]{2,1,0:T(1,128)} %copy.51), calls=%async_computation.1 | async-start | bytes 557056 | tf_op jit(solution)/shard_map/all_to_all | solution.py:64
  67.9 14.4 %copy-start.12 = (f32[2048]{0:T(1024)S(1)}, f32[2048]{0:T(1024)}, u32[]{:S(2)}) copy-start(f32[2048]{0:T(1024)} %param.26) | copy-start | bytes 24580
  79.6 11.0 %all-to-all-start.2 = ((bf16[32,16,128]{2,1,0:T(8,128)(2,1)}), bf16[32,16,128]{2,1,0:T(8,128)(2,1)S(1)}, u32[]{:S(2)}, u32[]{:S(2)}) async-start(bf16[32,16,128]{2,1,0:T(8,128)(2,1)} %copy.53), calls=%async_computation.2 | async-start | bytes 262144 | tf_op jit(solution)/shard_map/all_to_all | solution.py:86
  82.3 8.3 %copy-start.13 = (bf16[1,1,2048]{2,1,0:T(2,128)(2,1)S(1)}, bf16[1,1,2048]{2,1,0:T(2,128)(2,1)}, u32[]{:S(2)}) copy-start(bf16[1,1,2048]{2,1,0:T(2,128)(2,1)} %param.23) | copy-start | bytes 12292
  82.3 8.3 %copy-start.2 = (bf16[64,2048]{1,0:T(8,128)(2,1)S(1)}, bf16[64,2048]{1,0:T(8,128)(2,1)}, u32[]{:S(2)}) copy-start(bf16[64,2048]{1,0:T(8,128)(2,1)} %param.25) | copy-start | bytes 786436
  84.3 10.5 %copy-start.5 = (bf16[32,16,2048]{2,1,0:T(8,128)(2,1)S(1)}, bf16[32,16,2048]{2,1,0:T(8,128)(2,1)}, u32[]{:S(2)}) copy-start(bf16[32,16,2048]{2,1,0:T(8,128)(2,1)} %fusion.2) | copy-start | bytes 6291460
  92.1 28.9 %all-to-all-start.3 = ((bf16[32,8,2048]{2,1,0:T(8,128)(2,1)}), bf16[32,8,2048]{2,1,0:T(8,128)(2,1)S(1)}, u32[]{:S(2)}, u32[]{:S(2)}) async-start(bf16[32,8,2048]{2,1,0:T(8,128)(2,1)} %fusion.25), calls=%async_computation.3 | async-start | bytes 2097152 | tf_op jit(solution)/shard_map/all_to_all | solution.py:114
  94.7 4.7 %copy-start.17 = (bf16[1,2048,1024]{2,1,0:T(8,128)(2,1)S(1)}, bf16[1,2048,1024]{2,1,0:T(8,128)(2,1)}, u32[]{:S(2)}) copy-start(bf16[1,2048,1024]{2,1,0:T(8,128)(2,1)} %param.30) | copy-start | bytes 12582916
  99.4 2.6 %copy-start.16 = (bf16[1,1024,2048]{2,1,0:T(8,128)(2,1)S(1)}, bf16[1,1024,2048]{2,1,0:T(8,128)(2,1)}, u32[]{:S(2)}) copy-start(bf16[1,1024,2048]{2,1,0:T(8,128)(2,1)} %param.31) | copy-start | bytes 12582916
  120.9 52.4 %all-to-all-start.4 = ((bf16[32,16,2048]{2,1,0:T(8,128)(2,1)}), bf16[32,16,2048]{2,1,0:T(8,128)(2,1)S(1)}, u32[]{:S(2)}, u32[]{:S(2)}) async-start(bf16[32,16,2048]{2,1,0:T(8,128)(2,1)} %fusion.19), calls=%async_computation.4 | async-start | bytes 4194304 | tf_op jit(solution)/shard_map/all_to_all | solution.py:138
  136.4 41.1 %copy-start.14 = (f32[65,8]{0,1:T(8,128)S(1)}, f32[65,8]{0,1:T(8,128)}, u32[]{:S(2)}) copy-start(f32[65,8]{0,1:T(8,128)} %param.28) | copy-start | bytes 6244
  173.4 30.3 %all-to-all-start.5 = ((bf16[32,8,2048]{2,1,0:T(8,128)(2,1)}), bf16[32,8,2048]{2,1,0:T(8,128)(2,1)S(1)}, u32[]{:S(2)}, u32[]{:S(2)}) async-start(bf16[32,8,2048]{2,1,0:T(8,128)(2,1)} %fusion.22), calls=%async_computation.5 | async-start | bytes 2097152 | tf_op jit(solution)/shard_map/all_to_all | solution.py:138
  204.0 1.2 copy-start.7
  204.0 1.2 copy-start.8
  (1 other events, 1.0 us)

commit v15 on v13

--- a/solution.py
+++ b/solution.py
@@ -107,7 +107,10 @@
     select = jnp.any(
         slot_index.reshape(row_count, -1)[None, :, :] == slots[:, None, None], axis=2
     ).astype(jnp.bfloat16)
-    outgoing = jnp.dot(select, normed, preferred_element_type=jnp.float32).astype(jnp.bfloat16)
+    numbers = jnp.arange(1, row_count + 1, dtype=jnp.float32).astype(jnp.bfloat16)
+    which = jnp.dot(select, numbers, preferred_element_type=jnp.float32).astype(jnp.int32) - 1
+    which = jnp.where(which < 0, row_count, which)
+    outgoing = jnp.take(normed, which, axis=0, mode="fill", fill_value=0).astype(jnp.bfloat16)
     tensor_count = lax.axis_size("tensor")
     outgoing = outgoing.reshape(tensor_count, slot_count // tensor_count, normed.shape[1])
     return lax.all_to_all(outgoing, "tensor", split_axis=0, concat_axis=0, tiled=True)

time: 208 us -> 214 us (1.029)
  other arithmetic: 9.51 us -> 15.6 us
  local copies, waits for them, and re-layouts: 18.3 us -> 23.7 us
  matrix products: 34 us -> 31 us
  waiting for transfers between devices: 120 us -> 117 us
    dot_general x2, matrix products: 4.51 us -> 0.27 us  [dispatch(): jnp.dot(select, numbers, preferred_element_type=jnp.float32)]
    gather x0 -> x2, local copies, waits for them, and re-layouts: none -> 3.82 us  [dispatch(): jnp.take(normed, which, axis=0, mode='fill', fill_value=0)]
    all_to_all x2, waiting for transfers between devices: 42.5 us -> 39.7 us  [dispatch(): lax.all_to_all(outgoing, 'tensor', split_axis=0, concat_axis=0, tiled=True)]
    select_n x0 -> x3, other arithmetic: none -> 2.68 us  [dispatch(): jnp.take(normed, which, axis=0, mode='fill', fill_value=0)]
    unnamed x45 -> x39, local copies, waits for them, and re-layouts: 10.6 us -> 11.4 us
where the time goes in v15:
time: 214 us; the launch traced here: 213 us
  waiting for transfers between devices  117 us (55%)
  matrix products  31 us (14%)
  starting transfers between devices  24.4 us (11%)
  local copies, waits for them, and re-layouts  23.7 us (11%)
  other arithmetic  15.6 us (7%)
    all_to_all x2, waiting for transfers between devices, give_back(): lax.all_to_all(lax.psum_scatter(done, 'dp', scatter_dimension=0, tiled=Tr...  60.4 us
    all_to_all x2, waiting for transfers between devices, dispatch(): lax.all_to_all(outgoing, 'tensor', split_axis=0, concat_axis=0, tiled=True)  39.7 us
    unnamed x39, local copies, waits for them, and re-layouts  11.4 us
    dot_general x2, matrix products, expert_mlp(): return jnp.dot(active, down_w, preferred_element_type=jnp.float32)  11.2 us
    all_to_all x1, waiting for transfers between devices, attention_finish(): received = lax.all_to_all(payload, 'tensor', 0, 0, tiled=True)  10.4 us
    dot_general x2, matrix products, expert_mlp(): gate = jnp.dot(flat_rows, gate_w, preferred_element_type=jnp.float32)  10.1 us
    all_to_all x2, starting transfers between devices, dispatch(): lax.all_to_all(outgoing, 'tensor', split_axis=0, concat_axis=0, tiled=True)  9.94 us
    all_to_all x2, starting transfers between devices, give_back(): lax.all_to_all(lax.psum_scatter(done, 'dp', scatter_dimension=0, tiled=Tr...  7.68 us
  transfers between devices with their start and end apart: 6, of which 6 were waited for; matrix products, arithmetic and copies ran while one was open for 24% of the time, Pallas kernels for 0%

profile of v15, /device:TPU:0, one launch (start us, length us, event | category | flops | bytes accessed | tf_op | source)
XLA Modules:
  0.0 212.9 jit_solution(15183281308208848400)
XLA Ops:
  2.6 2.5 %gather_fusion.3 = bf16[512,2048]{1,0:T(8,128)(2,1)S(1)} fusion(bf16[64,2048]{1,0:T(8,128)(2,1)S(1)} %copy-done.1, s32[1024]{0:T(1024)S(1)} %pad_clamp_fusion.1), kind=kCustom, calls=%fused_computation.3 | custom fusion | bytes 4196352 | tf_op jit(solution)/shard_map/jit(_take)/gather | solution.py:113
  6.6 7.3 %all-to-all-start = ((bf16[32,16,2048]{2,1,0:T(8,128)(2,1)}), bf16[32,16,2048]{2,1,0:T(8,128)(2,1)S(1)}, u32[]{:S(2)}, u32[]{:S(2)}) async-start(bf16[32,16,2048]{2,1,0:T(8,128)(2,1)} %broadcast_select_fusion), calls=%async_computation | async-start | bytes 4194304 | tf_op jit(solution)/shard_map/all_to_all | solution.py:116
  14.1 5.6 %copy.61 = bf16[128,8,16,128]{3,2,1,0:T(8,128)(2,1)} copy(bf16[128,8,16,128]{3,1,2,0:T(8,128)(2,1)} %bitcast.152) | data formatting | bytes 8388608
  20.0 3.7 %copy.64 = bf16[128,8,16,128]{3,2,1,0:T(8,128)(2,1)S(1)} copy(bf16[128,8,16,128]{3,1,2,0:T(8,128)(2,1)} %bitcast.153) | data formatting | bytes 8388608
  23.9 2.5 %fusion.28 = (f32[32,16]{0,1:T(8,128)S(1)}, f32[16,4,256,32]{2,3,1,0:T(8,128)S(1)}) fusion(pred[4,32,256]{2,1,0:T(8,128)(4,1)S(1)} %broadcast_and_fusion, bf16[32,16,128,1]{2,1,0,3:T(8,128)(2,1)S(1)} %bitcast.167, bf16[4,256,16,128]{3,2,1,0:T(8,128)(2,1)S(1)} %bitcast.154), kind=kOutput, calls=%fused_computation.36 | convolution fusion | flops 135790080 | bytes 6457344 | tf_op jit(solution)/shard_map/rhd,gjhd->grhj/dot_general | solution.py:35
  26.4 2.5 %fusion.44 = f32[32,16,128]{2,0,1:T(8,128)S(1)} fusion(bf16[4,256,16,128]{3,2,1,0:T(8,128)(2,1)S(1)} %bitcast.155, f32[16,4,256,32]{2,3,1,0:T(8,128)S(1)} %get-tuple-element.28, f32[32,16]{0,1:T(8,128)S(1)} %get-tuple-element.22, pred[4,32,256]{2,1,0:T(8,128)(4,1)S(1)} %broadcast_and_fusion), kind=kOutput, calls=%fused_computation.48 | convolution fusion | flops 136314880 | bytes 6588416 | tf_op jit(solution)/shard_map/grhj,gjhd->rhd/dot_general | solution.py:48
  31.5 2.2 %fusion.33 = f32[32,16]{0,1:T(8,128)S(1)} fusion(f32[16,4,256,32]{2,3,1,0:T(8,128)} %copy-done.5, f32[32,16]{0,1:T(8,128)S(1)} %get-tuple-element.22, pred[4,32,256]{2,1,0:T(8,128)(4,1)S(1)} %broadcast_and_fusion), kind=kLoop, calls=%fused_computation.41 | loop fusion | flops 2096640 | bytes 2134016 | tf_op jit(solution)/shard_map/reduce_sum | solution.py:47
  37.7 25.1 %all-to-all-done = bf16[32,16,2048]{2,1,0:T(8,128)(2,1)S(1)} async-done(((bf16[32,16,2048]{2,1,0:T(8,128)(2,1)}), bf16[32,16,2048]{2,1,0:T(8,128)(2,1)S(1)}, u32[]{:S(2)}, u32[]{:S(2)}) %all-to-all-start) | async-done | bytes 2097184 | tf_op jit(solution)/shard_map/all_to_all | solution.py:116
  63.8 4.2 %all-to-all-start.1 = ((f32[32,1,2112]{2,1,0:T(1,128)}), f32[32,1,2112]{2,1,0:T(1,128)S(1)}, u32[]{:S(2)}, u32[]{:S(2)}) async-start(f32[32,1,2112]{2,1,0:T(1,128)} %copy.51), calls=%async_computation.1 | async-start | bytes 557056 | tf_op jit(solution)/shard_map/all_to_all | solution.py:64
  68.5 10.4 %all-to-all-done.1 = f32[32,1,2112]{2,1,0:T(1,128)S(1)} async-done(((f32[32,1,2112]{2,1,0:T(1,128)}), f32[32,1,2112]{2,1,0:T(1,128)S(1)}, u32[]{:S(2)}, u32[]{:S(2)}) %all-to-all-start.1) | async-done | bytes 270368 | tf_op jit(solution)/shard_map/all_to_all | solution.py:64
  82.5 2.6 %all-to-all-start.2 = ((bf16[32,16,128]{2,1,0:T(8,128)(2,1)}), bf16[32,16,128]{2,1,0:T(8,128)(2,1)S(1)}, u32[]{:S(2)}, u32[]{:S(2)}) async-start(bf16[32,16,128]{2,1,0:T(8,128)(2,1)} %copy.53), calls=%async_computation.2 | async-start | bytes 262144 | tf_op jit(solution)/shard_map/all_to_all | solution.py:86
  85.1 1.9 fusion.2
  87.0 6.3 %all-to-all-done.2 = bf16[32,16,128]{2,1,0:T(8,128)(2,1)S(1)} async-done(((bf16[32,16,128]{2,1,0:T(8,128)(2,1)}), bf16[32,16,128]{2,1,0:T(8,128)(2,1)S(1)}, u32[]{:S(2)}, u32[]{:S(2)}) %all-to-all-start.2) | async-done | bytes 131104 | tf_op jit(solution)/shard_map/all_to_all | solution.py:86
  95.9 2.6 %all-to-all-start.3 = ((bf16[32,8,2048]{2,1,0:T(8,128)(2,1)}), bf16[32,8,2048]{2,1,0:T(8,128)(2,1)S(1)}, u32[]{:S(2)}, u32[]{:S(2)}) async-start(bf16[32,8,2048]{2,1,0:T(8,128)(2,1)} %bitcast_select_fusion.1), calls=%async_computation.3 | async-start | bytes 2097152 | tf_op jit(solution)/shard_map/all_to_all | solution.py:116
  98.6 5.3 %fusion.13 = f32[512,1024]{1,0:T(8,128)S(1)} fusion(bf16[512,2048]{1,0:T(8,128)(2,1)} %bitcast.158, bf16[1,2048,1024]{2,1,0:T(8,128)(2,1)} %param.29), kind=kOutput, calls=%fused_computation.20 | convolution fusion | flops 2147483648 | bytes 8388608 | tf_op jit(solution)/shard_map/dot_general | solution.py:14
  103.9 2.5 %multiply_convert_fusion = bf16[512,1024]{1,0:T(8,128)(2,1)S(1)} fusion(f32[512,1024]{1,0:T(8,128)S(1)} %fusion.13, bf16[512,2048]{1,0:T(8,128)(2,1)S(1)} %bitcast.159, bf16[1,2048,1024]{2,1,0:T(8,128)(2,1)S(1)} %copy-done.14), kind=kOutput, calls=%fused_computation.39 | convolution fusion | flops 2150629376 | bytes 9437184 | tf_op jit(solution)/shard_map/dot_general | solution.py:15
  106.4 3.7 %fusion.19 = bf16[32,16,2048]{2,1,0:T(8,128)(2,1)} fusion(bf16[32,16,1024]{2,1,0:T(8,128)(2,1)S(1)} %bitcast.176, bf16[1,1024,2048]{2,1,0:T(8,128)(2,1)S(1)} %copy-done.13), kind=kOutput, calls=%fused_computation.27 | convolution fusion | flops 2148532224 | bytes 7340032 | tf_op jit(solution)/shard_map/dot_general | solution.py:17
  110.2 14.6 %all-to-all-done.3 = bf16[32,8,2048]{2,1,0:T(8,128)(2,1)S(1)} async-done(((bf16[32,8,2048]{2,1,0:T(8,128)(2,1)}), bf16[32,8,2048]{2,1,0:T(8,128)(2,1)S(1)}, u32[]{:S(2)}, u32[]{:S(2)}) %all-to-all-start.3) | async-done | bytes 1048608 | tf_op jit(solution)/shard_map/all_to_all | solution.py:116
  125.7 3.5 %all-to-all-start.4 = ((bf16[32,16,2048]{2,1,0:T(8,128)(2,1)}), bf16[32,16,2048]{2,1,0:T(8,128)(2,1)S(1)}, u32[]{:S(2)}, u32[]{:S(2)}) async-start(bf16[32,16,2048]{2,1,0:T(8,128)(2,1)} %fusion.19), calls=%async_computation.4 | async-start | bytes 4194304 | tf_op jit(solution)/shard_map/all_to_all | solution.py:140
  130.8 4.8 %fusion.11 = f32[256,1024]{1,0:T(8,128)} fusion(bf16[1,2048,1024]{2,1,0:T(8,128)(2,1)} %param.29, bf16[32,8,2048]{2,1,0:T(8,128)(2,1)} %copy-done.3, f32[2048]{0:T(1024)S(1)} %copy-done.9, f32[32,8]{1,0:T(8,128)S(1)} %add_rsqrt_fusion), kind=kOutput, calls=%fused_computation.18 | convolution fusion | flops 1075838976 | bytes 6300672 | tf_op jit(solution)/shard_map/dot_general | solution.py:14
  135.6 7.5 %fusion.22 = bf16[32,8,2048]{2,1,0:T(8,128)(2,1)} fusion(bf16[1,1024,2048]{2,1,0:T(8,128)(2,1)} %param.31, bf16[1,2048,1024]{2,1,0:T(8,128)(2,1)} %param.30, f32[256,1024]{1,0:T(8,128)} %fusion.11, bf16[32,8,2048]{2,1,0:T(8,128)(2,1)} %copy-done.3, f32[2048]{0:T(1024)S(1)} %copy-done.9, f32[32,8]{1,0:T(8,128)S(1)} %add_rsqrt_fusion), kind=kOutput, calls=%fused_computation.30 | convolution fusion | flops 2151677952 | bytes 11543552 | tf_op jit(solution)/shard_map/dot_general | solution.py:17
  143.1 35.1 %all-to-all-done.4 = bf16[32,16,2048]{2,1,0:T(8,128)(2,1)S(1)} async-done(((bf16[32,16,2048]{2,1,0:T(8,128)(2,1)}), bf16[32,16,2048]{2,1,0:T(8,128)(2,1)S(1)}, u32[]{:S(2)}, u32[]{:S(2)}) %all-to-all-start.4) | async-done | bytes 2097184 | tf_op jit(solution)/shard_map/all_to_all | solution.py:140
  178.2 4.1 %all-to-all-start.5 = ((bf16[32,8,2048]{2,1,0:T(8,128)(2,1)}), bf16[32,8,2048]{2,1,0:T(8,128)(2,1)}, u32[]{:S(2)}, u32[]{:S(2)}) async-start(bf16[32,8,2048]{2,1,0:T(8,128)(2,1)} %fusion.22), calls=%async_computation.5 | async-start | bytes 2097152 | tf_op jit(solution)/shard_map/all_to_all | solution.py:140
  183.2 25.3 %all-to-all-done.5 = bf16[32,8,2048]{2,1,0:T(8,128)(2,1)} async-done(((bf16[32,8,2048]{2,1,0:T(8,128)(2,1)}), bf16[32,8,2048]{2,1,0:T(8,128)(2,1)}, u32[]{:S(2)}, u32[]{:S(2)}) %all-to-all-start.5) | async-done | bytes 1048608 | tf_op jit(solution)/shard_map/all_to_all | solution.py:140
  (122 shorter events, 25.8 us)
Async XLA Ops:
  0.6 81.0 %copy-start = (bf16[64,2048]{1,0:T(8,128)(2,1)S(1)}, bf16[64,2048]{1,0:T(8,128)(2,1)}, u32[]{:S(2)}) copy-start(bf16[64,2048]{1,0:T(8,128)(2,1)} %param.24) | copy-start | bytes 786436
  0.6 2.0 copy-start.1
  6.6 7.3 %copy-start.15 = (s32[1,32]{1,0:T(1,128)S(1)}, s32[1,32]{1,0:T(1,128)}, u32[]{:S(2)}) copy-start(s32[1,32]{1,0:T(1,128)} %param.21) | copy-start | bytes 388
  6.6 7.4 %copy-start.7 = (bf16[1,32,2048]{2,1,0:T(8,128)(2,1)S(1)}, bf16[1,32,2048]{2,1,0:T(8,128)(2,1)}, u32[]{:S(2)}) copy-start(bf16[1,32,2048]{2,1,0:T(8,128)(2,1)} %param.16) | copy-start | bytes 393220
  6.6 56.2 %all-to-all-start = ((bf16[32,16,2048]{2,1,0:T(8,128)(2,1)}), bf16[32,16,2048]{2,1,0:T(8,128)(2,1)S(1)}, u32[]{:S(2)}, u32[]{:S(2)}) async-start(bf16[32,16,2048]{2,1,0:T(8,128)(2,1)} %broadcast_select_fusion), calls=%async_computation | async-start | bytes 4194304 | tf_op jit(solution)/shard_map/all_to_all | solution.py:116
  14.0 5.6 %copy-start.6 = (bf16[1,32,2048]{2,1,0:T(8,128)(2,1)S(1)}, bf16[1,32,2048]{2,1,0:T(8,128)(2,1)}, u32[]{:S(2)}) copy-start(bf16[1,32,2048]{2,1,0:T(8,128)(2,1)} %param.17) | copy-start | bytes 393220
  14.0 5.7 %copy-start.12 = (s32[1,4]{1,0:T(1,128)S(1)}, s32[1,4]{1,0:T(1,128)}, u32[]{:S(2)}) copy-start(s32[1,4]{1,0:T(1,128)} %param.22) | copy-start | bytes 52
  20.0 3.9 %copy-start.2 = (bf16[128,8,16,128]{3,2,1,0:T(8,128)(2,1)S(1)}, bf16[128,8,16,128]{3,2,1,0:T(8,128)(2,1)}, u32[]{:S(2)}) copy-start(bf16[128,8,16,128]{3,2,1,0:T(8,128)(2,1)} %copy.61) | copy-start | bytes 12582916
  26.4 2.5 %copy-start.5 = (f32[16,4,256,32]{2,3,1,0:T(8,128)}, f32[16,4,256,32]{2,3,1,0:T(8,128)S(1)}, u32[]{:S(2)}) copy-start(f32[16,4,256,32]{2,3,1,0:T(8,128)S(1)} %get-tuple-element.28) | copy-start | bytes 6291460
  29.2 6.6 %copy-start.8 = (s32[65,8]{0,1:T(8,128)S(1)}, s32[65,8]{0,1:T(8,128)}, u32[]{:S(2)}) copy-start(s32[65,8]{0,1:T(8,128)} %param.27) | copy-start | bytes 6244
  63.8 15.1 %all-to-all-start.1 = ((f32[32,1,2112]{2,1,0:T(1,128)}), f32[32,1,2112]{2,1,0:T(1,128)S(1)}, u32[]{:S(2)}, u32[]{:S(2)}) async-start(f32[32,1,2112]{2,1,0:T(1,128)} %copy.51), calls=%async_computation.1 | async-start | bytes 557056 | tf_op jit(solution)/shard_map/all_to_all | solution.py:64
  68.5 16.6 %copy-start.9 = (f32[2048]{0:T(1024)S(1)}, f32[2048]{0:T(1024)}, u32[]{:S(2)}) copy-start(f32[2048]{0:T(1024)} %param.26) | copy-start | bytes 24580
  82.5 10.8 %all-to-all-start.2 = ((bf16[32,16,128]{2,1,0:T(8,128)(2,1)}), bf16[32,16,128]{2,1,0:T(8,128)(2,1)S(1)}, u32[]{:S(2)}, u32[]{:S(2)}) async-start(bf16[32,16,128]{2,1,0:T(8,128)(2,1)} %copy.53), calls=%async_computation.2 | async-start | bytes 262144 | tf_op jit(solution)/shard_map/all_to_all | solution.py:86
  85.1 8.3 %copy-start.10 = (bf16[1,1,2048]{2,1,0:T(2,128)(2,1)S(1)}, bf16[1,1,2048]{2,1,0:T(2,128)(2,1)}, u32[]{:S(2)}) copy-start(bf16[1,1,2048]{2,1,0:T(2,128)(2,1)} %param.23) | copy-start | bytes 12292
  95.9 28.9 %all-to-all-start.3 = ((bf16[32,8,2048]{2,1,0:T(8,128)(2,1)}), bf16[32,8,2048]{2,1,0:T(8,128)(2,1)S(1)}, u32[]{:S(2)}, u32[]{:S(2)}) async-start(bf16[32,8,2048]{2,1,0:T(8,128)(2,1)} %bitcast_select_fusion.1), calls=%async_computation.3 | async-start | bytes 2097152 | tf_op jit(solution)/shard_map/all_to_all | solution.py:116
  98.5 5.3 %copy-start.4 = (bf16[32,16,2048]{2,1,0:T(8,128)(2,1)S(1)}, bf16[32,16,2048]{2,1,0:T(8,128)(2,1)}, u32[]{:S(2)}) copy-start(bf16[32,16,2048]{2,1,0:T(8,128)(2,1)} %fusion.2) | copy-start | bytes 6291460
  98.6 5.3 %copy-start.14 = (bf16[1,2048,1024]{2,1,0:T(8,128)(2,1)S(1)}, bf16[1,2048,1024]{2,1,0:T(8,128)(2,1)}, u32[]{:S(2)}) copy-start(bf16[1,2048,1024]{2,1,0:T(8,128)(2,1)} %param.30) | copy-start | bytes 12582916
  103.9 2.5 %copy-start.13 = (bf16[1,1024,2048]{2,1,0:T(8,128)(2,1)S(1)}, bf16[1,1024,2048]{2,1,0:T(8,128)(2,1)}, u32[]{:S(2)}) copy-start(bf16[1,1024,2048]{2,1,0:T(8,128)(2,1)} %param.31) | copy-start | bytes 12582916
  124.8 1.0 copy-start.3
  125.7 52.4 %all-to-all-start.4 = ((bf16[32,16,2048]{2,1,0:T(8,128)(2,1)}), bf16[32,16,2048]{2,1,0:T(8,128)(2,1)S(1)}, u32[]{:S(2)}, u32[]{:S(2)}) async-start(bf16[32,16,2048]{2,1,0:T(8,128)(2,1)} %fusion.19), calls=%async_computation.4 | async-start | bytes 4194304 | tf_op jit(solution)/shard_map/all_to_all | solution.py:140
  143.1 39.3 %copy-start.11 = (f32[65,8]{0,1:T(8,128)S(1)}, f32[65,8]{0,1:T(8,128)}, u32[]{:S(2)}) copy-start(f32[65,8]{0,1:T(8,128)} %param.28) | copy-start | bytes 6244
  178.2 30.4 %all-to-all-start.5 = ((bf16[32,8,2048]{2,1,0:T(8,128)(2,1)}), bf16[32,8,2048]{2,1,0:T(8,128)(2,1)}, u32[]{:S(2)}, u32[]{:S(2)}) async-start(bf16[32,8,2048]{2,1,0:T(8,128)(2,1)} %fusion.22), calls=%async_computation.5 | async-start | bytes 2097152 | tf_op jit(solution)/shard_map/all_to_all | solution.py:140

commit v16 on v14

--- a/solution.py
+++ b/solution.py
@@ -207,9 +207,8 @@
     second_done = experts_on(second_in, experts, norm_gain)
     first_back, second_done = lax.optimization_barrier((first_back, second_done))
     second_back = give_back(second_done)
-    returned = jnp.concatenate([first_back, second_back], axis=1).reshape(
-        tensor_count * stride, model_width
-    )
+    first_back = first_back.reshape(tensor_count * early, model_width)
+    second_back = second_back.reshape(tensor_count * late, model_width)
     place = jnp.concatenate(
         [
             prefill_routes * stride + prefill_rank,
@@ -227,10 +226,20 @@
     low = (rest - middle.astype(jnp.float32)).astype(jnp.bfloat16)
 
     def combined(lo, hi, row_float):
-        parts = jnp.dot(
-            jnp.concatenate([high[lo:hi], middle[lo:hi], low[lo:hi]], axis=0),
-            returned,
-            preferred_element_type=jnp.float32,
+        weights = jnp.concatenate([high[lo:hi], middle[lo:hi], low[lo:hi]], axis=0).reshape(
+            3 * (hi - lo), tensor_count, stride
+        )
+        parts = (
+            jnp.dot(
+                weights[:, :, :early].reshape(3 * (hi - lo), tensor_count * early),
+                first_back,
+                preferred_element_type=jnp.float32,
+            )
+            + jnp.dot(
+                weights[:, :, early:].reshape(3 * (hi - lo), tensor_count * late),
+                second_back,
+                preferred_element_type=jnp.float32,
+            )
         ).reshape(3, hi - lo, model_width)
         weighted = (parts[0] + parts[1]) + parts[2]
         return (row_float + weighted).astype(jnp.bfloat16)

time: 208 us -> 211 us (1.014)
  matrix products: 34 us -> 40.7 us
  waiting for transfers between devices: 120 us -> 117 us
    dot_general x2 -> x4, matrix products: 1.3 us -> 7.44 us  [the longest x2 5.94 us: combined(): jnp.dot(weights[:, :, :early].reshape(3 * (hi - lo), tensor_count * early...]
    all_to_all x2, waiting for transfers between devices: 61.1 us -> 58.6 us  [give_back(): lax.all_to_all(lax.psum_scatter(done, 'dp', scatter_dimension=0, tiled=Tr...]
    unnamed x45 -> x41, local copies, waits for them, and re-layouts: 10.6 us -> 10.6 us
  transfers between devices with their start and end apart: 6 -> 6, of which waited for: 6 -> 6; matrix products, arithmetic and copies ran while one was open for 24% -> 25% of each run, Pallas kernels for 0% -> 0%
where the time goes in v16:
time: 211 us; the launch traced here: 210 us
  waiting for transfers between devices  117 us (55%)
  matrix products  40.7 us (19%)
  starting transfers between devices  24.6 us (12%)
  local copies, waits for them, and re-layouts  17.5 us (8%)
  other arithmetic  9.17 us (4%)
    all_to_all x2, waiting for transfers between devices, give_back(): lax.all_to_all(lax.psum_scatter(done, 'dp', scatter_dimension=0, tiled=Tr...  58.6 us
    all_to_all x2, waiting for transfers between devices, dispatch(): lax.all_to_all(outgoing, 'tensor', split_axis=0, concat_axis=0, tiled=True)  42 us
    dot_general x2, matrix products, expert_mlp(): return jnp.dot(active, down_w, preferred_element_type=jnp.float32)  10.8 us
    unnamed x41, local copies, waits for them, and re-layouts  10.6 us
    all_to_all x2, starting transfers between devices, dispatch(): lax.all_to_all(outgoing, 'tensor', split_axis=0, concat_axis=0, tiled=True)  9.94 us
    dot_general x2, matrix products, expert_mlp(): gate = jnp.dot(flat_rows, gate_w, preferred_element_type=jnp.float32)  9.8 us
    all_to_all x1, waiting for transfers between devices, attention_finish(): received = lax.all_to_all(payload, 'tensor', 0, 0, tiled=True)  9.73 us
    all_to_all x2, starting transfers between devices, give_back(): lax.all_to_all(lax.psum_scatter(done, 'dp', scatter_dimension=0, tiled=Tr...  7.9 us
  transfers between devices with their start and end apart: 6, of which 6 were waited for; matrix products, arithmetic and copies ran while one was open for 25% of the time, Pallas kernels for 0%

profile of v16, /device:TPU:0, one launch (start us, length us, event | category | flops | bytes accessed | tf_op | source)
XLA Modules:
  0.0 209.8 jit_solution(3106415134149697157)
XLA Ops:
  2.3 3.0 %convolution_convert_fusion = bf16[512,2048]{1,0:T(8,128)(2,1)} fusion(bf16[512,64]{0,1:T(8,128)(2,1)S(1)} %convert_element_type.214, bf16[64,2048]{1,0:T(8,128)(2,1)} %param.25), kind=kOutput, calls=%fused_computation.25 | convolution fusion | flops 135266304 | bytes 2424832 | tf_op jit(solution)/shard_map/dot_general | solution.py:111
  5.4 7.3 %all-to-all-start = ((bf16[32,16,2048]{2,1,0:T(8,128)(2,1)}), bf16[32,16,2048]{2,1,0:T(8,128)(2,1)S(1)}, u32[]{:S(2)}, u32[]{:S(2)}) async-start(bf16[32,16,2048]{2,1,0:T(8,128)(2,1)} %bitcast.155), calls=%async_computation | async-start | bytes 4194304 | tf_op jit(solution)/shard_map/all_to_all | solution.py:114
  12.7 5.6 %copy.98 = bf16[128,8,16,128]{3,2,1,0:T(8,128)(2,1)} copy(bf16[128,8,16,128]{3,1,2,0:T(8,128)(2,1)} %bitcast.156) | data formatting | bytes 8388608
  18.6 3.7 %copy.101 = bf16[128,8,16,128]{3,2,1,0:T(8,128)(2,1)S(1)} copy(bf16[128,8,16,128]{3,1,2,0:T(8,128)(2,1)} %bitcast.157) | data formatting | bytes 8388608
  22.6 2.5 %fusion.31 = (f32[32,16]{0,1:T(8,128)S(1)}, f32[16,4,256,32]{2,3,1,0:T(8,128)S(1)}) fusion(pred[4,32,256]{2,1,0:T(8,128)(4,1)S(1)} %broadcast_and_fusion, bf16[32,16,128,1]{2,1,0,3:T(8,128)(2,1)S(1)} %bitcast.173, bf16[4,256,16,128]{3,2,1,0:T(8,128)(2,1)S(1)} %bitcast.158), kind=kOutput, calls=%fused_computation.42 | convolution fusion | flops 135790080 | bytes 6457344 | tf_op jit(solution)/shard_map/rhd,gjhd->grhj/dot_general | solution.py:35
  25.1 2.5 %fusion.49 = f32[32,16,128]{2,0,1:T(8,128)S(1)} fusion(bf16[4,256,16,128]{3,2,1,0:T(8,128)(2,1)S(1)} %bitcast.159, f32[16,4,256,32]{2,3,1,0:T(8,128)S(1)} %get-tuple-element.26, f32[32,16]{0,1:T(8,128)S(1)} %get-tuple-element.20, pred[4,32,256]{2,1,0:T(8,128)(4,1)S(1)} %broadcast_and_fusion), kind=kOutput, calls=%fused_computation.55 | convolution fusion | flops 136314880 | bytes 6588416 | tf_op jit(solution)/shard_map/grhj,gjhd->rhd/dot_general | solution.py:48
  34.2 27.3 %all-to-all-done = bf16[32,16,2048]{2,1,0:T(8,128)(2,1)S(1)} async-done(((bf16[32,16,2048]{2,1,0:T(8,128)(2,1)}), bf16[32,16,2048]{2,1,0:T(8,128)(2,1)S(1)}, u32[]{:S(2)}, u32[]{:S(2)}) %all-to-all-start) | async-done | bytes 2097184 | tf_op jit(solution)/shard_map/all_to_all | solution.py:114
  62.5 4.0 %all-to-all-start.1 = ((f32[32,1,2112]{2,1,0:T(1,128)}), f32[32,1,2112]{2,1,0:T(1,128)S(1)}, u32[]{:S(2)}, u32[]{:S(2)}) async-start(f32[32,1,2112]{2,1,0:T(1,128)} %copy.77), calls=%async_computation.1 | async-start | bytes 557056 | tf_op jit(solution)/shard_map/all_to_all | solution.py:64
  67.9 9.7 %all-to-all-done.1 = f32[32,1,2112]{2,1,0:T(1,128)S(1)} async-done(((f32[32,1,2112]{2,1,0:T(1,128)}), f32[32,1,2112]{2,1,0:T(1,128)S(1)}, u32[]{:S(2)}, u32[]{:S(2)}) %all-to-all-start.1) | async-done | bytes 270368 | tf_op jit(solution)/shard_map/all_to_all | solution.py:64
  79.6 2.8 %all-to-all-start.2 = ((bf16[32,16,128]{2,1,0:T(8,128)(2,1)}), bf16[32,16,128]{2,1,0:T(8,128)(2,1)S(1)}, u32[]{:S(2)}, u32[]{:S(2)}) async-start(bf16[32,16,128]{2,1,0:T(8,128)(2,1)} %copy.79), calls=%async_computation.2 | async-start | bytes 262144 | tf_op jit(solution)/shard_map/all_to_all | solution.py:86
  84.2 6.3 %all-to-all-done.2 = bf16[32,16,128]{2,1,0:T(8,128)(2,1)S(1)} async-done(((bf16[32,16,128]{2,1,0:T(8,128)(2,1)}), bf16[32,16,128]{2,1,0:T(8,128)(2,1)S(1)}, u32[]{:S(2)}, u32[]{:S(2)}) %all-to-all-start.2) | async-done | bytes 131104 | tf_op jit(solution)/shard_map/all_to_all | solution.py:86
  92.1 2.6 %all-to-all-start.3 = ((bf16[32,8,2048]{2,1,0:T(8,128)(2,1)}), bf16[32,8,2048]{2,1,0:T(8,128)(2,1)S(1)}, u32[]{:S(2)}, u32[]{:S(2)}) async-start(bf16[32,8,2048]{2,1,0:T(8,128)(2,1)} %fusion.26), calls=%async_computation.3 | async-start | bytes 2097152 | tf_op jit(solution)/shard_map/all_to_all | solution.py:114
  94.7 5.3 %fusion.13 = f32[512,1024]{1,0:T(8,128)S(1)} fusion(bf16[512,2048]{1,0:T(8,128)(2,1)} %bitcast.162, bf16[1,2048,1024]{2,1,0:T(8,128)(2,1)} %param.29), kind=kOutput, calls=%fused_computation.18 | convolution fusion | flops 2147483648 | bytes 8388608 | tf_op jit(solution)/shard_map/dot_general | solution.py:14
  100.1 2.5 %multiply_convert_fusion = bf16[512,1024]{1,0:T(8,128)(2,1)S(1)} fusion(f32[512,1024]{1,0:T(8,128)S(1)} %fusion.13, bf16[512,2048]{1,0:T(8,128)(2,1)S(1)} %bitcast.163, bf16[1,2048,1024]{2,1,0:T(8,128)(2,1)S(1)} %copy-done.14), kind=kOutput, calls=%fused_computation.45 | convolution fusion | flops 2150629376 | bytes 9437184 | tf_op jit(solution)/shard_map/dot_general | solution.py:15
  102.6 3.7 %fusion.19 = bf16[32,16,2048]{2,1,0:T(8,128)(2,1)} fusion(bf16[32,16,1024]{2,1,0:T(8,128)(2,1)S(1)} %bitcast.180, bf16[1,1024,2048]{2,1,0:T(8,128)(2,1)S(1)} %copy-done.13), kind=kOutput, calls=%fused_computation.24 | convolution fusion | flops 2148532224 | bytes 7340032 | tf_op jit(solution)/shard_map/dot_general | solution.py:17
  106.3 14.7 %all-to-all-done.3 = bf16[32,8,2048]{2,1,0:T(8,128)(2,1)S(1)} async-done(((bf16[32,8,2048]{2,1,0:T(8,128)(2,1)}), bf16[32,8,2048]{2,1,0:T(8,128)(2,1)S(1)}, u32[]{:S(2)}, u32[]{:S(2)}) %all-to-all-start.3) | async-done | bytes 1048608 | tf_op jit(solution)/shard_map/all_to_all | solution.py:114
  120.9 3.7 %all-to-all-start.4 = ((bf16[32,16,2048]{2,1,0:T(8,128)(2,1)}), bf16[32,16,2048]{2,1,0:T(8,128)(2,1)}, u32[]{:S(2)}, u32[]{:S(2)}) async-start(bf16[32,16,2048]{2,1,0:T(8,128)(2,1)} %fusion.19), calls=%async_computation.4 | async-start | bytes 4194304 | tf_op jit(solution)/shard_map/all_to_all | solution.py:138
  124.9 4.5 %fusion.11 = f32[256,1024]{1,0:T(8,128)} fusion(bf16[1,2048,1024]{2,1,0:T(8,128)(2,1)} %param.29, bf16[32,8,2048]{2,1,0:T(8,128)(2,1)S(1)} %all-to-all-done.3, f32[2048]{0:T(1024)S(1)} %copy-done.9, f32[32,8]{1,0:T(8,128)S(1)} %add_rsqrt_fusion), kind=kOutput, calls=%fused_computation.16 | convolution fusion | flops 1075838976 | bytes 6300672 | tf_op jit(solution)/shard_map/dot_general | solution.py:14
  129.4 7.1 %fusion.22 = bf16[32,8,2048]{2,1,0:T(8,128)(2,1)} fusion(bf16[1,1024,2048]{2,1,0:T(8,128)(2,1)} %param.31, bf16[1,2048,1024]{2,1,0:T(8,128)(2,1)} %param.30, f32[256,1024]{1,0:T(8,128)} %fusion.11, bf16[32,8,2048]{2,1,0:T(8,128)(2,1)S(1)} %all-to-all-done.3, f32[2048]{0:T(1024)S(1)} %copy-done.9, f32[32,8]{1,0:T(8,128)S(1)} %add_rsqrt_fusion), kind=kOutput, calls=%fused_computation.31 | convolution fusion | flops 2151677952 | bytes 11543552 | tf_op jit(solution)/shard_map/dot_general | solution.py:17
  136.6 36.9 %all-to-all-done.4 = bf16[32,16,2048]{2,1,0:T(8,128)(2,1)} async-done(((bf16[32,16,2048]{2,1,0:T(8,128)(2,1)}), bf16[32,16,2048]{2,1,0:T(8,128)(2,1)}, u32[]{:S(2)}, u32[]{:S(2)}) %all-to-all-start.4) | async-done | bytes 2097184 | tf_op jit(solution)/shard_map/all_to_all | solution.py:138
  173.5 4.2 %all-to-all-start.5 = ((bf16[32,8,2048]{2,1,0:T(8,128)(2,1)}), bf16[32,8,2048]{2,1,0:T(8,128)(2,1)S(1)}, u32[]{:S(2)}, u32[]{:S(2)}) async-start(bf16[32,8,2048]{2,1,0:T(8,128)(2,1)} %fusion.22), calls=%async_computation.5 | async-start | bytes 2097152 | tf_op jit(solution)/shard_map/all_to_all | solution.py:138
  179.2 2.8 %convolution_bitcast_fusion.3 = f32[3,2048]{1,0:T(4,128)S(1)} fusion(bf16[3,32,16]{1,0,2:T(4,128)(2,1)S(1)} %copy.95, bf16[32,16,2048]{2,1,0:T(8,128)(2,1)} %all-to-all-done.4), kind=kOutput, calls=%fused_computation.36 | convolution fusion | flops 6291456 | bytes 2124800 | tf_op jit(solution)/shard_map/dot_general | solution.py:233
  182.1 21.7 %all-to-all-done.5 = bf16[32,8,2048]{2,1,0:T(8,128)(2,1)S(1)} async-done(((bf16[32,8,2048]{2,1,0:T(8,128)(2,1)}), bf16[32,8,2048]{2,1,0:T(8,128)(2,1)S(1)}, u32[]{:S(2)}, u32[]{:S(2)}) %all-to-all-start.5) | async-done | bytes 1048608 | tf_op jit(solution)/shard_map/all_to_all | solution.py:138
  205.9 3.1 %fusion.25 = f32[192,2048]{1,0:T(8,128)S(1)} fusion(f32[192,2048]{1,0:T(8,128)S(1)} %convolution_bitcast_fusion, bf16[32,16,2048]{2,1,0:T(8,128)(2,1)} %all-to-all-done.4, bf16[192,32,16]{0,2,1:T(8,128)(2,1)S(1)} %slice.99), kind=kOutput, calls=%fused_computation.32 | convolution fusion | flops 403046400 | bytes 5439488 | tf_op jit(solution)/shard_map/dot_general | solution.py:233
  (122 shorter events, 21.0 us)
Async XLA Ops:
  0.6 78.0 %copy-start = (bf16[64,2048]{1,0:T(8,128)(2,1)S(1)}, bf16[64,2048]{1,0:T(8,128)(2,1)}, u32[]{:S(2)}) copy-start(bf16[64,2048]{1,0:T(8,128)(2,1)} %param.24) | copy-start | bytes 786436
  5.4 7.3 %copy-start.7 = (bf16[1,32,2048]{2,1,0:T(8,128)(2,1)S(1)}, bf16[1,32,2048]{2,1,0:T(8,128)(2,1)}, u32[]{:S(2)}) copy-start(bf16[1,32,2048]{2,1,0:T(8,128)(2,1)} %param.16) | copy-start | bytes 393220
  5.4 56.2 %all-to-all-start = ((bf16[32,16,2048]{2,1,0:T(8,128)(2,1)}), bf16[32,16,2048]{2,1,0:T(8,128)(2,1)S(1)}, u32[]{:S(2)}, u32[]{:S(2)}) async-start(bf16[32,16,2048]{2,1,0:T(8,128)(2,1)} %bitcast.155), calls=%async_computation | async-start | bytes 4194304 | tf_op jit(solution)/shard_map/all_to_all | solution.py:114
  12.7 5.6 %copy-start.6 = (bf16[1,32,2048]{2,1,0:T(8,128)(2,1)S(1)}, bf16[1,32,2048]{2,1,0:T(8,128)(2,1)}, u32[]{:S(2)}) copy-start(bf16[1,32,2048]{2,1,0:T(8,128)(2,1)} %param.17) | copy-start | bytes 393220
  18.6 3.8 %copy-start.15 = (s32[1,32]{1,0:T(1,128)S(1)}, s32[1,32]{1,0:T(1,128)}, u32[]{:S(2)}) copy-start(s32[1,32]{1,0:T(1,128)} %param.21) | copy-start | bytes 388
  18.6 3.8 %copy-start.12 = (s32[1,4]{1,0:T(1,128)S(1)}, s32[1,4]{1,0:T(1,128)}, u32[]{:S(2)}) copy-start(s32[1,4]{1,0:T(1,128)} %param.22) | copy-start | bytes 52
  18.6 4.0 %copy-start.1 = (bf16[128,8,16,128]{3,2,1,0:T(8,128)(2,1)S(1)}, bf16[128,8,16,128]{3,2,1,0:T(8,128)(2,1)}, u32[]{:S(2)}) copy-start(bf16[128,8,16,128]{3,2,1,0:T(8,128)(2,1)} %copy.98) | copy-start | bytes 12582916
  25.1 2.5 %copy-start.3 = (f32[16,4,256,32]{2,3,1,0:T(8,128)}, f32[16,4,256,32]{2,3,1,0:T(8,128)S(1)}, u32[]{:S(2)}) copy-start(f32[16,4,256,32]{2,3,1,0:T(8,128)S(1)} %get-tuple-element.26) | copy-start | bytes 6291460
  27.9 4.6 %copy-start.8 = (s32[65,8]{0,1:T(8,128)S(1)}, s32[65,8]{0,1:T(8,128)}, u32[]{:S(2)}) copy-start(s32[65,8]{0,1:T(8,128)} %param.27) | copy-start | bytes 6244
  29.1 4.8 %copy-start.5 = (f32[32,2048]{1,0:T(8,128)S(1)}, f32[32,2048]{1,0:T(8,128)}, u32[]{:S(2)}) copy-start(f32[32,2048]{1,0:T(8,128)} %reshape.378) | copy-start | bytes 786436
  62.5 15.1 %all-to-all-start.1 = ((f32[32,1,2112]{2,1,0:T(1,128)}), f32[32,1,2112]{2,1,0:T(1,128)S(1)}, u32[]{:S(2)}, u32[]{:S(2)}) async-start(f32[32,1,2112]{2,1,0:T(1,128)} %copy.77), calls=%async_computation.1 | async-start | bytes 557056 | tf_op jit(solution)/shard_map/all_to_all | solution.py:64
  67.9 14.4 %copy-start.9 = (f32[2048]{0:T(1024)S(1)}, f32[2048]{0:T(1024)}, u32[]{:S(2)}) copy-start(f32[2048]{0:T(1024)} %param.26) | copy-start | bytes 24580
  79.6 11.0 %all-to-all-start.2 = ((bf16[32,16,128]{2,1,0:T(8,128)(2,1)}), bf16[32,16,128]{2,1,0:T(8,128)(2,1)S(1)}, u32[]{:S(2)}, u32[]{:S(2)}) async-start(bf16[32,16,128]{2,1,0:T(8,128)(2,1)} %copy.79), calls=%async_computation.2 | async-start | bytes 262144 | tf_op jit(solution)/shard_map/all_to_all | solution.py:86
  82.3 8.3 %copy-start.10 = (bf16[1,1,2048]{2,1,0:T(2,128)(2,1)S(1)}, bf16[1,1,2048]{2,1,0:T(2,128)(2,1)}, u32[]{:S(2)}) copy-start(bf16[1,1,2048]{2,1,0:T(2,128)(2,1)} %param.23) | copy-start | bytes 12292
  82.3 8.3 %copy-start.2 = (bf16[64,2048]{1,0:T(8,128)(2,1)S(1)}, bf16[64,2048]{1,0:T(8,128)(2,1)}, u32[]{:S(2)}) copy-start(bf16[64,2048]{1,0:T(8,128)(2,1)} %param.25) | copy-start | bytes 786436
  92.1 28.9 %all-to-all-start.3 = ((bf16[32,8,2048]{2,1,0:T(8,128)(2,1)}), bf16[32,8,2048]{2,1,0:T(8,128)(2,1)S(1)}, u32[]{:S(2)}, u32[]{:S(2)}) async-start(bf16[32,8,2048]{2,1,0:T(8,128)(2,1)} %fusion.26), calls=%async_computation.3 | async-start | bytes 2097152 | tf_op jit(solution)/shard_map/all_to_all | solution.py:114
  94.7 5.3 %copy-start.4 = (bf16[32,16,2048]{2,1,0:T(8,128)(2,1)S(1)}, bf16[32,16,2048]{2,1,0:T(8,128)(2,1)}, u32[]{:S(2)}) copy-start(bf16[32,16,2048]{2,1,0:T(8,128)(2,1)} %fusion.2) | copy-start | bytes 6291460
  94.7 5.3 %copy-start.14 = (bf16[1,2048,1024]{2,1,0:T(8,128)(2,1)S(1)}, bf16[1,2048,1024]{2,1,0:T(8,128)(2,1)}, u32[]{:S(2)}) copy-start(bf16[1,2048,1024]{2,1,0:T(8,128)(2,1)} %param.30) | copy-start | bytes 12582916
  100.1 2.5 %copy-start.13 = (bf16[1,1024,2048]{2,1,0:T(8,128)(2,1)S(1)}, bf16[1,1024,2048]{2,1,0:T(8,128)(2,1)}, u32[]{:S(2)}) copy-start(bf16[1,1024,2048]{2,1,0:T(8,128)(2,1)} %param.31) | copy-start | bytes 12582916
  120.9 52.5 %all-to-all-start.4 = ((bf16[32,16,2048]{2,1,0:T(8,128)(2,1)}), bf16[32,16,2048]{2,1,0:T(8,128)(2,1)}, u32[]{:S(2)}, u32[]{:S(2)}) async-start(bf16[32,16,2048]{2,1,0:T(8,128)(2,1)} %fusion.19), calls=%async_computation.4 | async-start | bytes 4194304 | tf_op jit(solution)/shard_map/all_to_all | solution.py:138
  136.6 41.2 %copy-start.11 = (f32[65,8]{0,1:T(8,128)S(1)}, f32[65,8]{0,1:T(8,128)}, u32[]{:S(2)}) copy-start(f32[65,8]{0,1:T(8,128)} %param.28) | copy-start | bytes 6244
  173.5 30.3 %all-to-all-start.5 = ((bf16[32,8,2048]{2,1,0:T(8,128)(2,1)}), bf16[32,8,2048]{2,1,0:T(8,128)(2,1)S(1)}, u32[]{:S(2)}, u32[]{:S(2)}) async-start(bf16[32,8,2048]{2,1,0:T(8,128)(2,1)} %fusion.22), calls=%async_computation.5 | async-start | bytes 2097152 | tf_op jit(solution)/shard_map/all_to_all | solution.py:138
